TPU v7x, 256 devices: a whole 4x4x8 slice. The times are simulated.
256 devices in a mesh: dp: 32 (over y, z), tensor: 8 (over x, core).
Axes of the slice: x: 4, y: 4, z: 8, core: 2. Of those that a mesh axis runs over, the one named last changes fastest.
Arguments:
- residual_in: bfloat16 [2048, 2048], P(('dp', 'tensor')), may hold values from -6 to 6
- attn_gain: float32 [2048], replicated, may hold values from 0.5 to 1.5
- query_weight: bfloat16 [2048, 4096], P(None, 'tensor'), may hold values from -0.125 to 0.125
- kv_weight: bfloat16 [2048, 1024], P(None, 'tensor'), may hold values from -0.125 to 0.125
- query_gain: float32 [128], replicated, may hold values from 0.25 to 1.75
- key_gain: float32 [128], replicated, may hold values from 0.25 to 1.75
- out_weight: bfloat16 [4096, 2048], P('tensor'), may hold values from -0.09375 to 0.09375
- moe_gain: float32 [2048], replicated, may hold values from 0.5 to 1.5
- gate_weight: bfloat16 [128, 2048, 768], P('dp', None, 'tensor'), may hold values from -0.1875 to 0.1875
- lift_weight: bfloat16 [128, 2048, 768], P('dp', None, 'tensor'), may hold values from -0.1875 to 0.1875
- down_weight: bfloat16 [128, 768, 2048], P('dp', 'tensor'), may hold values from -0.21875 to 0.21875
- routes: int32 [2048, 8], P('dp'), may hold values from 0 to 127, as said below
- route_weights: float32 [2048, 8], P('dp'), may hold values from 0.5 to 1
- prefix_cache: bfloat16 [64, 2048, 1024], P('dp', 'tensor'), may hold values from -250 to 250
- suffix_cache: bfloat16 [2048, 128, 1024], P('dp', 'tensor'), may hold values from -250 to 250
- prefix_len: int32 [64], P('dp'), may hold values from 1 to 2048, as said below
- suffix_len: int32 [2048], P('dp'), may hold values from 1 to 128, as said below
- request_group: int32 [2048], P('dp'), may hold values from 0 to 63, as said below
Outputs:
- layer_out: bfloat16 [2048, 2048], P(('dp', 'tensor'))
- new_cache_rows: bfloat16 [2048, 1024], P('dp', 'tensor')
Inputs may be any that keep to these rules, and one draw needn't show every extreme that they name: `routes`: each block of 64 rows (the requests of one index of dp) names 64 of the experts exactly 8 times each and no other expert; one expert is among them in every block. `request_group`: request r belongs to one of the groups (r // 64) * 2 to (r // 64) * 2 + 1. `prefix_len`: some shared prompt has all 2048 slots live. `suffix_len`: some request has all 128 suffix slots live.
All inputs are finite; a program needn't handle non-finite values.
Results may differ from a plain program's by a relative error of at most 0.02.
Values may be sent and summed in bfloat16 or wider, within the bound.
No kernel may reach another device: no remote copies, remote signals or barrier semaphores. Data moves between devices by JAX's collectives and lax.ppermute only.
A program may use at most 128 MiB of HBM per device.

v0:
```python
import math

import jax
import jax.numpy as jnp
from jax import lax
from jax.sharding import PartitionSpec as P

EPSILON = 1e-06
THETA = 1000000.0
NEGATIVE = -1e30


def merged(array, axis, combine):
    everything = jax.tree.map(lambda part: lax.all_gather(part, axis), array)
    first = jax.tree.map(lambda part: part[0], everything)

    def hop(k, so_far):
        return combine(so_far, jax.tree.map(lambda part: part[k], everything))

    return lax.fori_loop(1, lax.axis_size(axis), hop, first)


def rms_scale(values, gain):
    mean_square = jnp.mean(values * values, axis=-1, keepdims=True)
    return values * lax.rsqrt(mean_square + EPSILON) * gain


def rotate(values, positions):
    half = values.shape[-1] // 2
    freqs = THETA ** (-jnp.arange(half).astype(jnp.float32) * 2.0 / values.shape[-1])
    angles = positions.astype(jnp.float32)[:, None] * freqs[None, :]
    angles = jnp.concatenate([angles, angles], axis=-1)
    cosine = jnp.cos(angles)[:, None, :]
    sine = jnp.sin(angles)[:, None, :]
    turned = jnp.concatenate([-values[..., half:], values[..., :half]], axis=-1)
    return values * cosine + turned * sine


def combine_parts(first, second):
    top_first, total_first, sums_first = first
    top_second, total_second, sums_second = second
    top_new = jnp.maximum(top_first, top_second)
    factor_first = jnp.exp(top_first - top_new)
    factor_second = jnp.exp(top_second - top_new)
    return (
        top_new,
        total_first * factor_first + total_second * factor_second,
        sums_first * factor_first[..., None] + sums_second * factor_second[..., None],
    )


def body(
    residual_in,
    attn_gain,
    query_weight,
    kv_weight,
    query_gain,
    key_gain,
    out_weight,
    moe_gain,
    gate_weight,
    lift_weight,
    down_weight,
    routes,
    route_weights,
    prefix_cache,
    suffix_cache,
    prefix_len,
    suffix_len,
    request_group,
):
    tensor_size = lax.axis_size("tensor")
    tensor_rank = lax.axis_index("tensor")
    dp_rank = lax.axis_index("dp")
    owners = lax.axis_size("dp")
    head_dim = query_gain.shape[0]
    requests = routes.shape[0]
    model_width = residual_in.shape[1]
    query_cols = query_weight.shape[1]
    kv_cols = kv_weight.shape[1]
    heads_here = query_cols // head_dim
    heads_all = heads_here * tensor_size
    kv_heads_all = kv_cols * tensor_size // (2 * head_dim)
    per_group = heads_all // kv_heads_all
    groups_dev = prefix_cache.shape[0]
    pre_local = prefix_cache.shape[1]
    suf_local = suffix_cache.shape[1]
    normed = rms_scale(residual_in.astype(jnp.float32), attn_gain).astype(jnp.bfloat16)
    piece = lax.all_gather(normed, "tensor", axis=0, tiled=True)
    projected = jnp.concatenate(
        [
            jnp.dot(piece, query_weight, preferred_element_type=jnp.float32),
            jnp.dot(piece, kv_weight, preferred_element_type=jnp.float32),
        ],
        axis=1,
    )
    query_raw = projected[:, :query_cols].reshape(requests, heads_here, head_dim)
    kv_raw = projected[:, query_cols:].reshape(requests, kv_cols // head_dim, head_dim)
    group_ids = dp_rank * groups_dev + jnp.arange(groups_dev)
    member = request_group[:, None] == group_ids[None, :]
    prefix_of = jnp.sum(jnp.where(member, prefix_len[None, :], 0), axis=1)
    positions = prefix_of + suffix_len
    queries = rotate(rms_scale(query_raw, query_gain), positions).astype(jnp.bfloat16)
    head_number = tensor_rank * (kv_cols // head_dim) + jnp.arange(kv_cols // head_dim)
    is_key = (head_number < kv_heads_all)[None, :, None]
    keyed = rotate(rms_scale(kv_raw, key_gain), positions)
    new_rows = jnp.where(is_key, keyed, kv_raw).astype(jnp.bfloat16).reshape(requests, kv_cols)
    joined = jnp.concatenate([queries.reshape(requests, query_cols), new_rows], axis=1)
    every_head = lax.all_gather(joined, "tensor", axis=1, tiled=True).reshape(
        requests, tensor_size, query_cols + kv_cols
    )
    all_queries = every_head[:, :, :query_cols].reshape(requests, kv_heads_all, per_group, head_dim)
    all_kv = every_head[:, :, query_cols:]
    own_keys = all_kv[:, :kv_heads_all]
    own_values = all_kv[:, kv_heads_all:].astype(jnp.float32)
    scale = 1.0 / math.sqrt(head_dim)
    split_at = kv_heads_all * head_dim
    pre_keys = prefix_cache[:, :, :split_at].reshape(groups_dev, pre_local, kv_heads_all, head_dim)
    pre_values = prefix_cache[:, :, split_at:].reshape(
        groups_dev, pre_local, kv_heads_all, head_dim
    )
    suf_keys = suffix_cache[:, :, :split_at].reshape(requests, suf_local, kv_heads_all, head_dim)
    suf_values = suffix_cache[:, :, split_at:].reshape(requests, suf_local, kv_heads_all, head_dim)
    pre_scores = (
        jnp.einsum("rgqd,npgd->rgqnp", all_queries, pre_keys, preferred_element_type=jnp.float32)
        * scale
    )
    suf_scores = (
        jnp.einsum("rgqd,rsgd->rgqs", all_queries, suf_keys, preferred_element_type=jnp.float32)
        * scale
    )
    own_scores = (
        jnp.einsum("rgqd,rgd->rgq", all_queries, own_keys, preferred_element_type=jnp.float32)
        * scale
    )
    pre_slots = tensor_rank * pre_local + jnp.arange(pre_local)
    pre_valid = (member[:, :, None] & (pre_slots[None, None, :] < prefix_len[None, :, None]))[
        :, None, None, :, :
    ]
    suf_slots = tensor_rank * suf_local + jnp.arange(suf_local)
    suf_valid = (suf_slots[None, :] < suffix_len[:, None])[:, None, None, :]
    own_valid = tensor_rank == 0
    top_pre = jnp.max(jnp.where(pre_valid, pre_scores, NEGATIVE), axis=(3, 4))
    top_suf = jnp.max(jnp.where(suf_valid, suf_scores, NEGATIVE), axis=3)
    top_own = jnp.where(own_valid, own_scores, NEGATIVE)
    top_local = jnp.maximum(jnp.maximum(top_pre, top_suf), top_own)
    pre_weights = jnp.where(pre_valid, jnp.exp(pre_scores - top_local[..., None, None]), 0.0)
    suf_weights = jnp.where(suf_valid, jnp.exp(suf_scores - top_local[..., None]), 0.0)
    own_weights = jnp.where(own_valid, jnp.exp(own_scores - top_local), 0.0)
    total_local = jnp.sum(pre_weights, axis=(3, 4)) + jnp.sum(suf_weights, axis=3) + own_weights
    sums_local = jnp.einsum(
        "rgqnp,npgd->rgqd",
        pre_weights.astype(jnp.bfloat16),
        pre_values,
        preferred_element_type=jnp.float32,
    )
    sums_local = sums_local + jnp.einsum(
        "rgqs,rsgd->rgqd",
        suf_weights.astype(jnp.bfloat16),
        suf_values,
        preferred_element_type=jnp.float32,
    )
    own_low = own_weights.astype(jnp.bfloat16).astype(jnp.float32)
    sums_local = sums_local + own_low[..., None] * own_values[:, :, None, :]
    top_local = top_local.reshape(requests, heads_all)
    total_local = total_local.reshape(requests, heads_all)
    sums_local = sums_local.reshape(requests, heads_all, head_dim)
    top_all, total_all, sums_all = merged(
        (top_local, total_local, sums_local), "tensor", combine_parts
    )
    total_mine = lax.dynamic_slice_in_dim(total_all, tensor_rank * heads_here, heads_here, 1)
    sums_mine = lax.dynamic_slice_in_dim(sums_all, tensor_rank * heads_here, heads_here, 1)
    mixed = sums_mine / total_mine[..., None]
    attn_heads = mixed.reshape(requests, query_cols).astype(jnp.bfloat16)
    attn_out = lax.psum_scatter(
        jnp.dot(attn_heads, out_weight, preferred_element_type=jnp.float32).astype(jnp.bfloat16),
        "tensor",
        scatter_dimension=0,
        tiled=True,
    ).astype(jnp.float32)
    middle = (residual_in.astype(jnp.float32) + attn_out).astype(jnp.bfloat16)
    moe_in = rms_scale(middle.astype(jnp.float32), moe_gain).astype(jnp.bfloat16)
    local_experts = gate_weight.shape[0]
    experts_all = local_experts * owners
    topk = routes.shape[1]
    capacity = 2 * requests * topk // experts_all
    flat_routes = routes.reshape(-1)
    onehot = (flat_routes[:, None] == jnp.arange(experts_all)[None, :]).astype(jnp.int32)
    running = jnp.cumsum(onehot, axis=0)
    slot_of = jnp.sum(onehot * running, axis=1) - 1
    code_of = (flat_routes * capacity + slot_of).reshape(requests, topk)
    code_span = jnp.arange(experts_all * capacity)
    placing = jnp.any(code_of[None, :, :] == code_span[:, None, None], axis=2).astype(jnp.bfloat16)
    share = route_weights / jnp.sum(route_weights, axis=1, keepdims=True)
    placed = jnp.dot(
        placing,
        lax.all_gather(moe_in, "tensor", axis=0, tiled=True),
        preferred_element_type=jnp.float32,
    )
    outgoing = placed.astype(jnp.bfloat16).reshape(owners, local_experts, capacity, model_width)
    rows = lax.all_to_all(outgoing, "dp", split_axis=0, concat_axis=0, tiled=True)
    gate_val = jnp.einsum("necd,edf->necf", rows, gate_weight, preferred_element_type=jnp.float32)
    lift_val = jnp.einsum("necd,edf->necf", rows, lift_weight, preferred_element_type=jnp.float32)
    hidden_units = (jax.nn.silu(gate_val) * lift_val).astype(jnp.bfloat16)
    returned = lax.all_to_all(
        jnp.einsum(
            "necf,efd->necd", hidden_units, down_weight, preferred_element_type=jnp.float32
        ).astype(jnp.bfloat16),
        "dp",
        split_axis=0,
        concat_axis=0,
        tiled=True,
    ).astype(jnp.float32)
    returned = returned.reshape(experts_all * capacity, model_width)
    picked_rows = returned[code_of]
    moe_out = lax.psum_scatter(
        jnp.sum(share[:, :, None] * picked_rows, axis=1).astype(jnp.bfloat16),
        "tensor",
        scatter_dimension=0,
        tiled=True,
    ).astype(jnp.float32)
    layer_out = (middle.astype(jnp.float32) + moe_out).astype(jnp.bfloat16)
    return (layer_out, new_rows)


def solution(mesh):
    in_specs = (
        P(("dp", "tensor"), None),
        P(),
        P(None, "tensor"),
        P(None, "tensor"),
        P(),
        P(),
        P("tensor", None),
        P(),
        P("dp", None, "tensor"),
        P("dp", None, "tensor"),
        P("dp", "tensor", None),
        P("dp", None),
        P("dp", None),
        P("dp", "tensor", None),
        P("dp", "tensor", None),
        P("dp"),
        P("dp"),
        P("dp"),
    )
    out_specs = (P(("dp", "tensor"), None), P("dp", "tensor"))
    return jax.shard_map(body, mesh=mesh, in_specs=in_specs, out_specs=out_specs, check_vma=False)
```

profile of v0, /device:TPU:32, one launch (start us, length us, event | category | flops | bytes accessed | tf_op | source)
XLA Modules:
  0.0 472.2 jit_solution(8575406757492180028)
XLA Ops:
  9.2 13.2 %all_gather.18 = bf16[64,2048]{1,0:T(8,128)(2,1)S(1)} all-gather(bf16[8,2048]{1,0:T(8,128)(2,1)S(1)} %fusion.79), channel_id=1, replica_groups=mesh['dp'=32,'tensor'=8] {'tensor'}, dimensions={0}, use_global_device_ids=true | all-gather | bytes 294912 | tf_op jit(solution)/shard_map/all_gather | solution.py:89
  24.6 2.1 fusion.100
  28.0 13.3 %all_gather.19 = bf16[64,5120]{1,0:T(8,128)(2,1)S(1)} all-gather(bf16[64,640]{1,0:T(8,128)(2,1)S(1)} %pad_maximum_fusion), channel_id=1, replica_groups=mesh['dp'=32,'tensor'=8] {'tensor'}, dimensions={1}, use_global_device_ids=true | all-gather | bytes 737280 | tf_op jit(solution)/shard_map/all_gather | solution.py:109
  42.5 2.1 fusion.98
  44.7 2.0 copy.234
  46.9 4.0 fusion.4
  51.0 3.0 slice_bitcast_fusion.1
  57.2 2.0 fusion.55
  59.2 3.3 fusion.23
  65.2 12.8 %all_gather.20 = f32[8,64,32]{1,2,0:T(8,128)S(1)} all-gather(f32[1,64,32]{1,2,0:T(8,128)S(1)} %bitcast.195), channel_id=1, replica_groups=mesh['dp'=32,'tensor'=8] {'tensor'}, dimensions={0}, use_global_device_ids=true | all-gather | bytes 73728 | tf_op jit(solution)/shard_map/all_gather | solution.py:14
  78.0 4.1 fusion.12
  82.3 13.5 %all_gather.21 = f32[8,64,32]{1,2,0:T(8,128)S(1)} all-gather(f32[1,64,32]{1,2,0:T(8,128)S(1)} %add_bitcast_fusion), channel_id=1, replica_groups=mesh['dp'=32,'tensor'=8] {'tensor'}, dimensions={0}, use_global_device_ids=true | all-gather | bytes 73728 | tf_op jit(solution)/shard_map/all_gather | solution.py:14
  96.7 22.5 %all-gather.2.cloned.1.call-done = f32[8,64,32,128]{3,2,1,0:T(8,128)} async-done(((f32[1,64,32,128]{3,2,1,0:T(8,128)}), f32[8,64,32,128]{3,2,1,0:T(8,128)}) %all-gather.2.cloned.1.call-update) | async-done | bytes 8388624 | tf_op jit(solution)/shard_map/all_gather | solution.py:14
  120.6 20.0 %while.19 = (s32[]{:T(128)}, f32[64,32]{1,0:T(8,128)S(1)}, f32[64,32]{1,0:T(8,128)S(1)}, f32[64,32,128]{2,1,0:T(8,128)S(1)}, f32[8,64,32]{1,2,0:T(8,128)S(1)}, /...) while((s32[]{:T(128)}, f32[64,32]{1,0:T(8,128)S(1)}, ...), condition=%wide.region_9.10_spmd, body=%wide.region_8.9_spmd.sunk | while | flops 798725 | bytes 3293335 | solution.py:20
  121.5 1.9 fusion.114
  124.4 1.9 fusion.114
  127.2 1.9 fusion.114
  130.1 1.9 fusion.114
  133.0 1.9 fusion.114
  135.8 1.9 fusion.114
  143.0 32.8 %reduce-scatter.3.cloned.1.call-done = bf16[8,2048]{1,0:T(8,128)(2,1)} async-done(((bf16[64,2048]{1,0:T(8,128)(2,1)}), bf16[8,2048]{1,0:T(8,128)(2,1)}) %reduce-scatter.3.cloned.1.call-update) | async-done | bytes 32784 | tf_op jit(solution)/shard_map/reduce_scatter | solution.py:175
  177.6 12.8 %all_gather.23 = bf16[64,2048]{1,0:T(8,128)(2,1)S(1)} all-gather(bf16[8,2048]{1,0:T(8,128)(2,1)S(1)} %fusion.83), channel_id=1, replica_groups=mesh['dp'=32,'tensor'=8] {'tensor'}, dimensions={0}, use_global_device_ids=true | all-gather | bytes 294912 | tf_op jit(solution)/shard_map/all_gather | solution.py:197
  191.7 106.1 %all_to_all.10 = bf16[32,4,8,2048]{3,2,1,0:T(8,128)(2,1)S(1)} all-to-all(bf16[32,4,8,2048]{3,2,1,0:T(8,128)(2,1)S(1)} %bitcast.183), channel_id=1, replica_groups=mesh['dp'=32,'tensor'=8] {'dp'}, dimensions={0} | all-to-all | bytes 8388608 | tf_op jit(solution)/shard_map/all_to_all | solution.py:201
  297.8 2.0 copy-done.2
  301.0 7.4 %convert_bitcast_fusion = bf16[32,4,8,2048]{3,2,0,1:T(8,128)(2,1)} fusion(bf16[4,96,2048]{2,1,0:T(8,128)(2,1)} %param.30, bf16[4,2048,96]{1,2,0:T(8,128)(2,1)} %param.29, bf16[32,4,8,2048]{3,2,1,0:T(8,128)(2,1)} %copy-done.2, f32[32,4,8,96]{3,2,0,1:T(8,128)S(1)} %fusion.27), kind=kOutput, calls=%fused_computation.19 | convolution fusion | flops 807993344 | bytes 11927552 | tf_op jit(solution)/shard_map/necf,efd->necd/dot_general | solution.py:206
  308.4 4.7 %copy.211 = bf16[32,4,8,2048]{3,2,1,0:T(8,128)(2,1)} copy(bf16[32,4,8,2048]{3,2,0,1:T(8,128)(2,1)} %convert_bitcast_fusion) | data formatting | bytes 8388608 | tf_op jit(solution)/shard_map/convert_element_type | solution.py:208
  313.1 5.8 %all-to-all-start.1 = ((bf16[32,4,8,2048]{3,2,1,0:T(8,128)(2,1)}), bf16[32,4,8,2048]{3,2,1,0:T(8,128)(2,1)}, u32[]{:S(2)}, u32[]{:S(2)}) async-start(bf16[32,4,8,2048]{3,2,1,0:T(8,128)(2,1)} %copy.211), calls=%async_computation.2 | async-start | bytes 8388608 | tf_op jit(solution)/shard_map/all_to_all | solution.py:205
  319.5 94.2 %all-to-all-done.1 = bf16[32,4,8,2048]{3,2,1,0:T(8,128)(2,1)} async-done(((bf16[32,4,8,2048]{3,2,1,0:T(8,128)(2,1)}), bf16[32,4,8,2048]{3,2,1,0:T(8,128)(2,1)}, u32[]{:S(2)}, u32[]{:S(2)}) %all-to-all-start.1) | async-done | bytes 4194336 | tf_op jit(solution)/shard_map/all_to_all | solution.py:205
  413.7 6.5 %bitcast_convert_fusion = f32[1024,2048]{1,0:T(8,128)} fusion(bf16[32,4,8,2048]{3,2,1,0:T(8,128)(2,1)} %all-to-all-done.1), kind=kLoop, calls=%fused_computation.11 | loop fusion | flops 2097152 | bytes 12582912 | tf_op jit(solution)/shard_map/reshape | solution.py:214
  420.2 8.9 %gather_fusion = f32[512,2048]{1,0:T(8,128)} fusion(f32[1024,2048]{1,0:T(8,128)} %bitcast_convert_fusion, s32[1024]{0:T(1024)S(1)} %pad_clamp_fusion), kind=kCustom, calls=%fused_computation | custom fusion | bytes 8390656 | tf_op jit(solution)/shard_map/gather | solution.py:215
  429.1 4.3 fusion.3
  433.4 30.9 %reduce-scatter.5.cloned.1.call-done = bf16[8,2048]{1,0:T(8,128)(2,1)} async-done(((bf16[64,2048]{1,0:T(8,128)(2,1)}), bf16[8,2048]{1,0:T(8,128)(2,1)}) %reduce-scatter.5.cloned.1.call-update) | async-done | bytes 32784 | tf_op jit(solution)/shard_map/reduce_scatter | solution.py:216
  (164 shorter events, 32.0 us)
Async XLA Ops:
  7.2 133.6 %copy-start = (bf16[512,2048]{1,0:T(8,128)(2,1)S(1)}, bf16[512,2048]{1,0:T(8,128)(2,1)}, u32[]{:S(2)}) copy-start(bf16[512,2048]{1,0:T(8,128)(2,1)} %param.26) | copy-start | bytes 6291460
  7.2 20.3 %copy-start.15 = (f32[128]{0:T(128)S(1)}, f32[128]{0:T(128)}, u32[]{:S(2)}) copy-start(f32[128]{0:T(128)} %param.25) | copy-start | bytes 1540
  7.2 19.7 %copy-start.16 = (f32[128]{0:T(128)S(1)}, f32[128]{0:T(128)}, u32[]{:S(2)}) copy-start(f32[128]{0:T(128)} %param.24) | copy-start | bytes 1540
  7.2 20.0 %copy-start.18 = (s32[2]{0:T(128)S(1)}, s32[2]{0:T(128)}, u32[]{:S(2)}) copy-start(s32[2]{0:T(128)} %param.35) | copy-start | bytes 28
  7.2 20.0 %copy-start.17 = (s32[64]{0:T(128)S(1)}, s32[64]{0:T(128)}, u32[]{:S(2)}) copy-start(s32[64]{0:T(128)} %param.37) | copy-start | bytes 772
  7.2 20.1 %copy-start.19 = (s32[64]{0:T(128)S(1)}, s32[64]{0:T(128)}, u32[]{:S(2)}) copy-start(s32[64]{0:T(128)} %param.36) | copy-start | bytes 772
  7.2 112.0 %all-gather.2.cloned.1.call-start = ((), (), s32[]{:S(2)}) async-start(), calls=%async_computation.4 | async-start | bytes 9437184 | tf_op jit(solution)/shard_map/all_gather | solution.py:14
  27.7 13.7 %copy-start.9 = (bf16[64,128]{1,0:T(8,128)(2,1)}, bf16[64,128]{1,0:T(8,128)(2,1)S(1)}, u32[]{:S(2)}) copy-start(bf16[64,128]{1,0:T(8,128)(2,1)S(1)} %get-tuple-element.258) | copy-start | bytes 49156
  42.5 13.3 %copy-start.7 = (f32[64,4,1,8]{0,3,1,2:T(8,128)}, f32[64,4,1,8]{0,3,1,2:T(8,128)S(1)}, u32[]{:S(2)}) copy-start(f32[64,4,1,8]{0,3,1,2:T(8,128)S(1)} %copy.216) | copy-start | bytes 24580
  57.2 5.4 %copy-start.3 = (bf16[64,2,4,8,128]{4,3,2,1,0:T(8,128)(2,1)S(1)}, bf16[64,2,4,8,128]{4,3,2,1,0:T(8,128)(2,1)}, u32[]{:S(2)}) copy-start(bf16[64,2,4,8,128]{4,3,2,1,0:T(8,128)(2,1)} %get-tuple-element.247) | copy-start | bytes 3145732
  62.5 1.9 copy-start.11
  64.4 17.9 %copy-start.8 = (f32[64,4,1,8]{0,3,1,2:T(8,128)S(1)}, f32[64,4,1,8]{0,3,1,2:T(8,128)}, u32[]{:S(2)}) copy-start(f32[64,4,1,8]{0,3,1,2:T(8,128)} %copy-done.7) | copy-start | bytes 24580
  64.4 111.4 %reduce-scatter.3.cloned.1.call-start = ((), (), s32[]{:S(2)}) async-start(), calls=%async_computation.5 | async-start | bytes 294912 | tf_op jit(solution)/shard_map/reduce_scatter | solution.py:175
  95.8 24.7 %copy-start.5 = (f32[8,64,32]{1,2,0:T(8,128)}, f32[8,64,32]{1,2,0:T(8,128)S(1)}, u32[]{:S(2)}) copy-start(f32[8,64,32]{1,2,0:T(8,128)S(1)} %all_gather.21) | copy-start | bytes 196612
  120.5 21.5 %copy-start.13 = (s32[512]{0:T(512)S(1)}, s32[512]{0:T(512)}, u32[]{:S(2)}) copy-start(s32[512]{0:T(512)} %fusion.67) | copy-start | bytes 6148
  120.5 21.6 %copy-start.12 = (s32[64,8]{0,1:T(8,128)S(1)}, s32[64,8]{0,1:T(8,128)}, u32[]{:S(2)}) copy-start(s32[64,8]{0,1:T(8,128)} %param.31) | copy-start | bytes 6148
  120.6 55.3 %copy-start.4 = (bf16[8,2048]{1,0:T(8,128)(2,1)S(1)}, bf16[8,2048]{1,0:T(8,128)(2,1)}, u32[]{:S(2)}) copy-start(bf16[8,2048]{1,0:T(8,128)(2,1)} %param.20) | copy-start | bytes 98308
  120.6 56.2 %copy-start.14 = (f32[2048]{0:T(1024)S(1)}, f32[2048]{0:T(1024)}, u32[]{:S(2)}) copy-start(f32[2048]{0:T(1024)} %param.27) | copy-start | bytes 24580
  191.7 108.1 %copy-start.20 = (bf16[4,2048,96]{1,2,0:T(8,128)(2,1)S(1)}, bf16[4,2048,96]{1,2,0:T(8,128)(2,1)}, u32[]{:S(2)}) copy-start(bf16[4,2048,96]{1,2,0:T(8,128)(2,1)} %param.28) | copy-start | bytes 4718596
  297.8 2.0 copy-start.2
  313.1 6.2 %copy-start.10 = (f32[64,8]{0,1:T(8,128)S(1)}, f32[64,8]{0,1:T(8,128)}, u32[]{:S(2)}) copy-start(f32[64,8]{0,1:T(8,128)} %param.32) | copy-start | bytes 6148
  313.1 100.6 %all-to-all-start.1 = ((bf16[32,4,8,2048]{3,2,1,0:T(8,128)(2,1)}), bf16[32,4,8,2048]{3,2,1,0:T(8,128)(2,1)}, u32[]{:S(2)}, u32[]{:S(2)}) async-start(bf16[32,4,8,2048]{3,2,1,0:T(8,128)(2,1)} %copy.211), calls=%async_computation.2 | async-start | bytes 8388608 | tf_op jit(solution)/shard_map/all_to_all | solution.py:205
  318.9 145.4 %reduce-scatter.5.cloned.1.call-start = ((), (), s32[]{:S(2)}) async-start(), calls=%async_computation.6 | async-start | bytes 294912 | tf_op jit(solution)/shard_map/reduce_scatter | solution.py:216
  420.2 45.6 %copy-start.1 = (bf16[512,2048]{1,0:T(8,128)(2,1)S(1)}, bf16[512,2048]{1,0:T(8,128)(2,1)}, u32[]{:S(2)}) copy-start(bf16[512,2048]{1,0:T(8,128)(2,1)} %param.26) | copy-start | bytes 6291460
  429.1 35.2 %copy-start.6 = (bf16[8,2048]{1,0:T(8,128)(2,1)S(1)}, bf16[8,2048]{1,0:T(8,128)(2,1)}, u32[]{:S(2)}) copy-start(bf16[8,2048]{1,0:T(8,128)(2,1)} %reduce-scatter.3.cloned.1.call-done) | copy-start | bytes 98308
Sparse Core Ops, SparseCore 0:
  64.5 54.6 all-gather.1
  142.1 33.6 reduce-scatter.2
  433.6 30.7 reduce-scatter.4
where the time goes:
time: 474 us; the launch traced here: 472 us
  waiting for transfers between devices  180 us (38%)
  blocking collectives  172 us (36%)
  other arithmetic  39.7 us (8%)
  local copies, waits for them, and re-layouts  35 us (7%)
  matrix products  24.6 us (5%)
  between operations  14.3 us (3%)
  starting transfers between devices  6.1 us (1%)
    all_to_all x1, blocking collectives, body(): lax.all_to_all(outgoing, 'dp', split_axis=0, concat_axis=0, tiled=True)  106 us
    all_to_all x1, waiting for transfers between devices, body(): lax.all_to_all(jnp.einsum('necf,efd->necd', hidden_units, down_weight, pr...  94.2 us
    reduce_scatter x1, waiting for transfers between devices, body(): lax.psum_scatter(jnp.dot(attn_heads, out_weight, preferred_element_type=j...  32.8 us
    reduce_scatter x1, waiting for transfers between devices, body(): lax.psum_scatter(jnp.sum(share[:, :, None] * picked_rows, axis=1).astype(...  30.9 us
    all_gather x2, blocking collectives, merged(): everything = jax.tree.map(lambda part: lax.all_gather(part, axis), array)  26.3 us
    all_gather x1, waiting for transfers between devices, merged(): everything = jax.tree.map(lambda part: lax.all_gather(part, axis), array)  22.5 us
    all_gather x1, blocking collectives, body(): lax.all_gather(joined, 'tensor', axis=1, tiled=True)  13.3 us
    add x7, other arithmetic, combine_parts(): sums_first * factor_first[..., None]  13.3 us
  transfers between devices with their start and end apart: 4, of which 4 were waited for; matrix products, arithmetic and copies ran while one was open for 2% of the time, Pallas kernels for 0%

commit v1 on v0

--- a/solution.py
+++ b/solution.py
@@ -8,16 +8,6 @@
 EPSILON = 1e-06
 THETA = 1000000.0
 NEGATIVE = -1e30
-
-
-def merged(array, axis, combine):
-    everything = jax.tree.map(lambda part: lax.all_gather(part, axis), array)
-    first = jax.tree.map(lambda part: part[0], everything)
-
-    def hop(k, so_far):
-        return combine(so_far, jax.tree.map(lambda part: part[k], everything))
-
-    return lax.fori_loop(1, lax.axis_size(axis), hop, first)
 
 
 def rms_scale(values, gain):
@@ -34,19 +24,6 @@
     sine = jnp.sin(angles)[:, None, :]
     turned = jnp.concatenate([-values[..., half:], values[..., :half]], axis=-1)
     return values * cosine + turned * sine
-
-
-def combine_parts(first, second):
-    top_first, total_first, sums_first = first
-    top_second, total_second, sums_second = second
-    top_new = jnp.maximum(top_first, top_second)
-    factor_first = jnp.exp(top_first - top_new)
-    factor_second = jnp.exp(top_second - top_new)
-    return (
-        top_new,
-        total_first * factor_first + total_second * factor_second,
-        sums_first * factor_first[..., None] + sums_second * factor_second[..., None],
-    )
 
 
 def body(
@@ -162,14 +139,23 @@
     )
     own_low = own_weights.astype(jnp.bfloat16).astype(jnp.float32)
     sums_local = sums_local + own_low[..., None] * own_values[:, :, None, :]
-    top_local = top_local.reshape(requests, heads_all)
-    total_local = total_local.reshape(requests, heads_all)
-    sums_local = sums_local.reshape(requests, heads_all, head_dim)
-    top_all, total_all, sums_all = merged(
-        (top_local, total_local, sums_local), "tensor", combine_parts
-    )
-    total_mine = lax.dynamic_slice_in_dim(total_all, tensor_rank * heads_here, heads_here, 1)
-    sums_mine = lax.dynamic_slice_in_dim(sums_all, tensor_rank * heads_here, heads_here, 1)
+    packed = jnp.concatenate(
+        [
+            sums_local.reshape(requests, heads_all, head_dim),
+            top_local.reshape(requests, heads_all, 1),
+            total_local.reshape(requests, heads_all, 1),
+        ],
+        axis=2,
+    )
+    packed = packed.reshape(requests, tensor_size, heads_here, head_dim + 2).transpose(1, 0, 2, 3)
+    parts = lax.all_to_all(packed, "tensor", 0, 0, tiled=True)
+    part_sums = parts[..., :head_dim]
+    part_top = parts[..., head_dim]
+    part_total = parts[..., head_dim + 1]
+    top_all = jnp.max(part_top, axis=0)
+    factor = jnp.exp(part_top - top_all[None])
+    total_mine = jnp.sum(part_total * factor, axis=0)
+    sums_mine = jnp.sum(part_sums * factor[..., None], axis=0)
     mixed = sums_mine / total_mine[..., None]
     attn_heads = mixed.reshape(requests, query_cols).astype(jnp.bfloat16)
     attn_out = lax.psum_scatter(
@@ -192,33 +178,35 @@
     code_span = jnp.arange(experts_all * capacity)
     placing = jnp.any(code_of[None, :, :] == code_span[:, None, None], axis=2).astype(jnp.bfloat16)
     share = route_weights / jnp.sum(route_weights, axis=1, keepdims=True)
-    placed = jnp.dot(
-        placing,
-        lax.all_gather(moe_in, "tensor", axis=0, tiled=True),
-        preferred_element_type=jnp.float32,
-    )
-    outgoing = placed.astype(jnp.bfloat16).reshape(owners, local_experts, capacity, model_width)
-    rows = lax.all_to_all(outgoing, "dp", split_axis=0, concat_axis=0, tiled=True)
+    width_here = model_width // tensor_size
+    gathered_in = lax.all_gather(moe_in, "tensor", axis=0, tiled=True)
+    cols_in = lax.dynamic_slice_in_dim(gathered_in, tensor_rank * width_here, width_here, 1)
+    placed = jnp.dot(placing, cols_in, preferred_element_type=jnp.float32)
+    outgoing = placed.astype(jnp.bfloat16).reshape(owners, local_experts * capacity, width_here)
+    arrived = lax.all_to_all(outgoing, "dp", split_axis=0, concat_axis=0, tiled=True)
+    rows = lax.all_gather(arrived, "tensor", axis=2, tiled=True).reshape(
+        owners, local_experts, capacity, model_width
+    )
     gate_val = jnp.einsum("necd,edf->necf", rows, gate_weight, preferred_element_type=jnp.float32)
     lift_val = jnp.einsum("necd,edf->necf", rows, lift_weight, preferred_element_type=jnp.float32)
     hidden_units = (jax.nn.silu(gate_val) * lift_val).astype(jnp.bfloat16)
+    partial_out = jnp.einsum(
+        "necf,efd->necd", hidden_units, down_weight, preferred_element_type=jnp.float32
+    ).astype(jnp.bfloat16)
+    summed_out = lax.psum_scatter(partial_out, "tensor", scatter_dimension=3, tiled=True)
     returned = lax.all_to_all(
-        jnp.einsum(
-            "necf,efd->necd", hidden_units, down_weight, preferred_element_type=jnp.float32
-        ).astype(jnp.bfloat16),
+        summed_out.reshape(owners, local_experts * capacity, width_here),
         "dp",
         split_axis=0,
         concat_axis=0,
         tiled=True,
     ).astype(jnp.float32)
-    returned = returned.reshape(experts_all * capacity, model_width)
+    returned = returned.reshape(experts_all * capacity, width_here)
     picked_rows = returned[code_of]
-    moe_out = lax.psum_scatter(
-        jnp.sum(share[:, :, None] * picked_rows, axis=1).astype(jnp.bfloat16),
-        "tensor",
-        scatter_dimension=0,
-        tiled=True,
-    ).astype(jnp.float32)
+    moe_cols = jnp.sum(share[:, :, None] * picked_rows, axis=1).astype(jnp.bfloat16)
+    moe_out = lax.all_to_all(moe_cols, "tensor", split_axis=0, concat_axis=1, tiled=True).astype(
+        jnp.float32
+    )
     layer_out = (middle.astype(jnp.float32) + moe_out).astype(jnp.bfloat16)
     return (layer_out, new_rows)
 

time: 474 us -> 330 us (0.70)
  blocking collectives: 172 us -> 76.7 us
  waiting for transfers between devices: 180 us -> 148 us
  other arithmetic: 39.7 us -> 24.5 us
  local copies, waits for them, and re-layouts: 35 us -> 21.9 us
  starting transfers between devices: 6.1 us -> 14.9 us
    all_to_all x1, blocking collectives: 106 us -> 28.1 us  [body(): lax.all_to_all(outgoing, 'dp', split_axis=0, concat_axis=0, tiled=True)]
    all_to_all x1 -> x2, waiting for transfers between devices: 94.2 us -> 40.7 us  [the longest x1 26 us: body(): parts = lax.all_to_all(packed, 'tensor', 0, 0, tiled=True)]
    all_gather x3 -> x1, blocking collectives: 39.1 us -> 12.8 us  [body(): gathered_in = lax.all_gather(moe_in, 'tensor', axis=0, tiled=True)]
    add x14 -> x1, other arithmetic: 13.5 us -> 0.02 us  [body(): jnp.sum(pre_weights, axis=(3, 4)) + jnp.sum(suf_weights, axis=3)]
    reduce_scatter x1, waiting for transfers between devices: 30.9 us -> 41.5 us  [body(): lax.psum_scatter(partial_out, 'tensor', scatter_dimension=3, tiled=True)]
    all_gather x1, waiting for transfers between devices: 22.5 us -> 32.7 us  [body(): lax.all_gather(arrived, 'tensor', axis=2, tiled=True)]
    all_to_all x0 -> x1, blocking collectives: none -> 9.21 us  [body(): lax.all_to_all(moe_cols, 'tensor', split_axis=0, concat_axis=1, tiled=True)]
    all_to_all x1 -> x2, starting transfers between devices: 5.76 us -> 14.6 us  [the longest x1 10.3 us: body(): lax.all_to_all(summed_out.reshape(owners, local_experts * capacity, width...]
  transfers between devices with their start and end apart: 4 -> 5, of which waited for: 4 -> 5; matrix products, arithmetic and copies ran while one was open for 2% -> 1% of each run, Pallas kernels for 0% -> 0%
where the time goes in v1:
time: 330 us; the launch traced here: 328 us
  waiting for transfers between devices  148 us (45%)
  blocking collectives  76.7 us (23%)
  matrix products  27.6 us (8%)
  other arithmetic  24.5 us (7%)
  local copies, waits for them, and re-layouts  21.9 us (7%)
  starting transfers between devices  14.9 us (5%)
  between operations  14.3 us (4%)
    reduce_scatter x1, waiting for transfers between devices, body(): lax.psum_scatter(partial_out, 'tensor', scatter_dimension=3, tiled=True)  41.5 us
    reduce_scatter x1, waiting for transfers between devices, body(): lax.psum_scatter(jnp.dot(attn_heads, out_weight, preferred_element_type=j...  33.3 us
    all_gather x1, waiting for transfers between devices, body(): lax.all_gather(arrived, 'tensor', axis=2, tiled=True)  32.7 us
    all_to_all x1, blocking collectives, body(): lax.all_to_all(outgoing, 'dp', split_axis=0, concat_axis=0, tiled=True)  28.1 us
    all_to_all x1, waiting for transfers between devices, body(): parts = lax.all_to_all(packed, 'tensor', 0, 0, tiled=True)  26 us
    all_to_all x1, waiting for transfers between devices, body(): lax.all_to_all(summed_out.reshape(owners, local_experts * capacity, width...  14.7 us
    all_gather x1, blocking collectives, body(): lax.all_gather(joined, 'tensor', axis=1, tiled=True)  13.3 us
    all_gather x1, blocking collectives, body(): piece = lax.all_gather(normed, 'tensor', axis=0, tiled=True)  13.2 us
  transfers between devices with their start and end apart: 5, of which 5 were waited for; matrix products, arithmetic and copies ran while one was open for 1% of the time, Pallas kernels for 0%

profile of v1, /device:TPU:32, one launch (start us, length us, event | category | flops | bytes accessed | tf_op | source)
XLA Modules:
  0.0 328.1 jit_solution(11157573521921684214)
XLA Ops:
  9.1 13.2 %all_gather.12 = bf16[64,2048]{1,0:T(8,128)(2,1)S(1)} all-gather(bf16[8,2048]{1,0:T(8,128)(2,1)S(1)} %fusion.76), channel_id=1, replica_groups=mesh['dp'=32,'tensor'=8] {'tensor'}, dimensions={0}, use_global_device_ids=true | all-gather | bytes 294912 | tf_op jit(solution)/shard_map/all_gather | solution.py:66
  24.5 2.1 fusion.103
  28.0 13.3 %all_gather.13 = bf16[64,5120]{1,0:T(8,128)(2,1)S(1)} all-gather(bf16[64,640]{1,0:T(8,128)(2,1)S(1)} %pad_maximum_fusion), channel_id=1, replica_groups=mesh['dp'=32,'tensor'=8] {'tensor'}, dimensions={1}, use_global_device_ids=true | all-gather | bytes 737280 | tf_op jit(solution)/shard_map/all_gather | solution.py:86
  42.5 2.1 fusion.101
  44.6 2.0 copy.300
  46.8 4.0 %fusion = (f32[64,4,8]{2,0,1:T(8,128)S(1)}, f32[4,64,8,2,256]{4,2,3,1,0:T(8,128)}) fusion(pred[64,2,256]{2,1,0:T(4,128)(4,1)S(1)} %broadcast_and_fusion, bf16[2,256,4,128,1]{1,3,2,0,4:T(8,128)(2,1)} %bitcast.193, bf16[64,4,8,128]{3,2,1,0:T(8,128)(2,1)S(1)} %reshape.324), kind=kOutput, calls=%fused_computation.3 | convolution fusion | flops 271579136 | bytes 5283840 | tf_op jit(solution)/shard_map/rgqd,npgd->rgqnp/dot_general | solution.py:102
  50.9 2.9 slice_bitcast_fusion
  53.9 1.7 select_reduce_fusion
  57.5 4.4 %fusion.7 = f32[64,4,8]{2,0,1:T(8,128)} fusion(f32[4,64,8,2,256]{4,2,3,1,0:T(8,128)} %get-tuple-element.27, f32[64,4,8]{2,0,1:T(8,128)S(1)} %copy.253, pred[64,2,256]{2,1,0:T(4,128)(4,1)S(1)} %broadcast_and_fusion), kind=kLoop, calls=%fused_computation.11 | loop fusion | flops 4192256 | bytes 4243456 | tf_op jit(solution)/shard_map/reduce_sum | solution.py:127
  62.0 3.2 fusion.19
  65.1 1.5 copy.259
  68.0 2.0 fusion.22
  71.4 1.4 copy.265
  72.8 1.4 copy.264
  74.2 3.3 maximum_bitcast_fusion
  77.5 4.3 %all-to-all-start = ((f32[8,64,4,130]{3,1,2,0:T(8,128)}), f32[8,64,4,130]{3,1,2,0:T(8,128)}, u32[]{:S(2)}, u32[]{:S(2)}) async-start(f32[8,64,4,130]{3,1,2,0:T(8,128)} %maximum_bitcast_fusion), calls=%async_computation | async-start | bytes 4194304 | tf_op jit(solution)/shard_map/all_to_all | solution.py:151
  83.0 26.0 %all-to-all-done = f32[8,64,4,130]{3,1,2,0:T(8,128)} async-done(((f32[8,64,4,130]{3,1,2,0:T(8,128)}), f32[8,64,4,130]{3,1,2,0:T(8,128)}, u32[]{:S(2)}, u32[]{:S(2)}) %all-to-all-start) | async-done | bytes 1064992 | tf_op jit(solution)/shard_map/all_to_all | solution.py:151
  109.0 3.0 fusion.100
  112.0 1.6 copy.303
  114.0 1.6 fusion.51
  117.9 33.3 %reduce-scatter.3.cloned.1.call-done = bf16[8,2048]{1,0:T(8,128)(2,1)} async-done(((bf16[64,2048]{1,0:T(8,128)(2,1)}), bf16[8,2048]{1,0:T(8,128)(2,1)}) %reduce-scatter.3.cloned.1.call-update) | async-done | bytes 32784 | tf_op jit(solution)/shard_map/reduce_scatter | solution.py:161
  152.9 12.8 %all_gather.14 = bf16[64,2048]{1,0:T(8,128)(2,1)S(1)} all-gather(bf16[8,2048]{1,0:T(8,128)(2,1)S(1)} %fusion.80), channel_id=1, replica_groups=mesh['dp'=32,'tensor'=8] {'tensor'}, dimensions={0}, use_global_device_ids=true | all-gather | bytes 294912 | tf_op jit(solution)/shard_map/all_gather | solution.py:182
  166.1 28.1 %all_to_all.25 = bf16[32,32,256]{2,1,0:T(8,128)(2,1)} all-to-all(bf16[32,32,256]{2,1,0:T(8,128)(2,1)S(1)} %bitcast.192), channel_id=1, replica_groups=mesh['dp'=32,'tensor'=8] {'dp'}, dimensions={0} | all-to-all | bytes 1048576 | tf_op jit(solution)/shard_map/all_to_all | solution.py:186
  194.3 32.7 %all-gather.2.cloned.1.call-done = bf16[32,32,2048]{2,1,0:T(8,128)(2,1)} async-done(((bf16[32,32,256]{2,1,0:T(8,128)(2,1)}), bf16[32,32,2048]{2,1,0:T(8,128)(2,1)}) %all-gather.2.cloned.1.call-update) | async-done | bytes 4194320 | tf_op jit(solution)/shard_map/all_gather | solution.py:187
  227.0 3.9 %fusion.23 = f32[32,4,8,96]{3,2,0,1:T(8,128)S(1)} fusion(bf16[4,2048,96]{1,2,0:T(8,128)(2,1)} %param.26, bf16[32,32,2048]{2,1,0:T(8,128)(2,1)} %all-gather.2.cloned.1.call-done), kind=kOutput, calls=%fused_computation.30 | convolution fusion | flops 402653184 | bytes 6160384 | tf_op jit(solution)/shard_map/necd,edf->necf/dot_general | solution.py:190
  230.9 7.4 %convert_bitcast_fusion = bf16[32,4,8,2048]{3,2,0,1:T(8,128)(2,1)} fusion(bf16[4,96,2048]{2,1,0:T(8,128)(2,1)} %param.28, bf16[4,2048,96]{1,2,0:T(8,128)(2,1)} %param.27, f32[32,4,8,96]{3,2,0,1:T(8,128)S(1)} %fusion.23, bf16[32,32,2048]{2,1,0:T(8,128)(2,1)} %all-gather.2.cloned.1.call-done), kind=kOutput, calls=%fused_computation.6 | convolution fusion | flops 807993344 | bytes 11927552 | tf_op jit(solution)/shard_map/necf,efd->necd/dot_general | solution.py:193
  238.4 41.5 %reduce-scatter.5.cloned.1.call-done = bf16[32,4,8,256]{3,2,0,1:T(8,128)(2,1)} async-done(((bf16[32,4,8,2048]{3,2,0,1:T(8,128)(2,1)}), bf16[32,4,8,256]{3,2,0,1:T(8,128)(2,1)}) %reduce-scatter.5.cloned.1.call-update) | async-done | bytes 524304 | tf_op jit(solution)/shard_map/reduce_scatter | solution.py:196
  279.9 1.9 copy.361
  281.8 10.3 %all-to-all-start.2 = ((bf16[32,32,256]{2,1,0:T(8,128)(2,1)}), bf16[32,32,256]{2,1,0:T(8,128)(2,1)}, u32[]{:S(2)}, u32[]{:S(2)}) async-start(bf16[32,32,256]{2,1,0:T(8,128)(2,1)} %bitcast.184), calls=%async_computation.4 | async-start | bytes 1048576 | tf_op jit(solution)/shard_map/all_to_all | solution.py:197
  292.4 14.7 %all-to-all-done.2 = bf16[32,32,256]{2,1,0:T(8,128)(2,1)} async-done(((bf16[32,32,256]{2,1,0:T(8,128)(2,1)}), bf16[32,32,256]{2,1,0:T(8,128)(2,1)}, u32[]{:S(2)}, u32[]{:S(2)}) %all-to-all-start.2) | async-done | bytes 524320 | tf_op jit(solution)/shard_map/all_to_all | solution.py:197
  308.2 2.2 gather_fusion
  311.7 9.2 %all_to_all.26 = bf16[8,8,256]{2,1,0:T(8,128)(2,1)S(1)} all-to-all(bf16[8,8,256]{2,1,0:T(8,128)(2,1)S(1)} %bitcast.202), channel_id=1, replica_groups=mesh['dp'=32,'tensor'=8] {'tensor'}, dimensions={0} | all-to-all | bytes 65536 | tf_op jit(solution)/shard_map/all_to_all | solution.py:207
  (127 shorter events, 20.7 us)
Async XLA Ops:
  7.2 108.5 %copy-start = (bf16[512,2048]{1,0:T(8,128)(2,1)S(1)}, bf16[512,2048]{1,0:T(8,128)(2,1)}, u32[]{:S(2)}) copy-start(bf16[512,2048]{1,0:T(8,128)(2,1)} %param.24) | copy-start | bytes 6291460
  7.2 20.2 %copy-start.12 = (f32[128]{0:T(128)S(1)}, f32[128]{0:T(128)}, u32[]{:S(2)}) copy-start(f32[128]{0:T(128)} %param.23) | copy-start | bytes 1540
  7.2 19.6 %copy-start.13 = (f32[128]{0:T(128)S(1)}, f32[128]{0:T(128)}, u32[]{:S(2)}) copy-start(f32[128]{0:T(128)} %param.22) | copy-start | bytes 1540
  7.2 19.9 %copy-start.15 = (s32[2]{0:T(128)S(1)}, s32[2]{0:T(128)}, u32[]{:S(2)}) copy-start(s32[2]{0:T(128)} %param.33) | copy-start | bytes 28
  7.2 19.9 %copy-start.14 = (s32[64]{0:T(128)S(1)}, s32[64]{0:T(128)}, u32[]{:S(2)}) copy-start(s32[64]{0:T(128)} %param.35) | copy-start | bytes 772
  7.2 20.1 %copy-start.16 = (s32[64]{0:T(128)S(1)}, s32[64]{0:T(128)}, u32[]{:S(2)}) copy-start(s32[64]{0:T(128)} %param.34) | copy-start | bytes 772
  27.6 13.7 %copy-start.8 = (bf16[64,128]{1,0:T(8,128)(2,1)}, bf16[64,128]{1,0:T(8,128)(2,1)S(1)}, u32[]{:S(2)}) copy-start(bf16[64,128]{1,0:T(8,128)(2,1)S(1)} %get-tuple-element.20) | copy-start | bytes 49156
  42.4 13.3 %copy-start.5 = (f32[64,4,1,8]{0,3,1,2:T(8,128)}, f32[64,4,1,8]{0,3,1,2:T(8,128)S(1)}, u32[]{:S(2)}) copy-start(f32[64,4,1,8]{0,3,1,2:T(8,128)S(1)} %copy.284) | copy-start | bytes 24580
  42.5 8.3 %copy-start.17 = (s32[64]{0:T(128)S(1)}, s32[64]{0:T(128)}, u32[]{:S(2)}) copy-start(s32[64]{0:T(128)} %param.34) | copy-start | bytes 772
  50.9 5.4 %copy-start.7 = (pred[64,16]{1,0:T(8,128)(4,1)}, pred[64,16]{1,0:T(8,128)(4,1)S(1)}, u32[]{:S(2)}) copy-start(pred[64,16]{1,0:T(8,128)(4,1)S(1)} %broadcast_compare_fusion) | copy-start | bytes 3076
  57.5 4.4 %copy-start.1 = (f32[4,64,8,2,256]{4,2,3,1,0:T(8,128)S(1)}, f32[4,64,8,2,256]{4,2,3,1,0:T(8,128)}, u32[]{:S(2)}) copy-start(f32[4,64,8,2,256]{4,2,3,1,0:T(8,128)} %get-tuple-element.27) | copy-start | bytes 12582916
  62.0 4.6 %copy-start.2 = (f32[64,4,8,16]{3,2,1,0:T(8,128)S(1)}, f32[64,4,8,16]{3,2,1,0:T(8,128)}, u32[]{:S(2)}) copy-start(f32[64,4,8,16]{3,2,1,0:T(8,128)} %get-tuple-element.29) | copy-start | bytes 393220
  66.6 4.7 %copy-start.6 = (f32[64,4,1,8]{0,3,1,2:T(8,128)S(1)}, f32[64,4,1,8]{0,3,1,2:T(8,128)}, u32[]{:S(2)}) copy-start(f32[64,4,1,8]{0,3,1,2:T(8,128)} %copy-done.5) | copy-start | bytes 24580
  74.2 7.8 %copy-start.10 = (s32[64,8]{0,1:T(8,128)S(1)}, s32[64,8]{0,1:T(8,128)}, u32[]{:S(2)}) copy-start(s32[64,8]{0,1:T(8,128)} %param.29) | copy-start | bytes 6148
  77.5 31.5 %all-to-all-start = ((f32[8,64,4,130]{3,1,2,0:T(8,128)}), f32[8,64,4,130]{3,1,2,0:T(8,128)}, u32[]{:S(2)}, u32[]{:S(2)}) async-start(f32[8,64,4,130]{3,1,2,0:T(8,128)} %maximum_bitcast_fusion), calls=%async_computation | async-start | bytes 4194304 | tf_op jit(solution)/shard_map/all_to_all | solution.py:151
  81.8 69.4 %reduce-scatter.3.cloned.1.call-start = ((), (), s32[]{:S(2)}) async-start(), calls=%async_computation.6 | async-start | bytes 294912 | tf_op jit(solution)/shard_map/reduce_scatter | solution.py:161
  112.0 39.2 %copy-start.3 = (bf16[8,2048]{1,0:T(8,128)(2,1)S(1)}, bf16[8,2048]{1,0:T(8,128)(2,1)}, u32[]{:S(2)}) copy-start(bf16[8,2048]{1,0:T(8,128)(2,1)} %param.18) | copy-start | bytes 98308
  112.0 40.1 %copy-start.11 = (f32[2048]{0:T(1024)S(1)}, f32[2048]{0:T(1024)}, u32[]{:S(2)}) copy-start(f32[2048]{0:T(1024)} %param.25) | copy-start | bytes 24580
  116.9 110.1 %all-gather.2.cloned.1.call-start = ((), (), s32[]{:S(2)}) async-start(), calls=%async_computation.7 | async-start | bytes 4718592 | tf_op jit(solution)/shard_map/all_gather | solution.py:187
  194.3 85.6 %reduce-scatter.5.cloned.1.call-start = ((), (), s32[]{:S(2)}) async-start(), calls=%async_computation.8 | async-start | bytes 4718592 | tf_op jit(solution)/shard_map/reduce_scatter | solution.py:196
  238.3 54.0 %copy-start.9 = (f32[64,8]{0,1:T(8,128)S(1)}, f32[64,8]{0,1:T(8,128)}, u32[]{:S(2)}) copy-start(f32[64,8]{0,1:T(8,128)} %param.30) | copy-start | bytes 6148
  281.8 39.1 %copy-start.4 = (bf16[8,2048]{1,0:T(8,128)(2,1)S(1)}, bf16[8,2048]{1,0:T(8,128)(2,1)}, u32[]{:S(2)}) copy-start(bf16[8,2048]{1,0:T(8,128)(2,1)} %reduce-scatter.3.cloned.1.call-done) | copy-start | bytes 98308
  281.8 25.3 %all-to-all-start.2 = ((bf16[32,32,256]{2,1,0:T(8,128)(2,1)}), bf16[32,32,256]{2,1,0:T(8,128)(2,1)}, u32[]{:S(2)}, u32[]{:S(2)}) async-start(bf16[32,32,256]{2,1,0:T(8,128)(2,1)} %bitcast.184), calls=%async_computation.4 | async-start | bytes 1048576 | tf_op jit(solution)/shard_map/all_to_all | solution.py:197
Sparse Core Ops, SparseCore 0:
  117.0 34.1 reduce-scatter.2
  194.4 32.5 all-gather.1
  238.5 41.3 reduce-scatter.4

commit v2 on v1

--- a/solution.py
+++ b/solution.py
@@ -3,11 +3,12 @@
 import jax
 import jax.numpy as jnp
 from jax import lax
-from jax.sharding import PartitionSpec as P
+from jax.sharding import Mesh, PartitionSpec as P
 
 EPSILON = 1e-06
 THETA = 1000000.0
 NEGATIVE = -1e30
+TENSOR = ("tx", "tc")
 
 
 def rms_scale(values, gain):
@@ -46,8 +47,12 @@
     suffix_len,
     request_group,
 ):
-    tensor_size = lax.axis_size("tensor")
-    tensor_rank = lax.axis_index("tensor")
+    tensor_size = lax.axis_size(TENSOR)
+    chip_rank = lax.axis_index("tx")
+    core_rank = lax.axis_index("tc")
+    chips = lax.axis_size("tx")
+    tensor_rank = chip_rank * lax.axis_size("tc") + core_rank
+    chunk_rank = core_rank * chips + chip_rank
     dp_rank = lax.axis_index("dp")
     owners = lax.axis_size("dp")
     head_dim = query_gain.shape[0]
@@ -62,8 +67,8 @@
     groups_dev = prefix_cache.shape[0]
     pre_local = prefix_cache.shape[1]
     suf_local = suffix_cache.shape[1]
-    normed = rms_scale(residual_in.astype(jnp.float32), attn_gain).astype(jnp.bfloat16)
-    piece = lax.all_gather(normed, "tensor", axis=0, tiled=True)
+    residual_all = lax.all_gather(residual_in, TENSOR, axis=0, tiled=True)
+    piece = rms_scale(residual_all.astype(jnp.float32), attn_gain).astype(jnp.bfloat16)
     projected = jnp.concatenate(
         [
             jnp.dot(piece, query_weight, preferred_element_type=jnp.float32),
@@ -83,7 +88,7 @@
     keyed = rotate(rms_scale(kv_raw, key_gain), positions)
     new_rows = jnp.where(is_key, keyed, kv_raw).astype(jnp.bfloat16).reshape(requests, kv_cols)
     joined = jnp.concatenate([queries.reshape(requests, query_cols), new_rows], axis=1)
-    every_head = lax.all_gather(joined, "tensor", axis=1, tiled=True).reshape(
+    every_head = lax.all_gather(joined, TENSOR, axis=1, tiled=True).reshape(
         requests, tensor_size, query_cols + kv_cols
     )
     all_queries = every_head[:, :, :query_cols].reshape(requests, kv_heads_all, per_group, head_dim)
@@ -148,7 +153,7 @@
         axis=2,
     )
     packed = packed.reshape(requests, tensor_size, heads_here, head_dim + 2).transpose(1, 0, 2, 3)
-    parts = lax.all_to_all(packed, "tensor", 0, 0, tiled=True)
+    parts = lax.all_to_all(packed, TENSOR, 0, 0, tiled=True)
     part_sums = parts[..., :head_dim]
     part_top = parts[..., head_dim]
     part_total = parts[..., head_dim + 1]
@@ -158,14 +163,13 @@
     sums_mine = jnp.sum(part_sums * factor[..., None], axis=0)
     mixed = sums_mine / total_mine[..., None]
     attn_heads = mixed.reshape(requests, query_cols).astype(jnp.bfloat16)
-    attn_out = lax.psum_scatter(
-        jnp.dot(attn_heads, out_weight, preferred_element_type=jnp.float32).astype(jnp.bfloat16),
-        "tensor",
-        scatter_dimension=0,
-        tiled=True,
-    ).astype(jnp.float32)
-    middle = (residual_in.astype(jnp.float32) + attn_out).astype(jnp.bfloat16)
-    moe_in = rms_scale(middle.astype(jnp.float32), moe_gain).astype(jnp.bfloat16)
+    attn_all = lax.psum(
+        jnp.dot(attn_heads, out_weight, preferred_element_type=jnp.float32), TENSOR
+    )
+    middle_all = (residual_all.astype(jnp.float32) + attn_all).astype(jnp.bfloat16)
+    tokens_here = residual_in.shape[0]
+    middle = lax.dynamic_slice_in_dim(middle_all, tensor_rank * tokens_here, tokens_here, 0)
+    moe_all = rms_scale(middle_all.astype(jnp.float32), moe_gain).astype(jnp.bfloat16)
     local_experts = gate_weight.shape[0]
     experts_all = local_experts * owners
     topk = routes.shape[1]
@@ -179,12 +183,12 @@
     placing = jnp.any(code_of[None, :, :] == code_span[:, None, None], axis=2).astype(jnp.bfloat16)
     share = route_weights / jnp.sum(route_weights, axis=1, keepdims=True)
     width_here = model_width // tensor_size
-    gathered_in = lax.all_gather(moe_in, "tensor", axis=0, tiled=True)
-    cols_in = lax.dynamic_slice_in_dim(gathered_in, tensor_rank * width_here, width_here, 1)
+    cols_in = lax.dynamic_slice_in_dim(moe_all, chunk_rank * width_here, width_here, 1)
     placed = jnp.dot(placing, cols_in, preferred_element_type=jnp.float32)
     outgoing = placed.astype(jnp.bfloat16).reshape(owners, local_experts * capacity, width_here)
     arrived = lax.all_to_all(outgoing, "dp", split_axis=0, concat_axis=0, tiled=True)
-    rows = lax.all_gather(arrived, "tensor", axis=2, tiled=True).reshape(
+    half_rows = lax.all_gather(arrived, "tx", axis=2, tiled=True)
+    rows = lax.all_gather(half_rows, "tc", axis=2, tiled=True).reshape(
         owners, local_experts, capacity, model_width
     )
     gate_val = jnp.einsum("necd,edf->necf", rows, gate_weight, preferred_element_type=jnp.float32)
@@ -193,7 +197,8 @@
     partial_out = jnp.einsum(
         "necf,efd->necd", hidden_units, down_weight, preferred_element_type=jnp.float32
     ).astype(jnp.bfloat16)
-    summed_out = lax.psum_scatter(partial_out, "tensor", scatter_dimension=3, tiled=True)
+    core_out = lax.psum_scatter(partial_out, "tc", scatter_dimension=3, tiled=True)
+    summed_out = lax.psum_scatter(core_out, "tx", scatter_dimension=3, tiled=True)
     returned = lax.all_to_all(
         summed_out.reshape(owners, local_experts * capacity, width_here),
         "dp",
@@ -204,33 +209,39 @@
     returned = returned.reshape(experts_all * capacity, width_here)
     picked_rows = returned[code_of]
     moe_cols = jnp.sum(share[:, :, None] * picked_rows, axis=1).astype(jnp.bfloat16)
-    moe_out = lax.all_to_all(moe_cols, "tensor", split_axis=0, concat_axis=1, tiled=True).astype(
-        jnp.float32
+    moe_chunks = lax.all_to_all(moe_cols, TENSOR, split_axis=0, concat_axis=1, tiled=True)
+    moe_out = (
+        moe_chunks.reshape(tokens_here, chips, tensor_size // chips, width_here)
+        .transpose(0, 2, 1, 3)
+        .reshape(tokens_here, model_width)
+        .astype(jnp.float32)
     )
     layer_out = (middle.astype(jnp.float32) + moe_out).astype(jnp.bfloat16)
     return (layer_out, new_rows)
 
 
 def solution(mesh):
+    cores = mesh.devices.shape[1] // 2
+    split_mesh = Mesh(mesh.devices.reshape(mesh.devices.shape[0], cores, 2), ("dp", "tx", "tc"))
     in_specs = (
-        P(("dp", "tensor"), None),
-        P(),
-        P(None, "tensor"),
-        P(None, "tensor"),
-        P(),
-        P(),
-        P("tensor", None),
-        P(),
-        P("dp", None, "tensor"),
-        P("dp", None, "tensor"),
-        P("dp", "tensor", None),
+        P(("dp", "tx", "tc"), None),
+        P(),
+        P(None, TENSOR),
+        P(None, TENSOR),
+        P(),
+        P(),
+        P(TENSOR, None),
+        P(),
+        P("dp", None, TENSOR),
+        P("dp", None, TENSOR),
+        P("dp", TENSOR, None),
         P("dp", None),
         P("dp", None),
-        P("dp", "tensor", None),
-        P("dp", "tensor", None),
+        P("dp", TENSOR, None),
+        P("dp", TENSOR, None),
         P("dp"),
         P("dp"),
         P("dp"),
     )
-    out_specs = (P(("dp", "tensor"), None), P("dp", "tensor"))
-    return jax.shard_map(body, mesh=mesh, in_specs=in_specs, out_specs=out_specs, check_vma=False)
+    out_specs = (P(("dp", "tx", "tc"), None), P("dp", TENSOR))
+    return jax.shard_map(body, mesh=split_mesh, in_specs=in_specs, out_specs=out_specs, check_vma=False)

time: 330 us -> 392 us (1.19)
  waiting for transfers between devices: 148 us -> 224 us
  blocking collectives: 76.7 us -> 52.4 us
  local copies, waits for them, and re-layouts: 21.9 us -> 27.5 us
    psum x0 -> x1, waiting for transfers between devices: none -> 65.4 us  [body(): lax.psum(jnp.dot(attn_heads, out_weight, preferred_element_type=jnp.float...]
    all_gather x1 -> x2, waiting for transfers between devices: 32.7 us -> 54.9 us  [the longest x1 33.2 us: body(): half_rows = lax.all_gather(arrived, 'tx', axis=2, tiled=True)]
    reduce_scatter x2, waiting for transfers between devices: 74.8 us -> 54.6 us  [the longest x1 35.9 us: body(): lax.psum_scatter(core_out, 'tx', scatter_dimension=3, tiled=True)]
    all_gather x3 -> x2, blocking collectives: 39.3 us -> 26.9 us  [the longest x1 13.5 us: body(): residual_all = lax.all_gather(residual_in, TENSOR, axis=0, tiled=True)]
    all_to_all x1 -> x0, blocking collectives: 9.21 us -> none  [body(): lax.all_to_all(moe_cols, 'tensor', split_axis=0, concat_axis=1, tiled=True)]
    all_to_all x1 -> x2, waiting for transfers between devices: 26 us -> 31.2 us  [the longest x1 25.8 us: body(): parts = lax.all_to_all(packed, TENSOR, 0, 0, tiled=True)]
    unnamed x44 -> x42, local copies, waits for them, and re-layouts: 8.22 us -> 8.87 us
  transfers between devices with their start and end apart: 5 -> 8, of which waited for: 5 -> 8; matrix products, arithmetic and copies ran while one was open for 1% -> 1% of each run, Pallas kernels for 0% -> 0%
where the time goes in v2:
time: 392 us; the launch traced here: 391 us
  waiting for transfers between devices  224 us (57%)
  blocking collectives  52.4 us (13%)
  matrix products  29.2 us (7%)
  local copies, waits for them, and re-layouts  27.5 us (7%)
  other arithmetic  25.3 us (6%)
  starting transfers between devices  18.2 us (5%)
  between operations  14.4 us (4%)
    psum x1, waiting for transfers between devices, body(): lax.psum(jnp.dot(attn_heads, out_weight, preferred_element_type=jnp.float...  65.4 us
    reduce_scatter x1, waiting for transfers between devices, body(): lax.psum_scatter(core_out, 'tx', scatter_dimension=3, tiled=True)  35.9 us
    all_gather x1, waiting for transfers between devices, body(): half_rows = lax.all_gather(arrived, 'tx', axis=2, tiled=True)  33.2 us
    all_to_all x1, waiting for transfers between devices, body(): parts = lax.all_to_all(packed, TENSOR, 0, 0, tiled=True)  25.8 us
    all_to_all x1, blocking collectives, body(): lax.all_to_all(outgoing, 'dp', split_axis=0, concat_axis=0, tiled=True)  25.5 us
    all_gather x1, waiting for transfers between devices, body(): lax.all_gather(half_rows, 'tc', axis=2, tiled=True)  21.8 us
    reduce_scatter x1, waiting for transfers between devices, body(): lax.psum_scatter(partial_out, 'tc', scatter_dimension=3, tiled=True)  18.7 us
    all_to_all x1, waiting for transfers between devices, body(): lax.all_to_all(summed_out.reshape(owners, local_experts * capacity, width...  17.3 us
  transfers between devices with their start and end apart: 8, of which 8 were waited for; matrix products, arithmetic and copies ran while one was open for 1% of the time, Pallas kernels for 0%

profile of v2, /device:TPU:32, one launch (start us, length us, event | category | flops | bytes accessed | tf_op | source)
XLA Modules:
  0.0 390.6 jit_solution(887518312369594651)
XLA Ops:
  7.3 13.5 %all_gather.12 = bf16[64,2048]{1,0:T(8,128)(2,1)S(1)} all-gather(bf16[8,2048]{1,0:T(8,128)(2,1)} %param.18), channel_id=1, replica_groups=mesh['dp'=32,'tx'=4,'tc'=2] {'tx','tc'}, dimensions={0}, use_global_device_ids=true | all-gather | bytes 294912 | tf_op jit(solution)/shard_map/all_gather | solution.py:70
  23.2 2.1 fusion.80
  26.8 13.3 %all_gather.13 = bf16[64,5120]{1,0:T(8,128)(2,1)S(1)} all-gather(bf16[64,640]{1,0:T(8,128)(2,1)S(1)} %pad_maximum_fusion), channel_id=1, replica_groups=mesh['dp'=32,'tx'=4,'tc'=2] {'tx','tc'}, dimensions={1}, use_global_device_ids=true | all-gather | bytes 737280 | tf_op jit(solution)/shard_map/all_gather | solution.py:91
  42.0 2.1 fusion.107
  44.0 2.0 copy.308
  46.2 4.6 %fusion = (f32[64,4,8]{2,0,1:T(8,128)}, f32[4,64,8,2,256]{4,2,3,1,0:T(8,128)}) fusion(pred[64,2,256]{2,1,0:T(4,128)(4,1)S(1)} %broadcast_and_fusion, bf16[2,256,4,128,1]{1,3,2,0,4:T(8,128)(2,1)} %bitcast.194, bf16[64,4,8,128]{3,2,1,0:T(8,128)(2,1)S(1)} %reshape.329), kind=kOutput, calls=%fused_computation.3 | convolution fusion | flops 271579136 | bytes 5283840 | tf_op jit(solution)/shard_map/rgqd,npgd->rgqnp/dot_general | solution.py:107
  50.8 1.6 copy.258
  52.5 2.9 slice_bitcast_fusion
  55.4 2.4 select_reduce_fusion
  62.0 4.4 %fusion.7 = f32[64,4,8]{2,0,1:T(8,128)} fusion(f32[4,64,8,2,256]{4,2,3,1,0:T(8,128)} %get-tuple-element.29, f32[64,4,8]{2,0,1:T(8,128)S(1)} %copy.260, pred[64,2,256]{2,1,0:T(4,128)(4,1)S(1)} %broadcast_and_fusion), kind=kLoop, calls=%fused_computation.11 | loop fusion | flops 4192256 | bytes 4243456 | tf_op jit(solution)/shard_map/reduce_sum | solution.py:132
  66.5 3.2 fusion.19
  72.8 2.0 fusion.22
  80.3 3.3 maximum_bitcast_fusion
  83.5 4.3 %all-to-all-start = ((f32[8,64,4,130]{3,1,2,0:T(8,128)}), f32[8,64,4,130]{3,1,2,0:T(8,128)}, u32[]{:S(2)}, u32[]{:S(2)}) async-start(f32[8,64,4,130]{3,1,2,0:T(8,128)} %maximum_bitcast_fusion), calls=%async_computation | async-start | bytes 4194304 | tf_op jit(solution)/shard_map/all_to_all | solution.py:156
  89.2 25.8 %all-to-all-done = f32[8,64,4,130]{3,1,2,0:T(8,128)} async-done(((f32[8,64,4,130]{3,1,2,0:T(8,128)}), f32[8,64,4,130]{3,1,2,0:T(8,128)}, u32[]{:S(2)}, u32[]{:S(2)}) %all-to-all-start) | async-done | bytes 1064992 | tf_op jit(solution)/shard_map/all_to_all | solution.py:156
  115.0 3.0 fusion.106
  118.1 1.6 copy.311
  124.7 65.4 %all-reduce.2.cloned.1.call-done = f32[64,2048]{1,0:T(8,128)} async-done(((f32[64,2048]{1,0:T(8,128)}), f32[64,2048]{1,0:T(8,128)}) %all-reduce.2.cloned.1.call-update) | async-done | bytes 524304 | tf_op jit(solution)/shard_map/psum | solution.py:166
  192.4 25.5 %all_to_all.25 = bf16[32,32,256]{2,1,0:T(8,128)(2,1)} all-to-all(bf16[32,32,256]{2,1,0:T(8,128)(2,1)S(1)} %bitcast.193), channel_id=1, replica_groups=mesh['dp'=32,'tx'=4,'tc'=2] {'dp'}, dimensions={0} | all-to-all | bytes 1048576 | tf_op jit(solution)/shard_map/all_to_all | solution.py:189
  218.0 33.2 %all-gather.3.cloned.1.call-done = bf16[32,32,1024]{2,1,0:T(8,128)(2,1)} async-done(((bf16[32,32,256]{2,1,0:T(8,128)(2,1)}), bf16[32,32,1024]{2,1,0:T(8,128)(2,1)}) %all-gather.3.cloned.1.call-update) | async-done | bytes 2097168 | tf_op jit(solution)/shard_map/all_gather | solution.py:190
  251.3 21.8 %all-gather.5.cloned.1.call-done = bf16[32,32,2048]{2,1,0:T(8,128)(2,1)} async-done(((bf16[32,32,1024]{2,1,0:T(8,128)(2,1)}), bf16[32,32,2048]{2,1,0:T(8,128)(2,1)}) %all-gather.5.cloned.1.call-update) | async-done | bytes 4194320 | tf_op jit(solution)/shard_map/all_gather | solution.py:191
  273.0 3.9 %fusion.23 = f32[32,4,8,96]{3,2,0,1:T(8,128)S(1)} fusion(bf16[4,2048,96]{1,2,0:T(8,128)(2,1)} %param.26, bf16[32,32,2048]{2,1,0:T(8,128)(2,1)} %all-gather.5.cloned.1.call-done), kind=kOutput, calls=%fused_computation.29 | convolution fusion | flops 402653184 | bytes 6160384 | tf_op jit(solution)/shard_map/necd,edf->necf/dot_general | solution.py:194
  276.9 7.4 %convert_bitcast_fusion = bf16[32,4,8,2048]{3,2,0,1:T(8,128)(2,1)} fusion(bf16[4,96,2048]{2,1,0:T(8,128)(2,1)} %param.28, bf16[4,2048,96]{1,2,0:T(8,128)(2,1)} %param.27, f32[32,4,8,96]{3,2,0,1:T(8,128)S(1)} %fusion.23, bf16[32,32,2048]{2,1,0:T(8,128)(2,1)} %all-gather.5.cloned.1.call-done), kind=kOutput, calls=%fused_computation.6 | convolution fusion | flops 807993344 | bytes 11927552 | tf_op jit(solution)/shard_map/necf,efd->necd/dot_general | solution.py:197
  284.4 18.7 %reduce-scatter.3.cloned.1.call-done = bf16[32,4,8,1024]{3,2,0,1:T(8,128)(2,1)} async-done(((bf16[32,4,8,2048]{3,2,0,1:T(8,128)(2,1)}), bf16[32,4,8,1024]{3,2,0,1:T(8,128)(2,1)}) %reduce-scatter.3.cloned.1.call-update) | async-done | bytes 2097168 | tf_op jit(solution)/shard_map/reduce_scatter | solution.py:200
  303.1 35.9 %reduce-scatter.5.cloned.1.call-done = bf16[32,4,8,256]{3,2,0,1:T(8,128)(2,1)} async-done(((bf16[32,4,8,1024]{3,2,0,1:T(8,128)(2,1)}), bf16[32,4,8,256]{3,2,0,1:T(8,128)(2,1)}) %reduce-scatter.5.cloned.1.call-update) | async-done | bytes 524304 | tf_op jit(solution)/shard_map/reduce_scatter | solution.py:201
  339.1 1.9 copy.369
  341.0 10.1 %all-to-all-start.2 = ((bf16[32,32,256]{2,1,0:T(8,128)(2,1)}), bf16[32,32,256]{2,1,0:T(8,128)(2,1)}, u32[]{:S(2)}, u32[]{:S(2)}) async-start(bf16[32,32,256]{2,1,0:T(8,128)(2,1)} %bitcast.185), calls=%async_computation.4 | async-start | bytes 1048576 | tf_op jit(solution)/shard_map/all_to_all | solution.py:202
  351.4 17.3 %all-to-all-done.2 = bf16[32,32,256]{2,1,0:T(8,128)(2,1)} async-done(((bf16[32,32,256]{2,1,0:T(8,128)(2,1)}), bf16[32,32,256]{2,1,0:T(8,128)(2,1)}, u32[]{:S(2)}, u32[]{:S(2)}) %all-to-all-start.2) | async-done | bytes 524320 | tf_op jit(solution)/shard_map/all_to_all | solution.py:202
  369.8 2.2 gather_fusion
  372.1 1.9 fusion.58
  373.9 3.3 all-to-all-start.3
  377.3 5.4 %all-to-all-done.3 = bf16[8,8,256]{2,1,0:T(8,128)(2,1)S(1)} async-done(((bf16[8,8,256]{2,1,0:T(8,128)(2,1)}), bf16[8,8,256]{2,1,0:T(8,128)(2,1)S(1)}, u32[]{:S(2)}, u32[]{:S(2)}) %all-to-all-start.3) | async-done | bytes 32800 | tf_op jit(solution)/shard_map/all_to_all | solution.py:212
  (132 shorter events, 30.0 us)
Async XLA Ops:
  7.2 114.5 %copy-start = (bf16[512,2048]{1,0:T(8,128)(2,1)S(1)}, bf16[512,2048]{1,0:T(8,128)(2,1)}, u32[]{:S(2)}) copy-start(bf16[512,2048]{1,0:T(8,128)(2,1)} %param.24) | copy-start | bytes 6291460
  7.2 19.0 %copy-start.9 = (f32[128]{0:T(128)S(1)}, f32[128]{0:T(128)}, u32[]{:S(2)}) copy-start(f32[128]{0:T(128)} %param.23) | copy-start | bytes 1540
  7.2 18.4 %copy-start.10 = (f32[128]{0:T(128)S(1)}, f32[128]{0:T(128)}, u32[]{:S(2)}) copy-start(f32[128]{0:T(128)} %param.22) | copy-start | bytes 1540
  7.2 18.7 %copy-start.12 = (s32[2]{0:T(128)S(1)}, s32[2]{0:T(128)}, u32[]{:S(2)}) copy-start(s32[2]{0:T(128)} %param.33) | copy-start | bytes 28
  7.2 18.7 %copy-start.11 = (s32[64]{0:T(128)S(1)}, s32[64]{0:T(128)}, u32[]{:S(2)}) copy-start(s32[64]{0:T(128)} %param.35) | copy-start | bytes 772
  7.2 18.9 %copy-start.15 = (s32[64]{0:T(128)S(1)}, s32[64]{0:T(128)}, u32[]{:S(2)}) copy-start(s32[64]{0:T(128)} %param.34) | copy-start | bytes 772
  23.2 3.0 copy-start.13
  26.2 14.1 %copy-start.14 = (s32[2]{0:T(128)S(1)}, s32[2]{0:T(128)}, u32[]{:S(2)}) copy-start(s32[2]{0:T(128)} %copy-done.13) | copy-start | bytes 28
  26.4 13.8 %copy-start.6 = (bf16[64,128]{1,0:T(8,128)(2,1)}, bf16[64,128]{1,0:T(8,128)(2,1)S(1)}, u32[]{:S(2)}) copy-start(bf16[64,128]{1,0:T(8,128)(2,1)S(1)} %get-tuple-element.22) | copy-start | bytes 49156
  41.9 10.5 %copy-start.16 = (s32[64]{0:T(128)S(1)}, s32[64]{0:T(128)}, u32[]{:S(2)}) copy-start(s32[64]{0:T(128)} %param.34) | copy-start | bytes 772
  52.5 5.3 %copy-start.5 = (pred[64,16]{1,0:T(8,128)(4,1)}, pred[64,16]{1,0:T(8,128)(4,1)S(1)}, u32[]{:S(2)}) copy-start(pred[64,16]{1,0:T(8,128)(4,1)S(1)} %broadcast_compare_fusion) | copy-start | bytes 3076
  60.2 1.8 copy-start.4
  62.0 4.4 %copy-start.1 = (f32[4,64,8,2,256]{4,2,3,1,0:T(8,128)S(1)}, f32[4,64,8,2,256]{4,2,3,1,0:T(8,128)}, u32[]{:S(2)}) copy-start(f32[4,64,8,2,256]{4,2,3,1,0:T(8,128)} %get-tuple-element.29) | copy-start | bytes 12582916
  66.5 4.7 %copy-start.2 = (f32[64,4,8,16]{3,2,1,0:T(8,128)S(1)}, f32[64,4,8,16]{3,2,1,0:T(8,128)}, u32[]{:S(2)}) copy-start(f32[64,4,8,16]{3,2,1,0:T(8,128)} %get-tuple-element.31) | copy-start | bytes 393220
  80.3 7.8 %copy-start.8 = (s32[64,8]{0,1:T(8,128)S(1)}, s32[64,8]{0,1:T(8,128)}, u32[]{:S(2)}) copy-start(s32[64,8]{0,1:T(8,128)} %param.29) | copy-start | bytes 6148
  83.5 31.5 %all-to-all-start = ((f32[8,64,4,130]{3,1,2,0:T(8,128)}), f32[8,64,4,130]{3,1,2,0:T(8,128)}, u32[]{:S(2)}, u32[]{:S(2)}) async-start(f32[8,64,4,130]{3,1,2,0:T(8,128)} %maximum_bitcast_fusion), calls=%async_computation | async-start | bytes 4194304 | tf_op jit(solution)/shard_map/all_to_all | solution.py:156
  87.9 102.2 %all-reduce.2.cloned.1.call-start = ((), (), s32[]{:S(2)}) async-start(), calls=%async_computation.6 | async-start | bytes 1048576 | tf_op jit(solution)/shard_map/psum | solution.py:166
  123.1 128.1 %all-gather.3.cloned.1.call-start = ((), (), s32[]{:S(2)}) async-start(), calls=%async_computation.7 | async-start | bytes 2621440 | tf_op jit(solution)/shard_map/all_gather | solution.py:190
  191.3 0.7 copy-start.3
  218.0 55.0 %all-gather.5.cloned.1.call-start = ((), (), s32[]{:S(2)}) async-start(), calls=%async_computation.8 | async-start | bytes 6291456 | tf_op jit(solution)/shard_map/all_gather | solution.py:191
  251.2 51.9 %reduce-scatter.3.cloned.1.call-start = ((), (), s32[]{:S(2)}) async-start(), calls=%async_computation.9 | async-start | bytes 6291456 | tf_op jit(solution)/shard_map/reduce_scatter | solution.py:200
  284.3 67.0 %copy-start.7 = (f32[64,8]{0,1:T(8,128)S(1)}, f32[64,8]{0,1:T(8,128)}, u32[]{:S(2)}) copy-start(f32[64,8]{0,1:T(8,128)} %param.30) | copy-start | bytes 6148
  284.4 54.7 %reduce-scatter.5.cloned.1.call-start = ((), (), s32[]{:S(2)}) async-start(), calls=%async_computation.10 | async-start | bytes 2621440 | tf_op jit(solution)/shard_map/reduce_scatter | solution.py:201
  341.0 27.7 %all-to-all-start.2 = ((bf16[32,32,256]{2,1,0:T(8,128)(2,1)}), bf16[32,32,256]{2,1,0:T(8,128)(2,1)}, u32[]{:S(2)}, u32[]{:S(2)}) async-start(bf16[32,32,256]{2,1,0:T(8,128)(2,1)} %bitcast.185), calls=%async_computation.4 | async-start | bytes 1048576 | tf_op jit(solution)/shard_map/all_to_all | solution.py:202
  373.9 8.7 %all-to-all-start.3 = ((bf16[8,8,256]{2,1,0:T(8,128)(2,1)}), bf16[8,8,256]{2,1,0:T(8,128)(2,1)S(1)}, u32[]{:S(2)}, u32[]{:S(2)}) async-start(bf16[8,8,256]{2,1,0:T(8,128)(2,1)} %bitcast.163), calls=%async_computation.5 | async-start | bytes 65536 | tf_op jit(solution)/shard_map/all_to_all | solution.py:212
Sparse Core Ops, SparseCore 0:
  123.2 66.8 all-reduce.1
  218.1 33.0 all-gather.2
  253.0 19.9 all-gather.4
  284.5 18.5 reduce-scatter.2
  305.5 33.5 reduce-scatter.4

commit v3 on v1

--- a/solution.py
+++ b/solution.py
@@ -62,8 +62,8 @@
     groups_dev = prefix_cache.shape[0]
     pre_local = prefix_cache.shape[1]
     suf_local = suffix_cache.shape[1]
-    normed = rms_scale(residual_in.astype(jnp.float32), attn_gain).astype(jnp.bfloat16)
-    piece = lax.all_gather(normed, "tensor", axis=0, tiled=True)
+    residual_all = lax.all_gather(residual_in, "tensor", axis=0, tiled=True)
+    piece = rms_scale(residual_all.astype(jnp.float32), attn_gain).astype(jnp.bfloat16)
     projected = jnp.concatenate(
         [
             jnp.dot(piece, query_weight, preferred_element_type=jnp.float32),
@@ -158,14 +158,24 @@
     sums_mine = jnp.sum(part_sums * factor[..., None], axis=0)
     mixed = sums_mine / total_mine[..., None]
     attn_heads = mixed.reshape(requests, query_cols).astype(jnp.bfloat16)
-    attn_out = lax.psum_scatter(
+    width_here = model_width // tensor_size
+    tokens_here = residual_in.shape[0]
+    attn_parts = lax.all_to_all(
         jnp.dot(attn_heads, out_weight, preferred_element_type=jnp.float32).astype(jnp.bfloat16),
         "tensor",
-        scatter_dimension=0,
+        split_axis=1,
+        concat_axis=0,
         tiled=True,
-    ).astype(jnp.float32)
-    middle = (residual_in.astype(jnp.float32) + attn_out).astype(jnp.bfloat16)
-    moe_in = rms_scale(middle.astype(jnp.float32), moe_gain).astype(jnp.bfloat16)
+    ).reshape(tensor_size, requests, width_here)
+    attn_cols = jnp.sum(attn_parts.astype(jnp.float32), axis=0)
+    residual_cols = lax.dynamic_slice_in_dim(residual_all, tensor_rank * width_here, width_here, 1)
+    middle_cols = (residual_cols.astype(jnp.float32) + attn_cols).astype(jnp.bfloat16)
+    middle_wide = middle_cols.astype(jnp.float32)
+    square_sum = lax.psum(jnp.sum(middle_wide * middle_wide, axis=1, keepdims=True), "tensor")
+    gain_cols = lax.dynamic_slice_in_dim(moe_gain, tensor_rank * width_here, width_here, 0)
+    cols_in = (
+        middle_wide * lax.rsqrt(square_sum / model_width + EPSILON) * gain_cols
+    ).astype(jnp.bfloat16)
     local_experts = gate_weight.shape[0]
     experts_all = local_experts * owners
     topk = routes.shape[1]
@@ -178,9 +188,6 @@
     code_span = jnp.arange(experts_all * capacity)
     placing = jnp.any(code_of[None, :, :] == code_span[:, None, None], axis=2).astype(jnp.bfloat16)
     share = route_weights / jnp.sum(route_weights, axis=1, keepdims=True)
-    width_here = model_width // tensor_size
-    gathered_in = lax.all_gather(moe_in, "tensor", axis=0, tiled=True)
-    cols_in = lax.dynamic_slice_in_dim(gathered_in, tensor_rank * width_here, width_here, 1)
     placed = jnp.dot(placing, cols_in, preferred_element_type=jnp.float32)
     outgoing = placed.astype(jnp.bfloat16).reshape(owners, local_experts * capacity, width_here)
     arrived = lax.all_to_all(outgoing, "dp", split_axis=0, concat_axis=0, tiled=True)
@@ -203,11 +210,9 @@
     ).astype(jnp.float32)
     returned = returned.reshape(experts_all * capacity, width_here)
     picked_rows = returned[code_of]
-    moe_cols = jnp.sum(share[:, :, None] * picked_rows, axis=1).astype(jnp.bfloat16)
-    moe_out = lax.all_to_all(moe_cols, "tensor", split_axis=0, concat_axis=1, tiled=True).astype(
-        jnp.float32
-    )
-    layer_out = (middle.astype(jnp.float32) + moe_out).astype(jnp.bfloat16)
+    moe_cols = jnp.sum(share[:, :, None] * picked_rows, axis=1)
+    layer_cols = (middle_wide + moe_cols).astype(jnp.bfloat16)
+    layer_out = lax.all_to_all(layer_cols, "tensor", split_axis=0, concat_axis=1, tiled=True)
     return (layer_out, new_rows)
 
 

time: 330 us -> 310 us (0.939)
  waiting for transfers between devices: 148 us -> 120 us
  local copies, waits for them, and re-layouts: 21.9 us -> 28.2 us
    reduce_scatter x1 -> x0, waiting for transfers between devices: 33.3 us -> none  [body(): lax.psum_scatter(jnp.dot(attn_heads, out_weight, preferred_element_type=j...]
    psum x0 -> x1, blocking collectives: none -> 12.6 us  [body(): lax.psum(jnp.sum(middle_wide * middle_wide, axis=1, keepdims=True), 'tens...]
    all_gather x2 -> x1, blocking collectives: 26 us -> 13.5 us  [body(): residual_all = lax.all_gather(residual_in, 'tensor', axis=0, tiled=True)]
    all_to_all x0 -> x1, waiting for transfers between devices: none -> 5.82 us  [body(): lax.all_to_all(jnp.dot(attn_heads, out_weight, preferred_element_type=jnp...]
    all_to_all x0 -> x1, starting transfers between devices: none -> 3.41 us  [body(): lax.all_to_all(jnp.dot(attn_heads, out_weight, preferred_element_type=jnp...]
    unnamed x44 -> x41, local copies, waits for them, and re-layouts: 8.22 us -> 8.82 us
where the time goes in v3:
time: 310 us; the launch traced here: 309 us
  waiting for transfers between devices  120 us (39%)
  blocking collectives  77.4 us (25%)
  matrix products  28.4 us (9%)
  local copies, waits for them, and re-layouts  28.2 us (9%)
  other arithmetic  22.2 us (7%)
  starting transfers between devices  18.2 us (6%)
  between operations  14.6 us (5%)
    reduce_scatter x1, waiting for transfers between devices, body(): lax.psum_scatter(partial_out, 'tensor', scatter_dimension=3, tiled=True)  41.5 us
    all_gather x1, waiting for transfers between devices, body(): lax.all_gather(arrived, 'tensor', axis=2, tiled=True)  31.8 us
    all_to_all x1, blocking collectives, body(): lax.all_to_all(outgoing, 'dp', split_axis=0, concat_axis=0, tiled=True)  28.7 us
    all_to_all x1, waiting for transfers between devices, body(): parts = lax.all_to_all(packed, 'tensor', 0, 0, tiled=True)  25.9 us
    all_to_all x1, waiting for transfers between devices, body(): lax.all_to_all(summed_out.reshape(owners, local_experts * capacity, width...  14.7 us
    all_gather x1, blocking collectives, body(): residual_all = lax.all_gather(residual_in, 'tensor', axis=0, tiled=True)  13.5 us
    all_gather x1, blocking collectives, body(): lax.all_gather(joined, 'tensor', axis=1, tiled=True)  13.3 us
    psum x1, blocking collectives, body(): lax.psum(jnp.sum(middle_wide * middle_wide, axis=1, keepdims=True), 'tens...  12.6 us
  transfers between devices with their start and end apart: 5, of which 5 were waited for; matrix products, arithmetic and copies ran while one was open for 1% of the time, Pallas kernels for 0%

profile of v3, /device:TPU:32, one launch (start us, length us, event | category | flops | bytes accessed | tf_op | source)
XLA Modules:
  0.0 308.8 jit_solution(2888269864150196117)
XLA Ops:
  7.3 13.5 %all_gather.9 = bf16[64,2048]{1,0:T(8,128)(2,1)S(1)} all-gather(bf16[8,2048]{1,0:T(8,128)(2,1)} %param.18), channel_id=1, replica_groups=mesh['dp'=32,'tensor'=8] {'tensor'}, dimensions={0}, use_global_device_ids=true | all-gather | bytes 294912 | tf_op jit(solution)/shard_map/all_gather | solution.py:65
  23.2 2.1 fusion.79
  26.8 13.3 %all_gather.10 = bf16[64,5120]{1,0:T(8,128)(2,1)S(1)} all-gather(bf16[64,640]{1,0:T(8,128)(2,1)S(1)} %pad_maximum_fusion), channel_id=1, replica_groups=mesh['dp'=32,'tensor'=8] {'tensor'}, dimensions={1}, use_global_device_ids=true | all-gather | bytes 737280 | tf_op jit(solution)/shard_map/all_gather | solution.py:86
  41.9 2.1 fusion.106
  44.0 2.0 copy.306
  46.2 4.6 %fusion = (f32[64,4,8]{2,0,1:T(8,128)}, f32[4,64,8,2,256]{4,2,3,1,0:T(8,128)}) fusion(pred[64,2,256]{2,1,0:T(4,128)(4,1)S(1)} %broadcast_and_fusion, bf16[2,256,4,128,1]{1,3,2,0,4:T(8,128)(2,1)} %bitcast.197, bf16[64,4,8,128]{3,2,1,0:T(8,128)(2,1)S(1)} %reshape.317), kind=kOutput, calls=%fused_computation.3 | convolution fusion | flops 271579136 | bytes 5283840 | tf_op jit(solution)/shard_map/rgqd,npgd->rgqnp/dot_general | solution.py:102
  50.8 1.6 copy.256
  52.5 2.9 slice_bitcast_fusion
  55.4 2.4 select_reduce_fusion
  62.0 4.4 %fusion.7 = f32[64,4,8]{2,0,1:T(8,128)} fusion(f32[4,64,8,2,256]{4,2,3,1,0:T(8,128)} %get-tuple-element.29, f32[64,4,8]{2,0,1:T(8,128)S(1)} %copy.258, pred[64,2,256]{2,1,0:T(4,128)(4,1)S(1)} %broadcast_and_fusion), kind=kLoop, calls=%fused_computation.11 | loop fusion | flops 4192256 | bytes 4243456 | tf_op jit(solution)/shard_map/reduce_sum | solution.py:127
  66.5 3.2 %fusion.19 = f32[64,4,8,128]{3,2,0,1:T(8,128)} fusion(f32[4,64,8,2,256]{4,2,3,1,0:T(8,128)S(1)} %copy-done.1, f32[64,4,8]{2,0,1:T(8,128)} %copy-done.3, pred[64,2,256]{2,1,0:T(4,128)(4,1)S(1)} %broadcast_and_fusion, bf16[2,256,4,128,1]{1,3,2,0,4:T(8,128)(2,1)} %bitcast.201), kind=kOutput, calls=%fused_computation.25 | convolution fusion | flops 272629760 | bytes 5808128 | tf_op jit(solution)/shard_map/rgqnp,npgd->rgqd/dot_general | solution.py:128
  71.2 1.6 fusion.53
  72.8 2.0 fusion.22
  80.3 3.3 %maximum_bitcast_fusion = f32[8,64,4,130]{3,1,2,0:T(8,128)} fusion(f32[64,8,4,1]{3,0,2,1:T(8,128)} %copy.270, f32[64,8,4,1]{3,0,2,1:T(8,128)} %copy.269, f32[64,8,4,128]{3,0,2,1:T(8,128)S(1)} %bitcast.192), kind=kLoop, calls=%fused_computation.15 | loop fusion | flops 532480 | bytes 2129920 | tf_op jit(solution)/shard_map/transpose | solution.py:150
  83.5 4.5 %all-to-all-start = ((f32[8,64,4,130]{3,1,2,0:T(8,128)}), f32[8,64,4,130]{3,1,2,0:T(8,128)}, u32[]{:S(2)}, u32[]{:S(2)}) async-start(f32[8,64,4,130]{3,1,2,0:T(8,128)} %maximum_bitcast_fusion), calls=%async_computation | async-start | bytes 4194304 | tf_op jit(solution)/shard_map/all_to_all | solution.py:151
  89.2 25.9 %all-to-all-done = f32[8,64,4,130]{3,1,2,0:T(8,128)} async-done(((f32[8,64,4,130]{3,1,2,0:T(8,128)}), f32[8,64,4,130]{3,1,2,0:T(8,128)}, u32[]{:S(2)}, u32[]{:S(2)}) %all-to-all-start) | async-done | bytes 1064992 | tf_op jit(solution)/shard_map/all_to_all | solution.py:151
  115.0 3.0 fusion.105
  118.1 1.6 copy.309
  120.1 1.6 fusion.51
  122.9 3.4 %all-to-all-start.1 = ((bf16[64,8,256]{2,0,1:T(8,128)(2,1)}), bf16[64,8,256]{2,0,1:T(8,128)(2,1)S(1)}, u32[]{:S(2)}, u32[]{:S(2)}) async-start(bf16[64,8,256]{2,0,1:T(8,128)(2,1)} %bitcast.188), calls=%async_computation.1 | async-start | bytes 524288 | tf_op jit(solution)/shard_map/all_to_all | solution.py:163
  128.0 5.8 %all-to-all-done.1 = bf16[64,8,256]{2,0,1:T(8,128)(2,1)S(1)} async-done(((bf16[64,8,256]{2,0,1:T(8,128)(2,1)}), bf16[64,8,256]{2,0,1:T(8,128)(2,1)S(1)}, u32[]{:S(2)}, u32[]{:S(2)}) %all-to-all-start.1) | async-done | bytes 262176 | tf_op jit(solution)/shard_map/all_to_all | solution.py:163
  133.9 12.6 %psum.7 = f32[64,1]{0,1:T(1,128)S(1)} all-reduce(f32[64,1]{0,1:T(1,128)S(1)} %bitcast.209), channel_id=1, replica_groups=mesh['dp'=32,'tensor'=8] {'tensor'}, use_global_device_ids=true, to_apply=%region_18.19 | all-reduce | flops 64 | bytes 512 | tf_op jit(solution)/shard_map/psum | solution.py:174
  147.0 28.7 %all_to_all.47 = bf16[32,32,256]{2,1,0:T(8,128)(2,1)} all-to-all(bf16[32,32,256]{2,1,0:T(8,128)(2,1)S(1)} %bitcast.196), channel_id=1, replica_groups=mesh['dp'=32,'tensor'=8] {'dp'}, dimensions={0} | all-to-all | bytes 1048576 | tf_op jit(solution)/shard_map/all_to_all | solution.py:193
  175.8 31.8 %all-gather.2.cloned.1.call-done = bf16[32,32,2048]{2,1,0:T(8,128)(2,1)} async-done(((bf16[32,32,256]{2,1,0:T(8,128)(2,1)}), bf16[32,32,2048]{2,1,0:T(8,128)(2,1)}) %all-gather.2.cloned.1.call-update) | async-done | bytes 4194320 | tf_op jit(solution)/shard_map/all_gather | solution.py:194
  207.5 3.9 %fusion.23 = f32[32,4,8,96]{3,2,0,1:T(8,128)S(1)} fusion(bf16[4,2048,96]{1,2,0:T(8,128)(2,1)} %param.26, bf16[32,32,2048]{2,1,0:T(8,128)(2,1)} %all-gather.2.cloned.1.call-done), kind=kOutput, calls=%fused_computation.30 | convolution fusion | flops 402653184 | bytes 6160384 | tf_op jit(solution)/shard_map/necd,edf->necf/dot_general | solution.py:197
  211.5 7.4 %convert_bitcast_fusion = bf16[32,4,8,2048]{3,2,0,1:T(8,128)(2,1)} fusion(bf16[4,96,2048]{2,1,0:T(8,128)(2,1)} %param.28, bf16[4,2048,96]{1,2,0:T(8,128)(2,1)} %param.27, f32[32,4,8,96]{3,2,0,1:T(8,128)S(1)} %fusion.23, bf16[32,32,2048]{2,1,0:T(8,128)(2,1)} %all-gather.2.cloned.1.call-done), kind=kOutput, calls=%fused_computation.6 | convolution fusion | flops 807993344 | bytes 11927552 | tf_op jit(solution)/shard_map/necf,efd->necd/dot_general | solution.py:200
  218.9 41.5 %reduce-scatter.2.cloned.1.call-done = bf16[32,4,8,256]{3,2,0,1:T(8,128)(2,1)} async-done(((bf16[32,4,8,2048]{3,2,0,1:T(8,128)(2,1)}), bf16[32,4,8,256]{3,2,0,1:T(8,128)(2,1)}) %reduce-scatter.2.cloned.1.call-update) | async-done | bytes 524304 | tf_op jit(solution)/shard_map/reduce_scatter | solution.py:203
  260.4 1.9 copy.369
  262.4 10.1 %all-to-all-start.3 = ((bf16[32,32,256]{2,1,0:T(8,128)(2,1)}), bf16[32,32,256]{2,1,0:T(8,128)(2,1)}, u32[]{:S(2)}, u32[]{:S(2)}) async-start(bf16[32,32,256]{2,1,0:T(8,128)(2,1)} %bitcast.187), calls=%async_computation.4 | async-start | bytes 1048576 | tf_op jit(solution)/shard_map/all_to_all | solution.py:204
  272.8 14.7 %all-to-all-done.3 = bf16[32,32,256]{2,1,0:T(8,128)(2,1)} async-done(((bf16[32,32,256]{2,1,0:T(8,128)(2,1)}), bf16[32,32,256]{2,1,0:T(8,128)(2,1)}, u32[]{:S(2)}, u32[]{:S(2)}) %all-to-all-start.3) | async-done | bytes 524320 | tf_op jit(solution)/shard_map/all_to_all | solution.py:204
  288.6 2.2 gather_fusion
  292.1 9.2 %all_to_all.48 = bf16[8,8,256]{2,1,0:T(8,128)(2,1)S(1)} all-to-all(bf16[8,8,256]{2,1,0:T(8,128)(2,1)S(1)} %fusion.88), channel_id=1, replica_groups=mesh['dp'=32,'tensor'=8] {'tensor'}, dimensions={0} | all-to-all | bytes 65536 | tf_op jit(solution)/shard_map/all_to_all | solution.py:215
  (123 shorter events, 25.1 us)
Async XLA Ops:
  7.2 114.5 %copy-start = (bf16[512,2048]{1,0:T(8,128)(2,1)S(1)}, bf16[512,2048]{1,0:T(8,128)(2,1)}, u32[]{:S(2)}) copy-start(bf16[512,2048]{1,0:T(8,128)(2,1)} %param.24) | copy-start | bytes 6291460
  7.2 19.0 %copy-start.8 = (f32[128]{0:T(128)S(1)}, f32[128]{0:T(128)}, u32[]{:S(2)}) copy-start(f32[128]{0:T(128)} %param.23) | copy-start | bytes 1540
  7.2 18.4 %copy-start.9 = (f32[128]{0:T(128)S(1)}, f32[128]{0:T(128)}, u32[]{:S(2)}) copy-start(f32[128]{0:T(128)} %param.22) | copy-start | bytes 1540
  7.2 18.7 %copy-start.11 = (s32[2]{0:T(128)S(1)}, s32[2]{0:T(128)}, u32[]{:S(2)}) copy-start(s32[2]{0:T(128)} %param.33) | copy-start | bytes 28
  7.2 18.7 %copy-start.10 = (s32[64]{0:T(128)S(1)}, s32[64]{0:T(128)}, u32[]{:S(2)}) copy-start(s32[64]{0:T(128)} %param.35) | copy-start | bytes 772
  7.2 18.9 %copy-start.14 = (s32[64]{0:T(128)S(1)}, s32[64]{0:T(128)}, u32[]{:S(2)}) copy-start(s32[64]{0:T(128)} %param.34) | copy-start | bytes 772
  23.2 3.0 copy-start.12
  26.2 14.1 %copy-start.13 = (s32[2]{0:T(128)S(1)}, s32[2]{0:T(128)}, u32[]{:S(2)}) copy-start(s32[2]{0:T(128)} %copy-done.12) | copy-start | bytes 28
  26.4 13.8 %copy-start.5 = (bf16[64,128]{1,0:T(8,128)(2,1)}, bf16[64,128]{1,0:T(8,128)(2,1)S(1)}, u32[]{:S(2)}) copy-start(bf16[64,128]{1,0:T(8,128)(2,1)S(1)} %get-tuple-element.35) | copy-start | bytes 49156
  41.9 10.5 %copy-start.15 = (s32[64]{0:T(128)S(1)}, s32[64]{0:T(128)}, u32[]{:S(2)}) copy-start(s32[64]{0:T(128)} %param.34) | copy-start | bytes 772
  52.5 5.3 %copy-start.4 = (pred[64,16]{1,0:T(8,128)(4,1)}, pred[64,16]{1,0:T(8,128)(4,1)S(1)}, u32[]{:S(2)}) copy-start(pred[64,16]{1,0:T(8,128)(4,1)S(1)} %broadcast_compare_fusion) | copy-start | bytes 3076
  60.2 1.8 copy-start.3
  62.0 4.4 %copy-start.1 = (f32[4,64,8,2,256]{4,2,3,1,0:T(8,128)S(1)}, f32[4,64,8,2,256]{4,2,3,1,0:T(8,128)}, u32[]{:S(2)}) copy-start(f32[4,64,8,2,256]{4,2,3,1,0:T(8,128)} %get-tuple-element.29) | copy-start | bytes 12582916
  66.5 4.7 %copy-start.2 = (f32[64,4,8,16]{3,2,1,0:T(8,128)S(1)}, f32[64,4,8,16]{3,2,1,0:T(8,128)}, u32[]{:S(2)}) copy-start(f32[64,4,8,16]{3,2,1,0:T(8,128)} %get-tuple-element.31) | copy-start | bytes 393220
  80.3 7.8 %copy-start.7 = (s32[64,8]{0,1:T(8,128)S(1)}, s32[64,8]{0,1:T(8,128)}, u32[]{:S(2)}) copy-start(s32[64,8]{0,1:T(8,128)} %param.29) | copy-start | bytes 6148
  83.5 31.5 %all-to-all-start = ((f32[8,64,4,130]{3,1,2,0:T(8,128)}), f32[8,64,4,130]{3,1,2,0:T(8,128)}, u32[]{:S(2)}, u32[]{:S(2)}) async-start(f32[8,64,4,130]{3,1,2,0:T(8,128)} %maximum_bitcast_fusion), calls=%async_computation | async-start | bytes 4194304 | tf_op jit(solution)/shard_map/all_to_all | solution.py:151
  122.9 10.8 %all-to-all-start.1 = ((bf16[64,8,256]{2,0,1:T(8,128)(2,1)}), bf16[64,8,256]{2,0,1:T(8,128)(2,1)S(1)}, u32[]{:S(2)}, u32[]{:S(2)}) async-start(bf16[64,8,256]{2,0,1:T(8,128)(2,1)} %bitcast.188), calls=%async_computation.1 | async-start | bytes 524288 | tf_op jit(solution)/shard_map/all_to_all | solution.py:163
  126.4 81.2 %all-gather.2.cloned.1.call-start = ((), (), s32[]{:S(2)}) async-start(), calls=%async_computation.6 | async-start | bytes 4718592 | tf_op jit(solution)/shard_map/all_gather | solution.py:194
  175.7 84.7 %reduce-scatter.2.cloned.1.call-start = ((), (), s32[]{:S(2)}) async-start(), calls=%async_computation.7 | async-start | bytes 4718592 | tf_op jit(solution)/shard_map/reduce_scatter | solution.py:203
  218.9 53.8 %copy-start.6 = (f32[64,8]{0,1:T(8,128)S(1)}, f32[64,8]{0,1:T(8,128)}, u32[]{:S(2)}) copy-start(f32[64,8]{0,1:T(8,128)} %param.30) | copy-start | bytes 6148
  262.4 25.1 %all-to-all-start.3 = ((bf16[32,32,256]{2,1,0:T(8,128)(2,1)}), bf16[32,32,256]{2,1,0:T(8,128)(2,1)}, u32[]{:S(2)}, u32[]{:S(2)}) async-start(bf16[32,32,256]{2,1,0:T(8,128)(2,1)} %bitcast.187), calls=%async_computation.4 | async-start | bytes 1048576 | tf_op jit(solution)/shard_map/all_to_all | solution.py:204
Sparse Core Ops, SparseCore 0:
  175.8 31.6 all-gather.1
  219.0 41.3 reduce-scatter.1

commit v4 on v3

--- a/solution.py
+++ b/solution.py
@@ -189,25 +189,34 @@
     placing = jnp.any(code_of[None, :, :] == code_span[:, None, None], axis=2).astype(jnp.bfloat16)
     share = route_weights / jnp.sum(route_weights, axis=1, keepdims=True)
     placed = jnp.dot(placing, cols_in, preferred_element_type=jnp.float32)
-    outgoing = placed.astype(jnp.bfloat16).reshape(owners, local_experts * capacity, width_here)
-    arrived = lax.all_to_all(outgoing, "dp", split_axis=0, concat_axis=0, tiled=True)
-    rows = lax.all_gather(arrived, "tensor", axis=2, tiled=True).reshape(
-        owners, local_experts, capacity, model_width
-    )
-    gate_val = jnp.einsum("necd,edf->necf", rows, gate_weight, preferred_element_type=jnp.float32)
-    lift_val = jnp.einsum("necd,edf->necf", rows, lift_weight, preferred_element_type=jnp.float32)
-    hidden_units = (jax.nn.silu(gate_val) * lift_val).astype(jnp.bfloat16)
-    partial_out = jnp.einsum(
-        "necf,efd->necd", hidden_units, down_weight, preferred_element_type=jnp.float32
-    ).astype(jnp.bfloat16)
-    summed_out = lax.psum_scatter(partial_out, "tensor", scatter_dimension=3, tiled=True)
-    returned = lax.all_to_all(
-        summed_out.reshape(owners, local_experts * capacity, width_here),
-        "dp",
-        split_axis=0,
-        concat_axis=0,
-        tiled=True,
-    ).astype(jnp.float32)
+    outgoing = placed.astype(jnp.bfloat16).reshape(owners, local_experts, capacity, width_here)
+    chunks = 2 if local_experts % 2 == 0 else 1
+    per_chunk = local_experts // chunks
+    pieces = []
+    for chunk in range(chunks):
+        lo = chunk * per_chunk
+        arrived = lax.all_to_all(
+            outgoing[:, lo : lo + per_chunk], "dp", split_axis=0, concat_axis=0, tiled=True
+        )
+        rows = lax.all_gather(arrived, "tensor", axis=3, tiled=True)
+        gate_val = jnp.einsum(
+            "necd,edf->necf", rows, gate_weight[lo : lo + per_chunk], preferred_element_type=jnp.float32
+        )
+        lift_val = jnp.einsum(
+            "necd,edf->necf", rows, lift_weight[lo : lo + per_chunk], preferred_element_type=jnp.float32
+        )
+        hidden_units = (jax.nn.silu(gate_val) * lift_val).astype(jnp.bfloat16)
+        partial_out = jnp.einsum(
+            "necf,efd->necd",
+            hidden_units,
+            down_weight[lo : lo + per_chunk],
+            preferred_element_type=jnp.float32,
+        ).astype(jnp.bfloat16)
+        summed_out = lax.psum_scatter(partial_out, "tensor", scatter_dimension=3, tiled=True)
+        pieces.append(
+            lax.all_to_all(summed_out, "dp", split_axis=0, concat_axis=0, tiled=True)
+        )
+    returned = jnp.concatenate(pieces, axis=1).astype(jnp.float32)
     returned = returned.reshape(experts_all * capacity, width_here)
     picked_rows = returned[code_of]
     moe_cols = jnp.sum(share[:, :, None] * picked_rows, axis=1)

time: 310 us -> 350 us (1.13)
  waiting for transfers between devices: 120 us -> 133 us
  starting transfers between devices: 18.2 us -> 28.2 us
  blocking collectives: 77.4 us -> 86.6 us
    reduce_scatter x1 -> x2, waiting for transfers between devices: 41.5 us -> 58.8 us  [body(): lax.psum_scatter(partial_out, 'tensor', scatter_dimension=3, tiled=True)]
    all_to_all x1 -> x2, blocking collectives: 28.7 us -> 38.9 us  [body(): lax.all_to_all(outgoing[:, lo:lo + per_chunk], 'dp', split_axis=0, concat...]
    all_to_all x1 -> x2, starting transfers between devices: 10.1 us -> 20 us  [body(): lax.all_to_all(summed_out, 'dp', split_axis=0, concat_axis=0, tiled=True)]
    all_to_all x1 -> x2, waiting for transfers between devices: 14.7 us -> 10.7 us  [body(): lax.all_to_all(summed_out, 'dp', split_axis=0, concat_axis=0, tiled=True)]
    dot_general x2 -> x4, matrix products: 11.3 us -> 14.2 us  [the longest x2 9.27 us: body(): jnp.einsum('necf,efd->necd', hidden_units, down_weight[lo:lo + per_chunk]...]
    all_gather x1 -> x2, waiting for transfers between devices: 31.8 us -> 31.3 us  [body(): rows = lax.all_gather(arrived, 'tensor', axis=3, tiled=True)]
    unnamed x41 -> x37, local copies, waits for them, and re-layouts: 8.82 us -> 8.82 us
  transfers between devices with their start and end apart: 5 -> 8, of which waited for: 5 -> 7; matrix products, arithmetic and copies ran while one was open for 1% -> 6% of each run, Pallas kernels for 0% -> 0%
where the time goes in v4:
time: 350 us; the launch traced here: 348 us
  waiting for transfers between devices  133 us (38%)
  blocking collectives  86.6 us (25%)
  local copies, waits for them, and re-layouts  31.4 us (9%)
  matrix products  30.4 us (9%)
  starting transfers between devices  28.2 us (8%)
  other arithmetic  24.3 us (7%)
  between operations  14.4 us (4%)
    reduce_scatter x2, waiting for transfers between devices, body(): lax.psum_scatter(partial_out, 'tensor', scatter_dimension=3, tiled=True)  58.8 us
    all_to_all x2, blocking collectives, body(): lax.all_to_all(outgoing[:, lo:lo + per_chunk], 'dp', split_axis=0, concat...  38.9 us
    all_gather x2, waiting for transfers between devices, body(): rows = lax.all_gather(arrived, 'tensor', axis=3, tiled=True)  31.3 us
    all_to_all x1, waiting for transfers between devices, body(): parts = lax.all_to_all(packed, 'tensor', 0, 0, tiled=True)  25.9 us
    all_to_all x2, starting transfers between devices, body(): lax.all_to_all(summed_out, 'dp', split_axis=0, concat_axis=0, tiled=True)  20 us
    all_gather x1, blocking collectives, body(): residual_all = lax.all_gather(residual_in, 'tensor', axis=0, tiled=True)  13.4 us
    all_gather x1, blocking collectives, body(): lax.all_gather(joined, 'tensor', axis=1, tiled=True)  13.3 us
    psum x1, blocking collectives, body(): lax.psum(jnp.sum(middle_wide * middle_wide, axis=1, keepdims=True), 'tens...  12.6 us
  transfers between devices with their start and end apart: 8, of which 7 were waited for; matrix products, arithmetic and copies ran while one was open for 6% of the time, Pallas kernels for 0%

profile of v4, /device:TPU:32, one launch (start us, length us, event | category | flops | bytes accessed | tf_op | source)
XLA Modules:
  0.0 347.9 jit_solution(8013380357234976281)
XLA Ops:
  9.6 13.4 %all_gather.12 = bf16[64,2048]{1,0:T(8,128)(2,1)S(1)} all-gather(bf16[8,2048]{1,0:T(8,128)(2,1)} %param.18), channel_id=1, replica_groups=mesh['dp'=32,'tensor'=8] {'tensor'}, dimensions={0}, use_global_device_ids=true | all-gather | bytes 294912 | tf_op jit(solution)/shard_map/all_gather | solution.py:65
  25.5 2.1 fusion.76
  28.9 13.3 %all_gather.13 = bf16[64,5120]{1,0:T(8,128)(2,1)S(1)} all-gather(bf16[64,640]{1,0:T(8,128)(2,1)S(1)} %pad_maximum_fusion.1), channel_id=1, replica_groups=mesh['dp'=32,'tensor'=8] {'tensor'}, dimensions={1}, use_global_device_ids=true | all-gather | bytes 737280 | tf_op jit(solution)/shard_map/all_gather | solution.py:86
  45.2 2.1 fusion.104
  47.3 2.1 copy.318
  49.4 2.9 slice_bitcast_fusion
  55.5 4.6 %fusion = (f32[64,4,8]{2,0,1:T(8,128)}, f32[4,64,8,2,256]{4,2,3,1,0:T(8,128)}) fusion(pred[64,2,256]{2,1,0:T(4,128)(4,1)S(1)} %broadcast_and_fusion, bf16[2,256,4,128,1]{1,3,2,0,4:T(8,128)(2,1)} %bitcast.209, bf16[64,4,8,128]{3,2,1,0:T(8,128)(2,1)S(1)} %reshape.309), kind=kOutput, calls=%fused_computation.3 | convolution fusion | flops 271579136 | bytes 5283840 | tf_op jit(solution)/shard_map/rgqd,npgd->rgqnp/dot_general | solution.py:102
  65.2 4.4 %fusion.3 = f32[64,4,8]{2,0,1:T(8,128)} fusion(f32[4,64,8,2,256]{4,2,3,1,0:T(8,128)} %get-tuple-element.31, f32[64,4,8]{2,0,1:T(8,128)S(1)} %copy.266, pred[64,2,256]{2,1,0:T(4,128)(4,1)S(1)} %broadcast_and_fusion), kind=kLoop, calls=%fused_computation.6 | loop fusion | flops 4192256 | bytes 4243456 | tf_op jit(solution)/shard_map/reduce_sum | solution.py:127
  69.6 3.2 fusion.14
  76.1 1.8 fusion.17
  82.4 3.2 maximum_bitcast_fusion
  85.7 4.7 %all-to-all-start = ((f32[8,64,4,130]{3,1,2,0:T(8,128)}), f32[8,64,4,130]{3,1,2,0:T(8,128)}, u32[]{:S(2)}, u32[]{:S(2)}) async-start(f32[8,64,4,130]{3,1,2,0:T(8,128)} %maximum_bitcast_fusion), calls=%async_computation | async-start | bytes 4194304 | tf_op jit(solution)/shard_map/all_to_all | solution.py:151
  91.5 25.9 %all-to-all-done = f32[8,64,4,130]{3,1,2,0:T(8,128)} async-done(((f32[8,64,4,130]{3,1,2,0:T(8,128)}), f32[8,64,4,130]{3,1,2,0:T(8,128)}, u32[]{:S(2)}, u32[]{:S(2)}) %all-to-all-start) | async-done | bytes 1064992 | tf_op jit(solution)/shard_map/all_to_all | solution.py:151
  117.3 3.1 fusion.103
  125.3 3.4 all-to-all-start.1
  130.4 5.8 %all-to-all-done.1 = bf16[64,8,256]{2,0,1:T(8,128)(2,1)S(1)} async-done(((bf16[64,8,256]{2,0,1:T(8,128)(2,1)}), bf16[64,8,256]{2,0,1:T(8,128)(2,1)S(1)}, u32[]{:S(2)}, u32[]{:S(2)}) %all-to-all-start.1) | async-done | bytes 262176 | tf_op jit(solution)/shard_map/all_to_all | solution.py:163
  136.3 12.6 %psum.7 = f32[64,1]{0,1:T(1,128)S(1)} all-reduce(f32[64,1]{0,1:T(1,128)S(1)} %bitcast.221), channel_id=1, replica_groups=mesh['dp'=32,'tensor'=8] {'tensor'}, use_global_device_ids=true, to_apply=%region_18.19 | all-reduce | flops 64 | bytes 512 | tf_op jit(solution)/shard_map/psum | solution.py:174
  149.4 23.3 %all_to_all.57 = bf16[32,2,8,256]{3,2,1,0:T(8,128)(2,1)S(1)} all-to-all(bf16[32,2,8,256]{3,2,1,0:T(8,128)(2,1)S(1)} %get-tuple-element.20), channel_id=1, replica_groups=mesh['dp'=32,'tensor'=8] {'dp'}, dimensions={0} | all-to-all | bytes 524288 | tf_op jit(solution)/shard_map/all_to_all | solution.py:198
  173.5 15.7 %all_to_all.58 = bf16[32,2,8,256]{3,2,1,0:T(8,128)(2,1)S(1)} all-to-all(bf16[32,2,8,256]{3,2,1,0:T(8,128)(2,1)S(1)} %get-tuple-element.19), channel_id=1, replica_groups=mesh['dp'=32,'tensor'=8] {'dp'}, dimensions={0} | all-to-all | bytes 524288 | tf_op jit(solution)/shard_map/all_to_all | solution.py:198
  189.9 6.3 %all-gather.5.cloned.1.call-done = bf16[32,2,8,2048]{3,2,0,1:T(8,128)(2,1)} async-done(((bf16[32,2,8,256]{3,2,0,1:T(8,128)(2,1)}), bf16[32,2,8,2048]{3,2,0,1:T(8,128)(2,1)}) %all-gather.5.cloned.1.call-update) | async-done | bytes 2097168 | tf_op jit(solution)/shard_map/all_gather | solution.py:201
  196.2 2.5 convolution_bitcast_fusion.1
  198.7 4.6 %fusion.6 = bf16[32,2,8,2048]{3,2,0,1:T(8,128)(2,1)} fusion(bf16[32,2,8,2048]{3,2,0,1:T(8,128)(2,1)} %all-gather.5.cloned.1.call-done, bf16[4,96,2048]{2,1,0:T(8,128)(2,1)} %param.28, bf16[4,2048,96]{1,2,0:T(8,128)(2,1)} %param.27, f32[32,2,8,96]{3,2,0,1:T(8,128)S(1)} %convolution_bitcast_fusion.1), kind=kOutput, calls=%fused_computation.11 | convolution fusion | flops 403996672 | bytes 5963776 | tf_op jit(solution)/shard_map/necf,efd->necd/dot_general | solution.py:209
  203.4 25.0 %all-gather.3.cloned.1.call-done = bf16[32,2,8,2048]{3,2,0,1:T(8,128)(2,1)} async-done(((bf16[32,2,8,256]{3,2,0,1:T(8,128)(2,1)}), bf16[32,2,8,2048]{3,2,0,1:T(8,128)(2,1)}) %all-gather.3.cloned.1.call-update) | async-done | bytes 2097168 | tf_op jit(solution)/shard_map/all_gather | solution.py:201
  228.4 2.5 convolution_bitcast_fusion.3
  230.8 4.7 %fusion.5 = bf16[32,2,8,2048]{3,2,0,1:T(8,128)(2,1)} fusion(bf16[32,2,8,2048]{3,2,0,1:T(8,128)(2,1)} %all-gather.3.cloned.1.call-done, bf16[4,96,2048]{2,1,0:T(8,128)(2,1)} %param.28, bf16[4,2048,96]{1,2,0:T(8,128)(2,1)} %param.27, f32[32,2,8,96]{3,2,0,1:T(8,128)S(1)} %convolution_bitcast_fusion.3), kind=kOutput, calls=%fused_computation.10 | convolution fusion | flops 403996672 | bytes 5963776 | tf_op jit(solution)/shard_map/necf,efd->necd/dot_general | solution.py:209
  235.5 32.8 %reduce-scatter.5.cloned.1.call-done = bf16[32,2,8,256]{3,2,0,1:T(8,128)(2,1)} async-done(((bf16[32,2,8,2048]{3,2,0,1:T(8,128)(2,1)}), bf16[32,2,8,256]{3,2,0,1:T(8,128)(2,1)}) %reduce-scatter.5.cloned.1.call-update) | async-done | bytes 262160 | tf_op jit(solution)/shard_map/reduce_scatter | solution.py:215
  270.0 10.1 %all-to-all-start.5 = ((bf16[32,2,8,256]{3,2,1,0:T(8,128)(2,1)}), bf16[32,2,8,256]{3,2,1,0:T(8,128)(2,1)S(1)}, u32[]{:S(2)}, u32[]{:S(2)}) async-start(bf16[32,2,8,256]{3,2,1,0:T(8,128)(2,1)} %copy.294), calls=%async_computation.7 | async-start | bytes 524288 | tf_op jit(solution)/shard_map/all_to_all | solution.py:217
  280.0 26.1 %reduce-scatter.3.cloned.1.call-done = bf16[32,2,8,256]{3,2,0,1:T(8,128)(2,1)} async-done(((bf16[32,2,8,2048]{3,2,0,1:T(8,128)(2,1)}), bf16[32,2,8,256]{3,2,0,1:T(8,128)(2,1)}) %reduce-scatter.3.cloned.1.call-update) | async-done | bytes 262160 | tf_op jit(solution)/shard_map/reduce_scatter | solution.py:215
  307.8 9.9 %all-to-all-start.3 = ((bf16[32,2,8,256]{3,2,1,0:T(8,128)(2,1)}), bf16[32,2,8,256]{3,2,1,0:T(8,128)(2,1)S(1)}, u32[]{:S(2)}, u32[]{:S(2)}) async-start(bf16[32,2,8,256]{3,2,1,0:T(8,128)(2,1)} %copy.292), calls=%async_computation.4 | async-start | bytes 524288 | tf_op jit(solution)/shard_map/all_to_all | solution.py:217
  318.0 10.7 %all-to-all-done.3 = bf16[32,2,8,256]{3,2,1,0:T(8,128)(2,1)S(1)} async-done(((bf16[32,2,8,256]{3,2,1,0:T(8,128)(2,1)}), bf16[32,2,8,256]{3,2,1,0:T(8,128)(2,1)S(1)}, u32[]{:S(2)}, u32[]{:S(2)}) %all-to-all-start.3) | async-done | bytes 262176 | tf_op jit(solution)/shard_map/all_to_all | solution.py:217
  328.9 2.2 gather_fusion
  332.4 8.3 %all_to_all.59 = bf16[8,8,256]{2,1,0:T(8,128)(2,1)S(1)} all-to-all(bf16[8,8,256]{2,1,0:T(8,128)(2,1)S(1)} %fusion.85), channel_id=1, replica_groups=mesh['dp'=32,'tensor'=8] {'tensor'}, dimensions={0} | all-to-all | bytes 65536 | tf_op jit(solution)/shard_map/all_to_all | solution.py:224
  (135 shorter events, 40.3 us)
Async XLA Ops:
  7.2 116.9 %copy-start = (bf16[512,2048]{1,0:T(8,128)(2,1)S(1)}, bf16[512,2048]{1,0:T(8,128)(2,1)}, u32[]{:S(2)}) copy-start(bf16[512,2048]{1,0:T(8,128)(2,1)} %param.24) | copy-start | bytes 6291460
  23.0 4.9 %copy-start.11 = (f32[128]{0:T(128)S(1)}, f32[128]{0:T(128)}, u32[]{:S(2)}) copy-start(f32[128]{0:T(128)} %param.22) | copy-start | bytes 1540
  24.6 3.6 %copy-start.13 = (s32[64]{0:T(128)S(1)}, s32[64]{0:T(128)}, u32[]{:S(2)}) copy-start(s32[64]{0:T(128)} %param.34) | copy-start | bytes 772
  24.6 3.6 %copy-start.10 = (f32[128]{0:T(128)S(1)}, f32[128]{0:T(128)}, u32[]{:S(2)}) copy-start(f32[128]{0:T(128)} %param.23) | copy-start | bytes 1540
  28.5 13.8 %copy-start.7 = (bf16[64,128]{1,0:T(8,128)(2,1)}, bf16[64,128]{1,0:T(8,128)(2,1)S(1)}, u32[]{:S(2)}) copy-start(bf16[64,128]{1,0:T(8,128)(2,1)S(1)} %get-tuple-element.37) | copy-start | bytes 49156
  28.8 14.2 %copy-start.12 = (s32[2]{0:T(128)S(1)}, s32[2]{0:T(128)}, u32[]{:S(2)}) copy-start(s32[2]{0:T(128)} %param.33) | copy-start | bytes 28
  43.8 8.5 %copy-start.6 = (pred[64,16]{1,0:T(8,128)(4,1)}, pred[64,16]{1,0:T(8,128)(4,1)S(1)}, u32[]{:S(2)}) copy-start(pred[64,16]{1,0:T(8,128)(4,1)S(1)} %broadcast_compare_fusion) | copy-start | bytes 3076
  55.5 7.2 %copy-start.5 = (bf16[64,4,128]{2,1,0:T(4,128)(2,1)S(1)}, bf16[64,4,128]{2,1,0:T(4,128)(2,1)}, u32[]{:S(2)}) copy-start(bf16[64,4,128]{2,1,0:T(4,128)(2,1)} %get-tuple-element.17) | copy-start | bytes 196612
  62.0 7.6 %copy-start.4 = (f32[64,4,8]{2,0,1:T(8,128)}, f32[64,4,8]{2,0,1:T(8,128)S(1)}, u32[]{:S(2)}) copy-start(f32[64,4,8]{2,0,1:T(8,128)S(1)} %copy.266) | copy-start | bytes 24580
  65.2 4.4 %copy-start.1 = (f32[4,64,8,2,256]{4,2,3,1,0:T(8,128)S(1)}, f32[4,64,8,2,256]{4,2,3,1,0:T(8,128)}, u32[]{:S(2)}) copy-start(f32[4,64,8,2,256]{4,2,3,1,0:T(8,128)} %get-tuple-element.31) | copy-start | bytes 12582916
  69.6 4.8 %copy-start.2 = (f32[64,4,8,16]{3,2,1,0:T(8,128)S(1)}, f32[64,4,8,16]{3,2,1,0:T(8,128)}, u32[]{:S(2)}) copy-start(f32[64,4,8,16]{3,2,1,0:T(8,128)} %get-tuple-element.33) | copy-start | bytes 393220
  74.4 1.7 copy-start.3
  85.7 4.7 %copy-start.9 = (s32[64,8]{0,1:T(8,128)S(1)}, s32[64,8]{0,1:T(8,128)}, u32[]{:S(2)}) copy-start(s32[64,8]{0,1:T(8,128)} %param.29) | copy-start | bytes 6148
  85.7 31.6 %all-to-all-start = ((f32[8,64,4,130]{3,1,2,0:T(8,128)}), f32[8,64,4,130]{3,1,2,0:T(8,128)}, u32[]{:S(2)}, u32[]{:S(2)}) async-start(f32[8,64,4,130]{3,1,2,0:T(8,128)} %maximum_bitcast_fusion), calls=%async_computation | async-start | bytes 4194304 | tf_op jit(solution)/shard_map/all_to_all | solution.py:151
  125.3 10.8 %all-to-all-start.1 = ((bf16[64,8,256]{2,0,1:T(8,128)(2,1)}), bf16[64,8,256]{2,0,1:T(8,128)(2,1)S(1)}, u32[]{:S(2)}, u32[]{:S(2)}) async-start(bf16[64,8,256]{2,0,1:T(8,128)(2,1)} %bitcast.200), calls=%async_computation.1 | async-start | bytes 524288 | tf_op jit(solution)/shard_map/all_to_all | solution.py:163
  128.8 67.5 %all-gather.5.cloned.1.call-start = ((), (), s32[]{:S(2)}) async-start(), calls=%async_computation.11 | async-start | bytes 2359296 | tf_op jit(solution)/shard_map/all_gather | solution.py:201
  173.4 54.9 %all-gather.3.cloned.1.call-start = ((), (), s32[]{:S(2)}) async-start(), calls=%async_computation.9 | async-start | bytes 2359296 | tf_op jit(solution)/shard_map/all_gather | solution.py:201
  189.9 78.4 %reduce-scatter.5.cloned.1.call-start = ((), (), s32[]{:S(2)}) async-start(), calls=%async_computation.12 | async-start | bytes 2359296 | tf_op jit(solution)/shard_map/reduce_scatter | solution.py:215
  203.4 102.8 %reduce-scatter.3.cloned.1.call-start = ((), (), s32[]{:S(2)}) async-start(), calls=%async_computation.10 | async-start | bytes 2359296 | tf_op jit(solution)/shard_map/reduce_scatter | solution.py:215
  235.5 82.2 %copy-start.8 = (f32[64,8]{0,1:T(8,128)S(1)}, f32[64,8]{0,1:T(8,128)}, u32[]{:S(2)}) copy-start(f32[64,8]{0,1:T(8,128)} %param.30) | copy-start | bytes 6148
  270.0 37.9 %all-to-all-start.5 = ((bf16[32,2,8,256]{3,2,1,0:T(8,128)(2,1)}), bf16[32,2,8,256]{3,2,1,0:T(8,128)(2,1)S(1)}, u32[]{:S(2)}, u32[]{:S(2)}) async-start(bf16[32,2,8,256]{3,2,1,0:T(8,128)(2,1)} %copy.294), calls=%async_computation.7 | async-start | bytes 524288 | tf_op jit(solution)/shard_map/all_to_all | solution.py:217
  307.8 21.0 %all-to-all-start.3 = ((bf16[32,2,8,256]{3,2,1,0:T(8,128)(2,1)}), bf16[32,2,8,256]{3,2,1,0:T(8,128)(2,1)S(1)}, u32[]{:S(2)}, u32[]{:S(2)}) async-start(bf16[32,2,8,256]{3,2,1,0:T(8,128)(2,1)} %copy.292), calls=%async_computation.4 | async-start | bytes 524288 | tf_op jit(solution)/shard_map/all_to_all | solution.py:217
Sparse Core Ops, SparseCore 0:
  173.6 22.6 all-gather.4
  198.1 30.2 all-gather.2
  230.9 37.3 reduce-scatter.4
  270.7 35.4 reduce-scatter.2

commit v5 on v3

--- a/solution.py
+++ b/solution.py
@@ -139,19 +139,20 @@
     )
     own_low = own_weights.astype(jnp.bfloat16).astype(jnp.float32)
     sums_local = sums_local + own_low[..., None] * own_values[:, :, None, :]
+    pair_rows = requests * heads_here // head_dim
+
+    def by_owner(values):
+        values = values.reshape(requests, tensor_size, heads_here, -1).transpose(1, 0, 2, 3)
+        return values.reshape(tensor_size, -1, head_dim)
+
     packed = jnp.concatenate(
-        [
-            sums_local.reshape(requests, heads_all, head_dim),
-            top_local.reshape(requests, heads_all, 1),
-            total_local.reshape(requests, heads_all, 1),
-        ],
-        axis=2,
-    )
-    packed = packed.reshape(requests, tensor_size, heads_here, head_dim + 2).transpose(1, 0, 2, 3)
+        [by_owner(sums_local), by_owner(top_local), by_owner(total_local)], axis=1
+    )
     parts = lax.all_to_all(packed, "tensor", 0, 0, tiled=True)
-    part_sums = parts[..., :head_dim]
-    part_top = parts[..., head_dim]
-    part_total = parts[..., head_dim + 1]
+    spread = requests * heads_here
+    part_sums = parts[:, :spread].reshape(tensor_size, requests, heads_here, head_dim)
+    part_top = parts[:, spread : spread + pair_rows].reshape(tensor_size, requests, heads_here)
+    part_total = parts[:, spread + pair_rows :].reshape(tensor_size, requests, heads_here)
     top_all = jnp.max(part_top, axis=0)
     factor = jnp.exp(part_top - top_all[None])
     total_mine = jnp.sum(part_total * factor, axis=0)

time: 310 us -> 294 us (0.948)
  waiting for transfers between devices: 120 us -> 107 us
  other arithmetic: 22.2 us -> 18.4 us
    all_to_all x1, waiting for transfers between devices: 25.9 us -> 13.5 us  [body(): parts = lax.all_to_all(packed, 'tensor', 0, 0, tiled=True)]
    transpose x1 -> x0, other arithmetic: 3.25 us -> none  [body(): packed.reshape(requests, tensor_size, heads_here, head_dim + 2)]
    unnamed x41 -> x39, local copies, waits for them, and re-layouts: 8.82 us -> 7.56 us
where the time goes in v5:
time: 294 us; the launch traced here: 292 us
  waiting for transfers between devices  107 us (36%)
  blocking collectives  77.6 us (26%)
  local copies, waits for them, and re-layouts  28.7 us (10%)
  matrix products  28.4 us (10%)
  other arithmetic  18.4 us (6%)
  starting transfers between devices  17.5 us (6%)
  between operations  14.6 us (5%)
    reduce_scatter x1, waiting for transfers between devices, body(): lax.psum_scatter(partial_out, 'tensor', scatter_dimension=3, tiled=True)  41.5 us
    all_gather x1, waiting for transfers between devices, body(): lax.all_gather(arrived, 'tensor', axis=2, tiled=True)  31.8 us
    all_to_all x1, blocking collectives, body(): lax.all_to_all(outgoing, 'dp', split_axis=0, concat_axis=0, tiled=True)  28.7 us
    all_to_all x1, waiting for transfers between devices, body(): lax.all_to_all(summed_out.reshape(owners, local_experts * capacity, width...  14.7 us
    all_gather x1, blocking collectives, body(): residual_all = lax.all_gather(residual_in, 'tensor', axis=0, tiled=True)  13.5 us
    all_to_all x1, waiting for transfers between devices, body(): parts = lax.all_to_all(packed, 'tensor', 0, 0, tiled=True)  13.5 us
    all_gather x1, blocking collectives, body(): lax.all_gather(joined, 'tensor', axis=1, tiled=True)  13.5 us
    psum x1, blocking collectives, body(): lax.psum(jnp.sum(middle_wide * middle_wide, axis=1, keepdims=True), 'tens...  12.6 us
  transfers between devices with their start and end apart: 5, of which 5 were waited for; matrix products, arithmetic and copies ran while one was open for 1% of the time, Pallas kernels for 0%

profile of v5, /device:TPU:32, one launch (start us, length us, event | category | flops | bytes accessed | tf_op | source)
XLA Modules:
  0.0 292.3 jit_solution(11085644443955566900)
XLA Ops:
  7.3 13.5 %all_gather.9 = bf16[64,2048]{1,0:T(8,128)(2,1)S(1)} all-gather(bf16[8,2048]{1,0:T(8,128)(2,1)} %param.18), channel_id=1, replica_groups=mesh['dp'=32,'tensor'=8] {'tensor'}, dimensions={0}, use_global_device_ids=true | all-gather | bytes 294912 | tf_op jit(solution)/shard_map/all_gather | solution.py:65
  20.9 1.4 multiply_reduce_fusion.1
  23.2 2.1 fusion.80
  26.8 13.5 %all_gather.10 = bf16[64,5120]{1,0:T(8,128)(2,1)S(1)} all-gather(bf16[64,640]{1,0:T(8,128)(2,1)S(1)} %pad_maximum_fusion.1), channel_id=1, replica_groups=mesh['dp'=32,'tensor'=8] {'tensor'}, dimensions={1}, use_global_device_ids=true | all-gather | bytes 737280 | tf_op jit(solution)/shard_map/all_gather | solution.py:86
  42.8 2.1 fusion.104
  44.9 2.0 copy.284
  47.0 4.6 %fusion = (f32[64,4,8]{2,0,1:T(8,128)}, f32[4,64,8,2,256]{4,2,3,1,0:T(8,128)}) fusion(pred[64,2,256]{2,1,0:T(4,128)(4,1)S(1)} %broadcast_and_fusion, bf16[2,256,4,128,1]{1,3,2,0,4:T(8,128)(2,1)} %bitcast.197, bf16[64,4,8,128]{3,2,1,0:T(8,128)(2,1)S(1)} %reshape.346), kind=kOutput, calls=%fused_computation.3 | convolution fusion | flops 271579136 | bytes 5283840 | tf_op jit(solution)/shard_map/rgqd,npgd->rgqnp/dot_general | solution.py:102
  51.6 1.6 copy.232
  53.3 2.9 %slice_bitcast_fusion = (bf16[64,2,4,8,128]{4,3,2,1,0:T(8,128)(2,1)}, bf16[64,2,4,8,128]{4,3,2,1,0:T(8,128)(2,1)S(1)}) fusion(bf16[64,16,1024]{2,1,0:T(8,128)(2,1)} %param.32), kind=kLoop, calls=%fused_computation.40 | loop fusion | bytes 4194304
  56.3 2.4 select_reduce_fusion
  59.6 1.4 convert_convert_fusion
  62.8 4.4 %fusion.7 = f32[64,4,8]{2,0,1:T(8,128)} fusion(f32[4,64,8,2,256]{4,2,3,1,0:T(8,128)} %get-tuple-element.29, f32[64,4,8]{2,0,1:T(8,128)S(1)} %copy.234, pred[64,2,256]{2,1,0:T(4,128)(4,1)S(1)} %broadcast_and_fusion), kind=kLoop, calls=%fused_computation.11 | loop fusion | flops 4192256 | bytes 4243456 | tf_op jit(solution)/shard_map/reduce_sum | solution.py:127
  67.3 3.2 %fusion.19 = f32[64,4,8,128]{3,2,0,1:T(8,128)} fusion(f32[4,64,8,2,256]{4,2,3,1,0:T(8,128)S(1)} %copy-done.1, f32[64,4,8]{2,0,1:T(8,128)} %copy-done.4, pred[64,2,256]{2,1,0:T(4,128)(4,1)S(1)} %broadcast_and_fusion, bf16[2,256,4,128,1]{1,3,2,0,4:T(8,128)(2,1)} %bitcast.202), kind=kOutput, calls=%fused_computation.24 | convolution fusion | flops 272629760 | bytes 5808128 | tf_op jit(solution)/shard_map/rgqnp,npgd->rgqd/dot_general | solution.py:128
  70.5 1.5 copy.240
  72.0 1.6 fusion.53
  73.6 2.0 fusion.22
  78.1 1.4 add_add_fusion
  83.1 3.7 %all-to-all-start = ((f32[8,260,128]{2,1,0:T(8,128)}), f32[8,260,128]{2,1,0:T(8,128)S(1)}, u32[]{:S(2)}, u32[]{:S(2)}) async-start(f32[8,260,128]{2,1,0:T(8,128)} %copy.250), calls=%async_computation | async-start | bytes 2162688 | tf_op jit(solution)/shard_map/all_to_all | solution.py:151
  89.5 13.5 %all-to-all-done = f32[8,260,128]{2,1,0:T(8,128)S(1)} async-done(((f32[8,260,128]{2,1,0:T(8,128)}), f32[8,260,128]{2,1,0:T(8,128)S(1)}, u32[]{:S(2)}, u32[]{:S(2)}) %all-to-all-start) | async-done | bytes 1064992 | tf_op jit(solution)/shard_map/all_to_all | solution.py:151
  106.5 3.4 %all-to-all-start.1 = ((bf16[64,8,256]{2,0,1:T(8,128)(2,1)}), bf16[64,8,256]{2,0,1:T(8,128)(2,1)S(1)}, u32[]{:S(2)}, u32[]{:S(2)}) async-start(bf16[64,8,256]{2,0,1:T(8,128)(2,1)} %bitcast.187), calls=%async_computation.1 | async-start | bytes 524288 | tf_op jit(solution)/shard_map/all_to_all | solution.py:164
  111.7 5.6 %all-to-all-done.1 = bf16[64,8,256]{2,0,1:T(8,128)(2,1)S(1)} async-done(((bf16[64,8,256]{2,0,1:T(8,128)(2,1)}), bf16[64,8,256]{2,0,1:T(8,128)(2,1)S(1)}, u32[]{:S(2)}, u32[]{:S(2)}) %all-to-all-start.1) | async-done | bytes 262176 | tf_op jit(solution)/shard_map/all_to_all | solution.py:164
  117.5 12.6 %psum.7 = f32[64,1]{0,1:T(1,128)S(1)} all-reduce(f32[64,1]{0,1:T(1,128)S(1)} %bitcast.213), channel_id=1, replica_groups=mesh['dp'=32,'tensor'=8] {'tensor'}, use_global_device_ids=true, to_apply=%region_18.19 | all-reduce | flops 64 | bytes 512 | tf_op jit(solution)/shard_map/psum | solution.py:175
  130.5 28.7 %all_to_all.47 = bf16[32,32,256]{2,1,0:T(8,128)(2,1)} all-to-all(bf16[32,32,256]{2,1,0:T(8,128)(2,1)S(1)} %bitcast.196), channel_id=1, replica_groups=mesh['dp'=32,'tensor'=8] {'dp'}, dimensions={0} | all-to-all | bytes 1048576 | tf_op jit(solution)/shard_map/all_to_all | solution.py:194
  159.3 31.8 %all-gather.2.cloned.1.call-done = bf16[32,32,2048]{2,1,0:T(8,128)(2,1)} async-done(((bf16[32,32,256]{2,1,0:T(8,128)(2,1)}), bf16[32,32,2048]{2,1,0:T(8,128)(2,1)}) %all-gather.2.cloned.1.call-update) | async-done | bytes 4194320 | tf_op jit(solution)/shard_map/all_gather | solution.py:195
  191.1 3.9 %fusion.23 = f32[32,4,8,96]{3,2,0,1:T(8,128)S(1)} fusion(bf16[4,2048,96]{1,2,0:T(8,128)(2,1)} %param.26, bf16[32,32,2048]{2,1,0:T(8,128)(2,1)} %all-gather.2.cloned.1.call-done), kind=kOutput, calls=%fused_computation.29 | convolution fusion | flops 402653184 | bytes 6160384 | tf_op jit(solution)/shard_map/necd,edf->necf/dot_general | solution.py:198
  195.0 7.4 %convert_bitcast_fusion = bf16[32,4,8,2048]{3,2,0,1:T(8,128)(2,1)} fusion(bf16[4,96,2048]{2,1,0:T(8,128)(2,1)} %param.28, bf16[4,2048,96]{1,2,0:T(8,128)(2,1)} %param.27, f32[32,4,8,96]{3,2,0,1:T(8,128)S(1)} %fusion.23, bf16[32,32,2048]{2,1,0:T(8,128)(2,1)} %all-gather.2.cloned.1.call-done), kind=kOutput, calls=%fused_computation.6 | convolution fusion | flops 807993344 | bytes 11927552 | tf_op jit(solution)/shard_map/necf,efd->necd/dot_general | solution.py:201
  202.4 41.5 %reduce-scatter.2.cloned.1.call-done = bf16[32,4,8,256]{3,2,0,1:T(8,128)(2,1)} async-done(((bf16[32,4,8,2048]{3,2,0,1:T(8,128)(2,1)}), bf16[32,4,8,256]{3,2,0,1:T(8,128)(2,1)}) %reduce-scatter.2.cloned.1.call-update) | async-done | bytes 524304 | tf_op jit(solution)/shard_map/reduce_scatter | solution.py:204
  244.0 1.9 copy.350
  245.9 10.1 %all-to-all-start.3 = ((bf16[32,32,256]{2,1,0:T(8,128)(2,1)}), bf16[32,32,256]{2,1,0:T(8,128)(2,1)}, u32[]{:S(2)}, u32[]{:S(2)}) async-start(bf16[32,32,256]{2,1,0:T(8,128)(2,1)} %bitcast.186), calls=%async_computation.4 | async-start | bytes 1048576 | tf_op jit(solution)/shard_map/all_to_all | solution.py:205
  256.4 14.7 %all-to-all-done.3 = bf16[32,32,256]{2,1,0:T(8,128)(2,1)} async-done(((bf16[32,32,256]{2,1,0:T(8,128)(2,1)}), bf16[32,32,256]{2,1,0:T(8,128)(2,1)}, u32[]{:S(2)}, u32[]{:S(2)}) %all-to-all-start.3) | async-done | bytes 524320 | tf_op jit(solution)/shard_map/all_to_all | solution.py:205
  272.1 2.2 gather_fusion
  275.6 9.2 %all_to_all.48 = bf16[8,8,256]{2,1,0:T(8,128)(2,1)S(1)} all-to-all(bf16[8,8,256]{2,1,0:T(8,128)(2,1)S(1)} %fusion.87), channel_id=1, replica_groups=mesh['dp'=32,'tensor'=8] {'tensor'}, dimensions={0} | all-to-all | bytes 65536 | tf_op jit(solution)/shard_map/all_to_all | solution.py:216
  (127 shorter events, 25.7 us)
Async XLA Ops:
  7.2 98.1 %copy-start = (bf16[512,2048]{1,0:T(8,128)(2,1)S(1)}, bf16[512,2048]{1,0:T(8,128)(2,1)}, u32[]{:S(2)}) copy-start(bf16[512,2048]{1,0:T(8,128)(2,1)} %param.24) | copy-start | bytes 6291460
  7.2 19.0 %copy-start.9 = (f32[128]{0:T(128)S(1)}, f32[128]{0:T(128)}, u32[]{:S(2)}) copy-start(f32[128]{0:T(128)} %param.23) | copy-start | bytes 1540
  7.2 18.4 %copy-start.10 = (f32[128]{0:T(128)S(1)}, f32[128]{0:T(128)}, u32[]{:S(2)}) copy-start(f32[128]{0:T(128)} %param.22) | copy-start | bytes 1540
  7.2 18.7 %copy-start.12 = (s32[2]{0:T(128)S(1)}, s32[2]{0:T(128)}, u32[]{:S(2)}) copy-start(s32[2]{0:T(128)} %param.33) | copy-start | bytes 28
  7.2 18.7 %copy-start.11 = (s32[64]{0:T(128)S(1)}, s32[64]{0:T(128)}, u32[]{:S(2)}) copy-start(s32[64]{0:T(128)} %param.35) | copy-start | bytes 772
  7.2 18.9 %copy-start.14 = (s32[64]{0:T(128)S(1)}, s32[64]{0:T(128)}, u32[]{:S(2)}) copy-start(s32[64]{0:T(128)} %param.34) | copy-start | bytes 772
  23.2 17.2 %copy-start.13 = (s32[2]{0:T(128)}, s32[2]{0:T(128)S(1)}, u32[]{:S(2)}) copy-start(s32[2]{0:T(128)S(1)} %iota_add_fusion.2) | copy-start | bytes 28
  26.4 13.9 %copy-start.6 = (bf16[64,128]{1,0:T(8,128)(2,1)}, bf16[64,128]{1,0:T(8,128)(2,1)S(1)}, u32[]{:S(2)}) copy-start(bf16[64,128]{1,0:T(8,128)(2,1)S(1)} %get-tuple-element.35) | copy-start | bytes 49156
  42.8 10.5 %copy-start.15 = (s32[64]{0:T(128)S(1)}, s32[64]{0:T(128)}, u32[]{:S(2)}) copy-start(s32[64]{0:T(128)} %param.34) | copy-start | bytes 772
  53.3 5.3 %copy-start.5 = (pred[64,16]{1,0:T(8,128)(4,1)}, pred[64,16]{1,0:T(8,128)(4,1)S(1)}, u32[]{:S(2)}) copy-start(pred[64,16]{1,0:T(8,128)(4,1)S(1)} %broadcast_compare_fusion) | copy-start | bytes 3076
  61.1 1.8 copy-start.4
  62.8 4.4 %copy-start.1 = (f32[4,64,8,2,256]{4,2,3,1,0:T(8,128)S(1)}, f32[4,64,8,2,256]{4,2,3,1,0:T(8,128)}, u32[]{:S(2)}) copy-start(f32[4,64,8,2,256]{4,2,3,1,0:T(8,128)} %get-tuple-element.29) | copy-start | bytes 12582916
  67.3 4.7 %copy-start.2 = (f32[64,4,8,16]{3,2,1,0:T(8,128)S(1)}, f32[64,4,8,16]{3,2,1,0:T(8,128)}, u32[]{:S(2)}) copy-start(f32[64,4,8,16]{3,2,1,0:T(8,128)} %get-tuple-element.31) | copy-start | bytes 393220
  81.1 5.7 %copy-start.8 = (s32[64,8]{0,1:T(8,128)S(1)}, s32[64,8]{0,1:T(8,128)}, u32[]{:S(2)}) copy-start(s32[64,8]{0,1:T(8,128)} %param.29) | copy-start | bytes 6148
  83.1 19.9 %all-to-all-start = ((f32[8,260,128]{2,1,0:T(8,128)}), f32[8,260,128]{2,1,0:T(8,128)S(1)}, u32[]{:S(2)}, u32[]{:S(2)}) async-start(f32[8,260,128]{2,1,0:T(8,128)} %copy.250), calls=%async_computation | async-start | bytes 2162688 | tf_op jit(solution)/shard_map/all_to_all | solution.py:151
  87.4 0.7 copy-start.3
  106.5 10.8 %all-to-all-start.1 = ((bf16[64,8,256]{2,0,1:T(8,128)(2,1)}), bf16[64,8,256]{2,0,1:T(8,128)(2,1)S(1)}, u32[]{:S(2)}, u32[]{:S(2)}) async-start(bf16[64,8,256]{2,0,1:T(8,128)(2,1)} %bitcast.187), calls=%async_computation.1 | async-start | bytes 524288 | tf_op jit(solution)/shard_map/all_to_all | solution.py:164
  109.9 81.2 %all-gather.2.cloned.1.call-start = ((), (), s32[]{:S(2)}) async-start(), calls=%async_computation.6 | async-start | bytes 4718592 | tf_op jit(solution)/shard_map/all_gather | solution.py:195
  159.2 84.7 %reduce-scatter.2.cloned.1.call-start = ((), (), s32[]{:S(2)}) async-start(), calls=%async_computation.7 | async-start | bytes 4718592 | tf_op jit(solution)/shard_map/reduce_scatter | solution.py:204
  202.4 53.8 %copy-start.7 = (f32[64,8]{0,1:T(8,128)S(1)}, f32[64,8]{0,1:T(8,128)}, u32[]{:S(2)}) copy-start(f32[64,8]{0,1:T(8,128)} %param.30) | copy-start | bytes 6148
  245.9 25.1 %all-to-all-start.3 = ((bf16[32,32,256]{2,1,0:T(8,128)(2,1)}), bf16[32,32,256]{2,1,0:T(8,128)(2,1)}, u32[]{:S(2)}, u32[]{:S(2)}) async-start(bf16[32,32,256]{2,1,0:T(8,128)(2,1)} %bitcast.186), calls=%async_computation.4 | async-start | bytes 1048576 | tf_op jit(solution)/shard_map/all_to_all | solution.py:205
Sparse Core Ops, SparseCore 0:
  159.4 31.6 all-gather.1
  202.6 41.3 reduce-scatter.1

commit v6 on v5

--- a/solution.py
+++ b/solution.py
@@ -198,10 +198,11 @@
     gate_val = jnp.einsum("necd,edf->necf", rows, gate_weight, preferred_element_type=jnp.float32)
     lift_val = jnp.einsum("necd,edf->necf", rows, lift_weight, preferred_element_type=jnp.float32)
     hidden_units = (jax.nn.silu(gate_val) * lift_val).astype(jnp.bfloat16)
-    partial_out = jnp.einsum(
-        "necf,efd->necd", hidden_units, down_weight, preferred_element_type=jnp.float32
+    hidden_all = lax.all_gather(hidden_units, "tensor", axis=3, tiled=True)
+    down_cols = lax.all_to_all(down_weight, "tensor", split_axis=2, concat_axis=1, tiled=True)
+    summed_out = jnp.einsum(
+        "necf,efd->necd", hidden_all, down_cols, preferred_element_type=jnp.float32
     ).astype(jnp.bfloat16)
-    summed_out = lax.psum_scatter(partial_out, "tensor", scatter_dimension=3, tiled=True)
     returned = lax.all_to_all(
         summed_out.reshape(owners, local_experts * capacity, width_here),
         "dp",

time: 294 us -> 321 us (1.092)
  blocking collectives: 77.6 us -> 126 us
  waiting for transfers between devices: 107 us -> 72.7 us
  local copies, waits for them, and re-layouts: 28.7 us -> 48.3 us
  matrix products: 28.4 us -> 24.5 us
    all_to_all x0 -> x1, blocking collectives: none -> 49.9 us  [body(): lax.all_to_all(down_weight, 'tensor', split_axis=2, concat_axis=1, tiled=...]
    reduce_scatter x1 -> x0, waiting for transfers between devices: 41.5 us -> none  [body(): lax.psum_scatter(partial_out, 'tensor', scatter_dimension=3, tiled=True)]
    all_gather x0 -> x1, local copies, waits for them, and re-layouts: none -> 9.09 us  [body(): hidden_all = lax.all_gather(hidden_units, 'tensor', axis=3, tiled=True)]
    unnamed x39 -> x42, local copies, waits for them, and re-layouts: 7.56 us -> 12.1 us
    all_to_all x0 -> x1, local copies, waits for them, and re-layouts: none -> 4.19 us  [body(): lax.all_to_all(down_weight, 'tensor', split_axis=2, concat_axis=1, tiled=...]
    all_gather x0 -> x1, waiting for transfers between devices: none -> 4 us  [body(): hidden_all = lax.all_gather(hidden_units, 'tensor', axis=3, tiled=True)]
    dot_general x1 -> x2, matrix products: 7.41 us -> 3.72 us  [the longest x1 2.47 us: body(): jnp.einsum('necf,efd->necd', hidden_all, down_cols, preferred_element_typ...]
  transfers between devices with their start and end apart: 5 -> 5, of which waited for: 5 -> 5; matrix products, arithmetic and copies ran while one was open for 1% -> 4% of each run, Pallas kernels for 0% -> 0%
where the time goes in v6:
time: 321 us; the launch traced here: 320 us
  blocking collectives  126 us (39%)
  waiting for transfers between devices  72.7 us (23%)
  local copies, waits for them, and re-layouts  48.3 us (15%)
  matrix products  24.5 us (8%)
  starting transfers between devices  17.5 us (5%)
  other arithmetic  16 us (5%)
  between operations  14.6 us (5%)
    all_to_all x1, blocking collectives, body(): lax.all_to_all(down_weight, 'tensor', split_axis=2, concat_axis=1, tiled=...  49.9 us
    all_gather x1, waiting for transfers between devices, body(): lax.all_gather(arrived, 'tensor', axis=2, tiled=True)  31.8 us
    all_to_all x1, blocking collectives, body(): lax.all_to_all(outgoing, 'dp', split_axis=0, concat_axis=0, tiled=True)  28.7 us
    all_to_all x1, waiting for transfers between devices, body(): lax.all_to_all(summed_out.reshape(owners, local_experts * capacity, width...  17.8 us
    all_gather x1, blocking collectives, body(): residual_all = lax.all_gather(residual_in, 'tensor', axis=0, tiled=True)  13.5 us
    all_to_all x1, waiting for transfers between devices, body(): parts = lax.all_to_all(packed, 'tensor', 0, 0, tiled=True)  13.5 us
    all_gather x1, blocking collectives, body(): lax.all_gather(joined, 'tensor', axis=1, tiled=True)  13.5 us
    psum x1, blocking collectives, body(): lax.psum(jnp.sum(middle_wide * middle_wide, axis=1, keepdims=True), 'tens...  12.6 us
  transfers between devices with their start and end apart: 5, of which 5 were waited for; matrix products, arithmetic and copies ran while one was open for 4% of the time, Pallas kernels for 0%

profile of v6, /device:TPU:32, one launch (start us, length us, event | category | flops | bytes accessed | tf_op | source)
XLA Modules:
  0.0 319.8 jit_solution(17496205011000543287)
XLA Ops:
  7.2 13.5 %all_gather.12 = bf16[64,2048]{1,0:T(8,128)(2,1)S(1)} all-gather(bf16[8,2048]{1,0:T(8,128)(2,1)} %param.18), channel_id=1, replica_groups=mesh['dp'=32,'tensor'=8] {'tensor'}, dimensions={0}, use_global_device_ids=true | all-gather | bytes 294912 | tf_op jit(solution)/shard_map/all_gather | solution.py:65
  20.9 1.4 multiply_reduce_fusion.1
  23.3 2.1 fusion.70
  26.8 13.5 %all_gather.13 = bf16[64,5120]{1,0:T(8,128)(2,1)S(1)} all-gather(bf16[64,640]{1,0:T(8,128)(2,1)S(1)} %pad_maximum_fusion.1), channel_id=1, replica_groups=mesh['dp'=32,'tensor'=8] {'tensor'}, dimensions={1}, use_global_device_ids=true | all-gather | bytes 737280 | tf_op jit(solution)/shard_map/all_gather | solution.py:86
  42.1 2.1 fusion.93
  44.2 2.0 copy.307
  46.4 4.6 %fusion = (f32[64,4,8]{2,0,1:T(8,128)}, f32[4,64,8,2,256]{4,2,3,1,0:T(8,128)}) fusion(pred[64,2,256]{2,1,0:T(4,128)(4,1)S(1)} %broadcast_and_fusion, bf16[2,256,4,128,1]{1,3,2,0,4:T(8,128)(2,1)} %bitcast.199, bf16[64,4,8,128]{3,2,1,0:T(8,128)(2,1)S(1)} %reshape.346), kind=kOutput, calls=%fused_computation.3 | convolution fusion | flops 271579136 | bytes 5283840 | tf_op jit(solution)/shard_map/rgqd,npgd->rgqnp/dot_general | solution.py:102
  52.1 2.9 slice_bitcast_fusion
  55.0 2.4 select_reduce_fusion
  60.3 4.4 %fusion.7 = f32[64,4,8]{2,0,1:T(8,128)} fusion(f32[4,64,8,2,256]{4,2,3,1,0:T(8,128)} %get-tuple-element.29, f32[64,4,8]{2,0,1:T(8,128)S(1)} %copy.253, pred[64,2,256]{2,1,0:T(4,128)(4,1)S(1)} %broadcast_and_fusion), kind=kLoop, calls=%fused_computation.10 | loop fusion | flops 4192256 | bytes 4243456 | tf_op jit(solution)/shard_map/reduce_sum | solution.py:127
  64.7 3.2 %fusion.18 = f32[64,4,8,128]{3,2,0,1:T(8,128)} fusion(f32[4,64,8,2,256]{4,2,3,1,0:T(8,128)S(1)} %copy-done.1, f32[64,4,8]{2,0,1:T(8,128)} %copy-done.6, pred[64,2,256]{2,1,0:T(4,128)(4,1)S(1)} %broadcast_and_fusion, bf16[2,256,4,128,1]{1,3,2,0,4:T(8,128)(2,1)} %bitcast.204), kind=kOutput, calls=%fused_computation.22 | convolution fusion | flops 272629760 | bytes 5808128 | tf_op jit(solution)/shard_map/rgqnp,npgd->rgqd/dot_general | solution.py:128
  69.6 2.2 fusion.49
  71.9 1.7 fusion.21
  81.1 3.7 %all-to-all-start = ((f32[8,260,128]{2,1,0:T(8,128)}), f32[8,260,128]{2,1,0:T(8,128)S(1)}, u32[]{:S(2)}, u32[]{:S(2)}) async-start(f32[8,260,128]{2,1,0:T(8,128)} %copy.269), calls=%async_computation | async-start | bytes 2162688 | tf_op jit(solution)/shard_map/all_to_all | solution.py:151
  87.5 13.5 %all-to-all-done = f32[8,260,128]{2,1,0:T(8,128)S(1)} async-done(((f32[8,260,128]{2,1,0:T(8,128)}), f32[8,260,128]{2,1,0:T(8,128)S(1)}, u32[]{:S(2)}, u32[]{:S(2)}) %all-to-all-start) | async-done | bytes 1064992 | tf_op jit(solution)/shard_map/all_to_all | solution.py:151
  104.5 3.4 %all-to-all-start.1 = ((bf16[64,8,256]{2,0,1:T(8,128)(2,1)}), bf16[64,8,256]{2,0,1:T(8,128)(2,1)S(1)}, u32[]{:S(2)}, u32[]{:S(2)}) async-start(bf16[64,8,256]{2,0,1:T(8,128)(2,1)} %bitcast.187), calls=%async_computation.1 | async-start | bytes 524288 | tf_op jit(solution)/shard_map/all_to_all | solution.py:164
  109.7 5.6 %all-to-all-done.1 = bf16[64,8,256]{2,0,1:T(8,128)(2,1)S(1)} async-done(((bf16[64,8,256]{2,0,1:T(8,128)(2,1)}), bf16[64,8,256]{2,0,1:T(8,128)(2,1)S(1)}, u32[]{:S(2)}, u32[]{:S(2)}) %all-to-all-start.1) | async-done | bytes 262176 | tf_op jit(solution)/shard_map/all_to_all | solution.py:164
  115.5 12.6 %psum.7 = f32[64,1]{0,1:T(1,128)S(1)} all-reduce(f32[64,1]{0,1:T(1,128)S(1)} %bitcast.215), channel_id=1, replica_groups=mesh['dp'=32,'tensor'=8] {'tensor'}, use_global_device_ids=true, to_apply=%region_18.19 | all-reduce | flops 64 | bytes 512 | tf_op jit(solution)/shard_map/psum | solution.py:175
  128.5 28.7 %all_to_all.65 = bf16[32,32,256]{2,1,0:T(8,128)(2,1)} all-to-all(bf16[32,32,256]{2,1,0:T(8,128)(2,1)S(1)} %bitcast.198), channel_id=1, replica_groups=mesh['dp'=32,'tensor'=8] {'dp'}, dimensions={0} | all-to-all | bytes 1048576 | tf_op jit(solution)/shard_map/all_to_all | solution.py:194
  157.3 31.8 %all-gather.3.cloned.1.call-done = bf16[32,32,2048]{2,1,0:T(8,128)(2,1)} async-done(((bf16[32,32,256]{2,1,0:T(8,128)(2,1)}), bf16[32,32,2048]{2,1,0:T(8,128)(2,1)}) %all-gather.3.cloned.1.call-update) | async-done | bytes 4194320 | tf_op jit(solution)/shard_map/all_gather | solution.py:195
  189.1 4.1 %fusion.22 = f32[32,4,8,96]{3,2,0,1:T(8,128)S(1)} fusion(bf16[4,2048,96]{1,2,0:T(8,128)(2,1)} %param.26, bf16[32,32,2048]{2,1,0:T(8,128)(2,1)} %all-gather.3.cloned.1.call-done), kind=kOutput, calls=%fused_computation.28 | convolution fusion | flops 402653184 | bytes 6160384 | tf_op jit(solution)/shard_map/necd,edf->necf/dot_general | solution.py:198
  194.7 2.1 copy.282
  196.9 4.2 %copy.283 = bf16[4,96,2048]{1,0,2:T(4,128)(2,1)} copy(bf16[4,96,2048]{2,1,0:T(8,128)(2,1)} %param.28) | data formatting | bytes 3145728 | tf_op args[10]
  201.1 49.9 %all_to_all.66 = bf16[4,96,2048]{1,0,2:T(4,128)(2,1)} all-to-all(bf16[4,96,2048]{1,0,2:T(4,128)(2,1)} %copy.283), channel_id=1, replica_groups=mesh['dp'=32,'tensor'=8] {'tensor'}, dimensions={2} | all-to-all | bytes 3145728 | tf_op jit(solution)/shard_map/all_to_all | solution.py:202
  251.0 4.2 %copy.284 = bf16[4,96,8,256]{3,1,2,0:T(8,128)(2,1)} copy(bf16[4,96,8,256]{1,0,3,2:T(4,128)(2,1)} %bitcast.191) | data formatting | bytes 3145728 | tf_op jit(solution)/shard_map/all_to_all | solution.py:202
  255.2 4.0 %all-gather.5.cloned.1.call-done = bf16[32,4,8,768]{0,2,1,3:T(8,128)(2,1)} async-done(((bf16[32,4,8,96]{0,2,1,3:T(8,128)(2,1)}), bf16[32,4,8,768]{0,2,1,3:T(8,128)(2,1)}) %all-gather.5.cloned.1.call-update) | async-done | bytes 1572880 | tf_op jit(solution)/shard_map/all_gather | solution.py:201
  259.2 9.1 %copy.285 = bf16[32,4,8,768]{3,2,0,1:T(8,128)(2,1)} copy(bf16[32,4,8,768]{0,2,1,3:T(8,128)(2,1)} %all-gather.5.cloned.1.call-done) | data formatting | bytes 3145728 | tf_op jit(solution)/shard_map/all_gather | solution.py:201
  268.3 2.5 fusion.32
  271.6 10.1 %all-to-all-start.4 = ((bf16[32,32,256]{2,1,0:T(8,128)(2,1)}), bf16[32,32,256]{2,1,0:T(8,128)(2,1)}, u32[]{:S(2)}, u32[]{:S(2)}) async-start(bf16[32,32,256]{2,1,0:T(8,128)(2,1)} %bitcast.186), calls=%async_computation.4 | async-start | bytes 1048576 | tf_op jit(solution)/shard_map/all_to_all | solution.py:206
  282.1 17.8 %all-to-all-done.4 = bf16[32,32,256]{2,1,0:T(8,128)(2,1)} async-done(((bf16[32,32,256]{2,1,0:T(8,128)(2,1)}), bf16[32,32,256]{2,1,0:T(8,128)(2,1)}, u32[]{:S(2)}, u32[]{:S(2)}) %all-to-all-start.4) | async-done | bytes 524320 | tf_op jit(solution)/shard_map/all_to_all | solution.py:206
  301.0 2.2 gather_fusion
  304.5 7.9 %all_to_all.67 = bf16[8,8,256]{2,1,0:T(8,128)(2,1)S(1)} all-to-all(bf16[8,8,256]{2,1,0:T(8,128)(2,1)S(1)} %fusion.77), channel_id=1, replica_groups=mesh['dp'=32,'tensor'=8] {'tensor'}, dimensions={0} | all-to-all | bytes 65536 | tf_op jit(solution)/shard_map/all_to_all | solution.py:217
  (135 shorter events, 31.6 us)
Async XLA Ops:
  7.2 96.1 %copy-start = (bf16[512,2048]{1,0:T(8,128)(2,1)S(1)}, bf16[512,2048]{1,0:T(8,128)(2,1)}, u32[]{:S(2)}) copy-start(bf16[512,2048]{1,0:T(8,128)(2,1)} %param.24) | copy-start | bytes 6291460
  20.7 4.9 %copy-start.11 = (f32[128]{0:T(128)S(1)}, f32[128]{0:T(128)}, u32[]{:S(2)}) copy-start(f32[128]{0:T(128)} %param.22) | copy-start | bytes 1540
  22.3 3.6 %copy-start.12 = (s32[64]{0:T(128)S(1)}, s32[64]{0:T(128)}, u32[]{:S(2)}) copy-start(s32[64]{0:T(128)} %param.35) | copy-start | bytes 772
  22.4 3.6 %copy-start.13 = (s32[2]{0:T(128)S(1)}, s32[2]{0:T(128)}, u32[]{:S(2)}) copy-start(s32[2]{0:T(128)} %param.33) | copy-start | bytes 28
  22.4 3.8 %copy-start.14 = (s32[64]{0:T(128)S(1)}, s32[64]{0:T(128)}, u32[]{:S(2)}) copy-start(s32[64]{0:T(128)} %param.34) | copy-start | bytes 772
  22.4 3.8 %copy-start.10 = (f32[128]{0:T(128)S(1)}, f32[128]{0:T(128)}, u32[]{:S(2)}) copy-start(f32[128]{0:T(128)} %param.23) | copy-start | bytes 1540
  26.4 14.0 %copy-start.7 = (bf16[64,128]{1,0:T(8,128)(2,1)}, bf16[64,128]{1,0:T(8,128)(2,1)S(1)}, u32[]{:S(2)}) copy-start(bf16[64,128]{1,0:T(8,128)(2,1)S(1)} %get-tuple-element.35) | copy-start | bytes 49156
  58.5 6.2 %copy-start.6 = (f32[64,4,8]{2,0,1:T(8,128)}, f32[64,4,8]{2,0,1:T(8,128)S(1)}, u32[]{:S(2)}) copy-start(f32[64,4,8]{2,0,1:T(8,128)S(1)} %copy.253) | copy-start | bytes 24580
  60.2 4.4 %copy-start.1 = (f32[4,64,8,2,256]{4,2,3,1,0:T(8,128)S(1)}, f32[4,64,8,2,256]{4,2,3,1,0:T(8,128)}, u32[]{:S(2)}) copy-start(f32[4,64,8,2,256]{4,2,3,1,0:T(8,128)} %get-tuple-element.29) | copy-start | bytes 12582916
  64.7 4.9 %copy-start.2 = (f32[64,4,8,16]{3,2,1,0:T(8,128)S(1)}, f32[64,4,8,16]{3,2,1,0:T(8,128)}, u32[]{:S(2)}) copy-start(f32[64,4,8,16]{3,2,1,0:T(8,128)} %get-tuple-element.31) | copy-start | bytes 393220
  68.7 3.2 %copy-start.3 = (bf16[64,2,4,8,128]{4,3,2,1,0:T(8,128)(2,1)S(1)}, bf16[64,2,4,8,128]{4,3,2,1,0:T(8,128)(2,1)}, u32[]{:S(2)}) copy-start(bf16[64,2,4,8,128]{4,3,2,1,0:T(8,128)(2,1)} %get-tuple-element.8) | copy-start | bytes 3145732
  68.7 3.2 %copy-start.5 = (f32[64,4,8]{2,0,1:T(8,128)S(1)}, f32[64,4,8]{2,0,1:T(8,128)}, u32[]{:S(2)}) copy-start(f32[64,4,8]{2,0,1:T(8,128)} %copy.259) | copy-start | bytes 24580
  79.9 4.9 %copy-start.9 = (s32[64,8]{0,1:T(8,128)S(1)}, s32[64,8]{0,1:T(8,128)}, u32[]{:S(2)}) copy-start(s32[64,8]{0,1:T(8,128)} %param.29) | copy-start | bytes 6148
  81.1 19.9 %all-to-all-start = ((f32[8,260,128]{2,1,0:T(8,128)}), f32[8,260,128]{2,1,0:T(8,128)S(1)}, u32[]{:S(2)}, u32[]{:S(2)}) async-start(f32[8,260,128]{2,1,0:T(8,128)} %copy.269), calls=%async_computation | async-start | bytes 2162688 | tf_op jit(solution)/shard_map/all_to_all | solution.py:151
  85.4 0.7 copy-start.4
  104.5 10.8 %all-to-all-start.1 = ((bf16[64,8,256]{2,0,1:T(8,128)(2,1)}), bf16[64,8,256]{2,0,1:T(8,128)(2,1)S(1)}, u32[]{:S(2)}, u32[]{:S(2)}) async-start(bf16[64,8,256]{2,0,1:T(8,128)(2,1)} %bitcast.187), calls=%async_computation.1 | async-start | bytes 524288 | tf_op jit(solution)/shard_map/all_to_all | solution.py:164
  107.9 81.2 %all-gather.3.cloned.1.call-start = ((), (), s32[]{:S(2)}) async-start(), calls=%async_computation.6 | async-start | bytes 4718592 | tf_op jit(solution)/shard_map/all_gather | solution.py:195
  157.2 101.9 %all-gather.5.cloned.1.call-start = ((), (), s32[]{:S(2)}) async-start(), calls=%async_computation.7 | async-start | bytes 7077888 | tf_op jit(solution)/shard_map/all_gather | solution.py:201
  189.1 4.1 %copy-start.15 = (bf16[32,32,2048]{2,1,0:T(8,128)(2,1)S(1)}, bf16[32,32,2048]{2,1,0:T(8,128)(2,1)}, u32[]{:S(2)}) copy-start(bf16[32,32,2048]{2,1,0:T(8,128)(2,1)} %all-gather.3.cloned.1.call-done) | copy-start | bytes 12582916
  189.1 4.4 %copy-start.16 = (bf16[4,2048,96]{1,2,0:T(8,128)(2,1)S(1)}, bf16[4,2048,96]{1,2,0:T(8,128)(2,1)}, u32[]{:S(2)}) copy-start(bf16[4,2048,96]{1,2,0:T(8,128)(2,1)} %param.27) | copy-start | bytes 4718596
  268.3 13.7 %copy-start.8 = (f32[64,8]{0,1:T(8,128)S(1)}, f32[64,8]{0,1:T(8,128)}, u32[]{:S(2)}) copy-start(f32[64,8]{0,1:T(8,128)} %param.30) | copy-start | bytes 6148
  271.6 28.2 %all-to-all-start.4 = ((bf16[32,32,256]{2,1,0:T(8,128)(2,1)}), bf16[32,32,256]{2,1,0:T(8,128)(2,1)}, u32[]{:S(2)}, u32[]{:S(2)}) async-start(bf16[32,32,256]{2,1,0:T(8,128)(2,1)} %bitcast.186), calls=%async_computation.4 | async-start | bytes 1048576 | tf_op jit(solution)/shard_map/all_to_all | solution.py:206
Sparse Core Ops, SparseCore 0:
  157.4 31.6 all-gather.2
  197.0 62.1 all-gather.4

commit v7 on v5

--- a/solution.py
+++ b/solution.py
@@ -120,7 +120,9 @@
     top_pre = jnp.max(jnp.where(pre_valid, pre_scores, NEGATIVE), axis=(3, 4))
     top_suf = jnp.max(jnp.where(suf_valid, suf_scores, NEGATIVE), axis=3)
     top_own = jnp.where(own_valid, own_scores, NEGATIVE)
-    top_local = jnp.maximum(jnp.maximum(top_pre, top_suf), top_own)
+    top_local = (
+        jnp.maximum(jnp.maximum(top_pre, top_suf), top_own).astype(jnp.bfloat16).astype(jnp.float32)
+    )
     pre_weights = jnp.where(pre_valid, jnp.exp(pre_scores - top_local[..., None, None]), 0.0)
     suf_weights = jnp.where(suf_valid, jnp.exp(suf_scores - top_local[..., None]), 0.0)
     own_weights = jnp.where(own_valid, jnp.exp(own_scores - top_local), 0.0)
@@ -145,14 +147,25 @@
         values = values.reshape(requests, tensor_size, heads_here, -1).transpose(1, 0, 2, 3)
         return values.reshape(tensor_size, -1, head_dim)
 
+    total_high = total_local.astype(jnp.bfloat16)
+    total_low = (total_local - total_high.astype(jnp.float32)).astype(jnp.bfloat16)
     packed = jnp.concatenate(
-        [by_owner(sums_local), by_owner(top_local), by_owner(total_local)], axis=1
-    )
-    parts = lax.all_to_all(packed, "tensor", 0, 0, tiled=True)
+        [
+            by_owner(sums_local.astype(jnp.bfloat16)),
+            by_owner(top_local.astype(jnp.bfloat16)),
+            by_owner(total_high),
+            by_owner(total_low),
+        ],
+        axis=1,
+    )
+    parts = lax.all_to_all(packed, "tensor", 0, 0, tiled=True).astype(jnp.float32)
     spread = requests * heads_here
     part_sums = parts[:, :spread].reshape(tensor_size, requests, heads_here, head_dim)
     part_top = parts[:, spread : spread + pair_rows].reshape(tensor_size, requests, heads_here)
-    part_total = parts[:, spread + pair_rows :].reshape(tensor_size, requests, heads_here)
+    part_total = (
+        parts[:, spread + pair_rows : spread + 2 * pair_rows]
+        + parts[:, spread + 2 * pair_rows :]
+    ).reshape(tensor_size, requests, heads_here)
     top_all = jnp.max(part_top, axis=0)
     factor = jnp.exp(part_top - top_all[None])
     total_mine = jnp.sum(part_total * factor, axis=0)
@@ -164,19 +177,14 @@
     attn_parts = lax.all_to_all(
         jnp.dot(attn_heads, out_weight, preferred_element_type=jnp.float32).astype(jnp.bfloat16),
         "tensor",
-        split_axis=1,
+        split_axis=0,
         concat_axis=0,
         tiled=True,
-    ).reshape(tensor_size, requests, width_here)
-    attn_cols = jnp.sum(attn_parts.astype(jnp.float32), axis=0)
-    residual_cols = lax.dynamic_slice_in_dim(residual_all, tensor_rank * width_here, width_here, 1)
-    middle_cols = (residual_cols.astype(jnp.float32) + attn_cols).astype(jnp.bfloat16)
-    middle_wide = middle_cols.astype(jnp.float32)
-    square_sum = lax.psum(jnp.sum(middle_wide * middle_wide, axis=1, keepdims=True), "tensor")
-    gain_cols = lax.dynamic_slice_in_dim(moe_gain, tensor_rank * width_here, width_here, 0)
-    cols_in = (
-        middle_wide * lax.rsqrt(square_sum / model_width + EPSILON) * gain_cols
-    ).astype(jnp.bfloat16)
+    ).reshape(tensor_size, tokens_here, model_width)
+    attn_out = jnp.sum(attn_parts.astype(jnp.float32), axis=0)
+    middle = (residual_in.astype(jnp.float32) + attn_out).astype(jnp.bfloat16)
+    moe_in = rms_scale(middle.astype(jnp.float32), moe_gain).astype(jnp.bfloat16)
+    cols_in = lax.all_to_all(moe_in, "tensor", split_axis=1, concat_axis=0, tiled=True)
     local_experts = gate_weight.shape[0]
     experts_all = local_experts * owners
     topk = routes.shape[1]
@@ -211,9 +219,9 @@
     ).astype(jnp.float32)
     returned = returned.reshape(experts_all * capacity, width_here)
     picked_rows = returned[code_of]
-    moe_cols = jnp.sum(share[:, :, None] * picked_rows, axis=1)
-    layer_cols = (middle_wide + moe_cols).astype(jnp.bfloat16)
-    layer_out = lax.all_to_all(layer_cols, "tensor", split_axis=0, concat_axis=1, tiled=True)
+    moe_cols = jnp.sum(share[:, :, None] * picked_rows, axis=1).astype(jnp.bfloat16)
+    moe_out = lax.all_to_all(moe_cols, "tensor", split_axis=0, concat_axis=1, tiled=True)
+    layer_out = (middle.astype(jnp.float32) + moe_out.astype(jnp.float32)).astype(jnp.bfloat16)
     return (layer_out, new_rows)
 
 

time: 294 us -> 274 us (0.932)
  blocking collectives: 77.6 us -> 64.9 us
  local copies, waits for them, and re-layouts: 28.7 us -> 19.3 us
  starting transfers between devices: 17.5 us -> 21.3 us
  other arithmetic: 18.4 us -> 15 us
  waiting for transfers between devices: 107 us -> 110 us
    psum x1 -> x0, blocking collectives: 12.6 us -> none  [body(): lax.psum(jnp.sum(middle_wide * middle_wide, axis=1, keepdims=True), 'tens...]
    all_to_all x1 -> x2, starting transfers between devices: 3.66 us -> 7.71 us  [the longest x1 4.36 us: body(): lax.all_to_all(packed, 'tensor', 0, 0, tiled=True).astype(jnp.float32)]
    unnamed x39 -> x36, local copies, waits for them, and re-layouts: 7.56 us -> 6.24 us
    all_to_all x1 -> x2, waiting for transfers between devices: 13.5 us -> 14 us  [the longest x1 9.35 us: body(): lax.all_to_all(packed, 'tensor', 0, 0, tiled=True).astype(jnp.float32)]
  transfers between devices with their start and end apart: 5 -> 6, of which waited for: 5 -> 6; matrix products, arithmetic and copies ran while one was open for 1% -> 1% of each run, Pallas kernels for 0% -> 0%
where the time goes in v7:
time: 274 us; the launch traced here: 273 us
  waiting for transfers between devices  110 us (40%)
  blocking collectives  64.9 us (24%)
  matrix products  27.7 us (10%)
  starting transfers between devices  21.3 us (8%)
  local copies, waits for them, and re-layouts  19.3 us (7%)
  other arithmetic  15 us (5%)
  between operations  14.7 us (5%)
    reduce_scatter x1, waiting for transfers between devices, body(): lax.psum_scatter(partial_out, 'tensor', scatter_dimension=3, tiled=True)  41.6 us
    all_gather x1, waiting for transfers between devices, body(): lax.all_gather(arrived, 'tensor', axis=2, tiled=True)  32.4 us
    all_to_all x1, blocking collectives, body(): lax.all_to_all(outgoing, 'dp', split_axis=0, concat_axis=0, tiled=True)  28.8 us
    all_to_all x1, waiting for transfers between devices, body(): lax.all_to_all(summed_out.reshape(owners, local_experts * capacity, width...  14.7 us
    all_gather x1, blocking collectives, body(): residual_all = lax.all_gather(residual_in, 'tensor', axis=0, tiled=True)  13.5 us
    all_gather x1, blocking collectives, body(): lax.all_gather(joined, 'tensor', axis=1, tiled=True)  13.3 us
    all_to_all x1, starting transfers between devices, body(): lax.all_to_all(summed_out.reshape(owners, local_experts * capacity, width...  10.1 us
    all_to_all x1, waiting for transfers between devices, body(): lax.all_to_all(packed, 'tensor', 0, 0, tiled=True).astype(jnp.float32)  9.35 us
  transfers between devices with their start and end apart: 6, of which 6 were waited for; matrix products, arithmetic and copies ran while one was open for 1% of the time, Pallas kernels for 0%

profile of v7, /device:TPU:32, one launch (start us, length us, event | category | flops | bytes accessed | tf_op | source)
XLA Modules:
  0.0 272.6 jit_solution(13333977363274659230)
XLA Ops:
  7.2 13.5 %all_gather.9 = bf16[64,2048]{1,0:T(8,128)(2,1)S(1)} all-gather(bf16[8,2048]{1,0:T(8,128)(2,1)} %param.18), channel_id=1, replica_groups=mesh['dp'=32,'tensor'=8] {'tensor'}, dimensions={0}, use_global_device_ids=true | all-gather | bytes 294912 | tf_op jit(solution)/shard_map/all_gather | solution.py:65
  20.9 1.4 multiply_reduce_fusion.1
  23.2 2.1 fusion.82
  26.8 13.3 %all_gather.10 = bf16[64,5120]{1,0:T(8,128)(2,1)S(1)} all-gather(bf16[64,640]{1,0:T(8,128)(2,1)S(1)} %pad_maximum_fusion.1), channel_id=1, replica_groups=mesh['dp'=32,'tensor'=8] {'tensor'}, dimensions={1}, use_global_device_ids=true | all-gather | bytes 737280 | tf_op jit(solution)/shard_map/all_gather | solution.py:86
  41.3 2.1 fusion.103
  43.4 2.0 copy.295
  45.6 4.0 %fusion = (bf16[64,4,8]{2,0,1:T(8,128)(2,1)S(1)}, f32[4,64,8,2,256]{4,2,3,1,0:T(8,128)}) fusion(pred[64,2,256]{2,1,0:T(4,128)(4,1)S(1)} %broadcast_and_fusion, bf16[2,256,4,128,1]{1,3,2,0,4:T(8,128)(2,1)} %bitcast.203, bf16[64,4,8,128]{3,2,1,0:T(8,128)(2,1)S(1)} %reshape.366), kind=kOutput, calls=%fused_computation.3 | convolution fusion | flops 271579136 | bytes 5279744 | tf_op jit(solution)/shard_map/rgqd,npgd->rgqnp/dot_general | solution.py:102
  49.7 2.9 %slice_bitcast_fusion = (bf16[64,2,4,8,128]{4,3,2,1,0:T(8,128)(2,1)}, bf16[64,2,4,8,128]{4,3,2,1,0:T(8,128)(2,1)S(1)}) fusion(bf16[64,16,1024]{2,1,0:T(8,128)(2,1)} %param.32), kind=kLoop, calls=%fused_computation.41 | loop fusion | bytes 4194304
  52.6 1.7 select_reduce_fusion
  56.3 4.4 %fusion.7 = f32[64,4,8]{2,0,1:T(8,128)} fusion(f32[4,64,8,2,256]{4,2,3,1,0:T(8,128)} %get-tuple-element.28, f32[64,4,8]{2,0,1:T(8,128)S(1)} %copy.244, pred[64,2,256]{2,1,0:T(4,128)(4,1)S(1)} %broadcast_and_fusion), kind=kLoop, calls=%fused_computation.11 | loop fusion | flops 4192256 | bytes 4243456 | tf_op jit(solution)/shard_map/reduce_sum | solution.py:129
  60.8 3.2 %fusion.20 = f32[64,4,8,128]{3,2,0,1:T(8,128)} fusion(f32[4,64,8,2,256]{4,2,3,1,0:T(8,128)S(1)} %copy-done.1, f32[64,4,8]{2,0,1:T(8,128)S(1)} %copy.244, pred[64,2,256]{2,1,0:T(4,128)(4,1)S(1)} %broadcast_and_fusion, bf16[2,256,4,128,1]{1,3,2,0,4:T(8,128)(2,1)} %bitcast.207), kind=kOutput, calls=%fused_computation.25 | convolution fusion | flops 272629760 | bytes 5808128 | tf_op jit(solution)/shard_map/rgqnp,npgd->rgqd/dot_general | solution.py:130
  63.9 1.5 copy.250
  66.2 2.0 fusion.24
  71.5 4.4 %all-to-all-start = ((bf16[8,262,128]{2,1,0:T(8,128)(2,1)}), bf16[8,262,128]{2,1,0:T(8,128)(2,1)}, u32[]{:S(2)}, u32[]{:S(2)}) async-start(bf16[8,262,128]{2,1,0:T(8,128)(2,1)} %copy.262), calls=%async_computation | async-start | bytes 1081344 | tf_op jit(solution)/shard_map/all_to_all | solution.py:161
  76.8 9.3 %all-to-all-done = bf16[8,262,128]{2,1,0:T(8,128)(2,1)} async-done(((bf16[8,262,128]{2,1,0:T(8,128)(2,1)}), bf16[8,262,128]{2,1,0:T(8,128)(2,1)}, u32[]{:S(2)}, u32[]{:S(2)}) %all-to-all-start) | async-done | bytes 536608 | tf_op jit(solution)/shard_map/all_to_all | solution.py:161
  86.2 1.1 copy_convert_fusion
  88.1 1.2 fusion.9
  89.3 3.4 %all-to-all-start.1 = ((bf16[8,8,2048]{2,1,0:T(8,128)(2,1)}), bf16[8,8,2048]{2,1,0:T(8,128)(2,1)S(1)}, u32[]{:S(2)}, u32[]{:S(2)}) async-start(bf16[8,8,2048]{2,1,0:T(8,128)(2,1)} %fusion.9), calls=%async_computation.1 | async-start | bytes 524288 | tf_op jit(solution)/shard_map/all_to_all | solution.py:177
  93.0 7.2 %all-to-all-done.1 = bf16[8,8,2048]{2,1,0:T(8,128)(2,1)S(1)} async-done(((bf16[8,8,2048]{2,1,0:T(8,128)(2,1)}), bf16[8,8,2048]{2,1,0:T(8,128)(2,1)S(1)}, u32[]{:S(2)}, u32[]{:S(2)}) %all-to-all-start.1) | async-done | bytes 262176 | tf_op jit(solution)/shard_map/all_to_all | solution.py:177
  101.1 3.3 %all-to-all-start.2 = ((bf16[8,8,256]{2,0,1:T(8,128)(2,1)}), bf16[8,8,256]{2,0,1:T(8,128)(2,1)S(1)}, u32[]{:S(2)}, u32[]{:S(2)}) async-start(bf16[8,8,256]{2,0,1:T(8,128)(2,1)} %bitcast.33), calls=%async_computation.2 | async-start | bytes 65536 | tf_op jit(solution)/shard_map/all_to_all | solution.py:187
  105.2 4.6 %all-to-all-done.2 = bf16[8,8,256]{2,0,1:T(8,128)(2,1)S(1)} async-done(((bf16[8,8,256]{2,0,1:T(8,128)(2,1)}), bf16[8,8,256]{2,0,1:T(8,128)(2,1)S(1)}, u32[]{:S(2)}, u32[]{:S(2)}) %all-to-all-start.2) | async-done | bytes 32800 | tf_op jit(solution)/shard_map/all_to_all | solution.py:187
  110.1 28.8 %all_to_all.53 = bf16[32,32,256]{2,1,0:T(8,128)(2,1)} all-to-all(bf16[32,32,256]{2,1,0:T(8,128)(2,1)S(1)} %bitcast.201), channel_id=1, replica_groups=mesh['dp'=32,'tensor'=8] {'dp'}, dimensions={0} | all-to-all | bytes 1048576 | tf_op jit(solution)/shard_map/all_to_all | solution.py:202
  139.0 32.4 %all-gather.2.cloned.1.call-done = bf16[32,32,2048]{2,1,0:T(8,128)(2,1)} async-done(((bf16[32,32,256]{2,1,0:T(8,128)(2,1)}), bf16[32,32,2048]{2,1,0:T(8,128)(2,1)}) %all-gather.2.cloned.1.call-update) | async-done | bytes 4194320 | tf_op jit(solution)/shard_map/all_gather | solution.py:203
  171.4 3.9 %fusion.25 = f32[32,4,8,96]{3,2,0,1:T(8,128)S(1)} fusion(bf16[4,2048,96]{1,2,0:T(8,128)(2,1)} %param.26, bf16[32,32,2048]{2,1,0:T(8,128)(2,1)} %all-gather.2.cloned.1.call-done), kind=kOutput, calls=%fused_computation.31 | convolution fusion | flops 402653184 | bytes 6160384 | tf_op jit(solution)/shard_map/necd,edf->necf/dot_general | solution.py:206
  175.3 7.4 %convert_bitcast_fusion = bf16[32,4,8,2048]{3,2,0,1:T(8,128)(2,1)} fusion(bf16[4,96,2048]{2,1,0:T(8,128)(2,1)} %param.28, bf16[4,2048,96]{1,2,0:T(8,128)(2,1)} %param.27, f32[32,4,8,96]{3,2,0,1:T(8,128)S(1)} %fusion.25, bf16[32,32,2048]{2,1,0:T(8,128)(2,1)} %all-gather.2.cloned.1.call-done), kind=kOutput, calls=%fused_computation.6 | convolution fusion | flops 807993344 | bytes 11927552 | tf_op jit(solution)/shard_map/necf,efd->necd/dot_general | solution.py:209
  182.8 41.6 %reduce-scatter.2.cloned.1.call-done = bf16[32,4,8,256]{3,2,0,1:T(8,128)(2,1)} async-done(((bf16[32,4,8,2048]{3,2,0,1:T(8,128)(2,1)}), bf16[32,4,8,256]{3,2,0,1:T(8,128)(2,1)}) %reduce-scatter.2.cloned.1.call-update) | async-done | bytes 524304 | tf_op jit(solution)/shard_map/reduce_scatter | solution.py:212
  224.4 1.9 copy.352
  226.3 10.1 %all-to-all-start.4 = ((bf16[32,32,256]{2,1,0:T(8,128)(2,1)}), bf16[32,32,256]{2,1,0:T(8,128)(2,1)}, u32[]{:S(2)}, u32[]{:S(2)}) async-start(bf16[32,32,256]{2,1,0:T(8,128)(2,1)} %bitcast.193), calls=%async_computation.5 | async-start | bytes 1048576 | tf_op jit(solution)/shard_map/all_to_all | solution.py:213
  236.7 14.7 %all-to-all-done.4 = bf16[32,32,256]{2,1,0:T(8,128)(2,1)} async-done(((bf16[32,32,256]{2,1,0:T(8,128)(2,1)}), bf16[32,32,256]{2,1,0:T(8,128)(2,1)}, u32[]{:S(2)}, u32[]{:S(2)}) %all-to-all-start.4) | async-done | bytes 524320 | tf_op jit(solution)/shard_map/all_to_all | solution.py:213
  252.5 2.2 gather_fusion
  254.7 1.3 fusion.59
  256.0 9.2 %all_to_all.54 = bf16[8,8,256]{2,1,0:T(8,128)(2,1)S(1)} all-to-all(bf16[8,8,256]{2,1,0:T(8,128)(2,1)S(1)} %bitcast.216), channel_id=1, replica_groups=mesh['dp'=32,'tensor'=8] {'tensor'}, dimensions={0} | all-to-all | bytes 65536 | tf_op jit(solution)/shard_map/all_to_all | solution.py:223
  (129 shorter events, 15.6 us)
Async XLA Ops:
  7.2 81.0 %copy-start = (bf16[512,2048]{1,0:T(8,128)(2,1)S(1)}, bf16[512,2048]{1,0:T(8,128)(2,1)}, u32[]{:S(2)}) copy-start(bf16[512,2048]{1,0:T(8,128)(2,1)} %param.24) | copy-start | bytes 6291460
  7.2 19.0 %copy-start.10 = (f32[128]{0:T(128)S(1)}, f32[128]{0:T(128)}, u32[]{:S(2)}) copy-start(f32[128]{0:T(128)} %param.23) | copy-start | bytes 1540
  7.2 18.4 %copy-start.11 = (f32[128]{0:T(128)S(1)}, f32[128]{0:T(128)}, u32[]{:S(2)}) copy-start(f32[128]{0:T(128)} %param.22) | copy-start | bytes 1540
  7.2 18.7 %copy-start.13 = (s32[2]{0:T(128)S(1)}, s32[2]{0:T(128)}, u32[]{:S(2)}) copy-start(s32[2]{0:T(128)} %param.33) | copy-start | bytes 28
  7.2 18.7 %copy-start.12 = (s32[64]{0:T(128)S(1)}, s32[64]{0:T(128)}, u32[]{:S(2)}) copy-start(s32[64]{0:T(128)} %param.35) | copy-start | bytes 772
  7.2 18.9 %copy-start.14 = (s32[64]{0:T(128)S(1)}, s32[64]{0:T(128)}, u32[]{:S(2)}) copy-start(s32[64]{0:T(128)} %param.34) | copy-start | bytes 772
  26.4 13.7 %copy-start.6 = (bf16[64,128]{1,0:T(8,128)(2,1)}, bf16[64,128]{1,0:T(8,128)(2,1)S(1)}, u32[]{:S(2)}) copy-start(bf16[64,128]{1,0:T(8,128)(2,1)S(1)} %get-tuple-element.21) | copy-start | bytes 49156
  41.2 13.2 %copy-start.3 = (f32[64,4,1,8]{0,3,1,2:T(8,128)}, f32[64,4,1,8]{0,3,1,2:T(8,128)S(1)}, u32[]{:S(2)}) copy-start(f32[64,4,1,8]{0,3,1,2:T(8,128)S(1)} %copy.279) | copy-start | bytes 24580
  56.3 4.4 %copy-start.1 = (f32[4,64,8,2,256]{4,2,3,1,0:T(8,128)S(1)}, f32[4,64,8,2,256]{4,2,3,1,0:T(8,128)}, u32[]{:S(2)}) copy-start(f32[4,64,8,2,256]{4,2,3,1,0:T(8,128)} %get-tuple-element.28) | copy-start | bytes 12582916
  60.8 4.7 %copy-start.2 = (f32[64,4,8,16]{3,2,1,0:T(8,128)S(1)}, f32[64,4,8,16]{3,2,1,0:T(8,128)}, u32[]{:S(2)}) copy-start(f32[64,4,8,16]{3,2,1,0:T(8,128)} %get-tuple-element.30) | copy-start | bytes 393220
  63.9 5.9 %copy-start.4 = (f32[64,4,1,8]{0,3,1,2:T(8,128)S(1)}, f32[64,4,1,8]{0,3,1,2:T(8,128)}, u32[]{:S(2)}) copy-start(f32[64,4,1,8]{0,3,1,2:T(8,128)} %copy-done.3) | copy-start | bytes 24580
  66.2 9.7 %copy-start.8 = (s32[64,8]{0,1:T(8,128)S(1)}, s32[64,8]{0,1:T(8,128)}, u32[]{:S(2)}) copy-start(s32[64,8]{0,1:T(8,128)} %param.29) | copy-start | bytes 6148
  71.5 14.7 %all-to-all-start = ((bf16[8,262,128]{2,1,0:T(8,128)(2,1)}), bf16[8,262,128]{2,1,0:T(8,128)(2,1)}, u32[]{:S(2)}, u32[]{:S(2)}) async-start(bf16[8,262,128]{2,1,0:T(8,128)(2,1)} %copy.262), calls=%async_computation | async-start | bytes 1081344 | tf_op jit(solution)/shard_map/all_to_all | solution.py:161
  76.5 23.7 %copy-start.5 = (bf16[8,2048]{1,0:T(8,128)(2,1)S(1)}, bf16[8,2048]{1,0:T(8,128)(2,1)}, u32[]{:S(2)}) copy-start(bf16[8,2048]{1,0:T(8,128)(2,1)} %param.18) | copy-start | bytes 98308
  76.5 23.8 %copy-start.9 = (f32[2048]{0:T(1024)S(1)}, f32[2048]{0:T(1024)}, u32[]{:S(2)}) copy-start(f32[2048]{0:T(1024)} %param.25) | copy-start | bytes 24580
  89.3 10.8 %all-to-all-start.1 = ((bf16[8,8,2048]{2,1,0:T(8,128)(2,1)}), bf16[8,8,2048]{2,1,0:T(8,128)(2,1)S(1)}, u32[]{:S(2)}, u32[]{:S(2)}) async-start(bf16[8,8,2048]{2,1,0:T(8,128)(2,1)} %fusion.9), calls=%async_computation.1 | async-start | bytes 524288 | tf_op jit(solution)/shard_map/all_to_all | solution.py:177
  101.1 8.7 %all-to-all-start.2 = ((bf16[8,8,256]{2,0,1:T(8,128)(2,1)}), bf16[8,8,256]{2,0,1:T(8,128)(2,1)S(1)}, u32[]{:S(2)}, u32[]{:S(2)}) async-start(bf16[8,8,256]{2,0,1:T(8,128)(2,1)} %bitcast.33), calls=%async_computation.2 | async-start | bytes 65536 | tf_op jit(solution)/shard_map/all_to_all | solution.py:187
  104.4 67.0 %all-gather.2.cloned.1.call-start = ((), (), s32[]{:S(2)}) async-start(), calls=%async_computation.7 | async-start | bytes 4718592 | tf_op jit(solution)/shard_map/all_gather | solution.py:203
  139.0 85.4 %reduce-scatter.2.cloned.1.call-start = ((), (), s32[]{:S(2)}) async-start(), calls=%async_computation.8 | async-start | bytes 4718592 | tf_op jit(solution)/shard_map/reduce_scatter | solution.py:212
  182.7 53.8 %copy-start.7 = (f32[64,8]{0,1:T(8,128)S(1)}, f32[64,8]{0,1:T(8,128)}, u32[]{:S(2)}) copy-start(f32[64,8]{0,1:T(8,128)} %param.30) | copy-start | bytes 6148
  226.3 25.0 %all-to-all-start.4 = ((bf16[32,32,256]{2,1,0:T(8,128)(2,1)}), bf16[32,32,256]{2,1,0:T(8,128)(2,1)}, u32[]{:S(2)}, u32[]{:S(2)}) async-start(bf16[32,32,256]{2,1,0:T(8,128)(2,1)} %bitcast.193), calls=%async_computation.5 | async-start | bytes 1048576 | tf_op jit(solution)/shard_map/all_to_all | solution.py:213
Sparse Core Ops, SparseCore 0:
  139.1 32.2 all-gather.1
  182.9 41.4 reduce-scatter.1

commit v8 on v7

--- a/solution.py
+++ b/solution.py
@@ -206,10 +206,15 @@
     gate_val = jnp.einsum("necd,edf->necf", rows, gate_weight, preferred_element_type=jnp.float32)
     lift_val = jnp.einsum("necd,edf->necf", rows, lift_weight, preferred_element_type=jnp.float32)
     hidden_units = (jax.nn.silu(gate_val) * lift_val).astype(jnp.bfloat16)
-    partial_out = jnp.einsum(
-        "necf,efd->necd", hidden_units, down_weight, preferred_element_type=jnp.float32
+    hidden_all = lax.all_gather(hidden_units, "tensor", axis=0)
+    ff_here = down_weight.shape[1]
+    down_split = down_weight.reshape(local_experts, ff_here, tensor_size, width_here).transpose(
+        2, 0, 1, 3
+    )
+    down_cols = lax.all_to_all(down_split, "tensor", 0, 0, tiled=True)
+    summed_out = jnp.einsum(
+        "tnecf,tefd->necd", hidden_all, down_cols, preferred_element_type=jnp.float32
     ).astype(jnp.bfloat16)
-    summed_out = lax.psum_scatter(partial_out, "tensor", scatter_dimension=3, tiled=True)
     returned = lax.all_to_all(
         summed_out.reshape(owners, local_experts * capacity, width_here),
         "dp",

time: 274 us -> 268 us (0.978)
  waiting for transfers between devices: 110 us -> 71.8 us
  blocking collectives: 64.9 us -> 98.2 us
    reduce_scatter x1 -> x0, waiting for transfers between devices: 41.6 us -> none  [body(): lax.psum_scatter(partial_out, 'tensor', scatter_dimension=3, tiled=True)]
    all_to_all x0 -> x1, blocking collectives: none -> 33.9 us  [body(): down_cols = lax.all_to_all(down_split, 'tensor', 0, 0, tiled=True)]
    all_to_all x1, waiting for transfers between devices: 14.7 us -> 17.8 us  [body(): lax.all_to_all(summed_out.reshape(owners, local_experts * capacity, width...]
    unnamed x36 -> x47, local copies, waits for them, and re-layouts: 6.24 us -> 8.93 us
    dot_general x1 -> x2, matrix products: 7.41 us -> 4.79 us  [the longest x1 2.84 us: body(): jnp.einsum('tnecf,tefd->necd', hidden_all, down_cols, preferred_element_t...]
  transfers between devices with their start and end apart: 6 -> 6, of which waited for: 6 -> 6; matrix products, arithmetic and copies ran while one was open for 1% -> 2% of each run, Pallas kernels for 0% -> 0%
where the time goes in v8:
time: 268 us; the launch traced here: 267 us
  blocking collectives  98.2 us (37%)
  waiting for transfers between devices  71.8 us (27%)
  matrix products  25 us (9%)
  starting transfers between devices  21.3 us (8%)
  local copies, waits for them, and re-layouts  20.5 us (8%)
  other arithmetic  15.1 us (6%)
  between operations  14.7 us (5%)
    all_to_all x1, blocking collectives, body(): down_cols = lax.all_to_all(down_split, 'tensor', 0, 0, tiled=True)  33.9 us
    all_gather x1, waiting for transfers between devices, body(): lax.all_gather(arrived, 'tensor', axis=2, tiled=True)  32.4 us
    all_to_all x1, blocking collectives, body(): lax.all_to_all(outgoing, 'dp', split_axis=0, concat_axis=0, tiled=True)  28.8 us
    all_to_all x1, waiting for transfers between devices, body(): lax.all_to_all(summed_out.reshape(owners, local_experts * capacity, width...  17.8 us
    all_gather x1, blocking collectives, body(): residual_all = lax.all_gather(residual_in, 'tensor', axis=0, tiled=True)  13.5 us
    all_gather x1, blocking collectives, body(): lax.all_gather(joined, 'tensor', axis=1, tiled=True)  13.3 us
    all_to_all x1, starting transfers between devices, body(): lax.all_to_all(summed_out.reshape(owners, local_experts * capacity, width...  10.1 us
    all_to_all x1, waiting for transfers between devices, body(): lax.all_to_all(packed, 'tensor', 0, 0, tiled=True).astype(jnp.float32)  9.37 us
  transfers between devices with their start and end apart: 6, of which 6 were waited for; matrix products, arithmetic and copies ran while one was open for 2% of the time, Pallas kernels for 0%

profile of v8, /device:TPU:32, one launch (start us, length us, event | category | flops | bytes accessed | tf_op | source)
XLA Modules:
  0.0 266.6 jit_solution(14060132747875362030)
XLA Ops:
  7.2 13.5 %all_gather.15 = bf16[64,2048]{1,0:T(8,128)(2,1)S(1)} all-gather(bf16[8,2048]{1,0:T(8,128)(2,1)} %param.18), channel_id=1, replica_groups=mesh['dp'=32,'tensor'=8] {'tensor'}, dimensions={0}, use_global_device_ids=true | all-gather | bytes 294912 | tf_op jit(solution)/shard_map/all_gather | solution.py:65
  20.9 1.4 multiply_reduce_fusion.1
  23.3 2.1 fusion.83
  26.8 13.3 %all_gather.16 = bf16[64,5120]{1,0:T(8,128)(2,1)S(1)} all-gather(bf16[64,640]{1,0:T(8,128)(2,1)S(1)} %pad_maximum_fusion.1), channel_id=1, replica_groups=mesh['dp'=32,'tensor'=8] {'tensor'}, dimensions={1}, use_global_device_ids=true | all-gather | bytes 737280 | tf_op jit(solution)/shard_map/all_gather | solution.py:86
  41.3 2.1 fusion.103
  43.4 2.0 copy.319
  45.6 4.0 %fusion = (bf16[64,4,8]{2,0,1:T(8,128)(2,1)S(1)}, f32[4,64,8,2,256]{4,2,3,1,0:T(8,128)}) fusion(pred[64,2,256]{2,1,0:T(4,128)(4,1)S(1)} %broadcast_and_fusion, bf16[2,256,4,128,1]{1,3,2,0,4:T(8,128)(2,1)} %bitcast.226, bf16[64,4,8,128]{3,2,1,0:T(8,128)(2,1)S(1)} %reshape.369), kind=kOutput, calls=%fused_computation.3 | convolution fusion | flops 271579136 | bytes 5279744 | tf_op jit(solution)/shard_map/rgqd,npgd->rgqnp/dot_general | solution.py:102
  49.7 2.9 %slice_bitcast_fusion = (bf16[64,2,4,8,128]{4,3,2,1,0:T(8,128)(2,1)}, bf16[64,2,4,8,128]{4,3,2,1,0:T(8,128)(2,1)S(1)}) fusion(bf16[64,16,1024]{2,1,0:T(8,128)(2,1)} %param.32), kind=kLoop, calls=%fused_computation.46 | loop fusion | bytes 4194304
  52.7 1.7 select_reduce_fusion
  56.4 4.4 %fusion.7 = f32[64,4,8]{2,0,1:T(8,128)} fusion(f32[4,64,8,2,256]{4,2,3,1,0:T(8,128)} %get-tuple-element.28, f32[64,4,8]{2,0,1:T(8,128)S(1)} %copy.262, pred[64,2,256]{2,1,0:T(4,128)(4,1)S(1)} %broadcast_and_fusion), kind=kLoop, calls=%fused_computation.10 | loop fusion | flops 4192256 | bytes 4243456 | tf_op jit(solution)/shard_map/reduce_sum | solution.py:129
  60.8 3.2 %fusion.25 = f32[64,4,8,128]{3,2,0,1:T(8,128)} fusion(f32[4,64,8,2,256]{4,2,3,1,0:T(8,128)S(1)} %copy-done.1, f32[64,4,8]{2,0,1:T(8,128)S(1)} %copy.262, pred[64,2,256]{2,1,0:T(4,128)(4,1)S(1)} %broadcast_and_fusion, bf16[2,256,4,128,1]{1,3,2,0,4:T(8,128)(2,1)} %bitcast.231), kind=kOutput, calls=%fused_computation.28 | convolution fusion | flops 272629760 | bytes 5808128 | tf_op jit(solution)/shard_map/rgqnp,npgd->rgqd/dot_general | solution.py:130
  64.0 1.5 copy.268
  66.7 1.8 fusion.32
  70.8 4.4 %all-to-all-start = ((bf16[8,262,128]{2,1,0:T(8,128)(2,1)}), bf16[8,262,128]{2,1,0:T(8,128)(2,1)}, u32[]{:S(2)}, u32[]{:S(2)}) async-start(bf16[8,262,128]{2,1,0:T(8,128)(2,1)} %copy.280), calls=%async_computation | async-start | bytes 1081344 | tf_op jit(solution)/shard_map/all_to_all | solution.py:161
  76.1 9.4 %all-to-all-done = bf16[8,262,128]{2,1,0:T(8,128)(2,1)} async-done(((bf16[8,262,128]{2,1,0:T(8,128)(2,1)}), bf16[8,262,128]{2,1,0:T(8,128)(2,1)}, u32[]{:S(2)}, u32[]{:S(2)}) %all-to-all-start) | async-done | bytes 536608 | tf_op jit(solution)/shard_map/all_to_all | solution.py:161
  87.5 1.2 fusion.9
  88.6 3.4 %all-to-all-start.1 = ((bf16[8,8,2048]{2,1,0:T(8,128)(2,1)}), bf16[8,8,2048]{2,1,0:T(8,128)(2,1)S(1)}, u32[]{:S(2)}, u32[]{:S(2)}) async-start(bf16[8,8,2048]{2,1,0:T(8,128)(2,1)} %fusion.9), calls=%async_computation.1 | async-start | bytes 524288 | tf_op jit(solution)/shard_map/all_to_all | solution.py:177
  92.3 7.2 %all-to-all-done.1 = bf16[8,8,2048]{2,1,0:T(8,128)(2,1)S(1)} async-done(((bf16[8,8,2048]{2,1,0:T(8,128)(2,1)}), bf16[8,8,2048]{2,1,0:T(8,128)(2,1)S(1)}, u32[]{:S(2)}, u32[]{:S(2)}) %all-to-all-start.1) | async-done | bytes 262176 | tf_op jit(solution)/shard_map/all_to_all | solution.py:177
  100.4 3.3 %all-to-all-start.2 = ((bf16[8,8,256]{2,0,1:T(8,128)(2,1)}), bf16[8,8,256]{2,0,1:T(8,128)(2,1)S(1)}, u32[]{:S(2)}, u32[]{:S(2)}) async-start(bf16[8,8,256]{2,0,1:T(8,128)(2,1)} %bitcast.33), calls=%async_computation.2 | async-start | bytes 65536 | tf_op jit(solution)/shard_map/all_to_all | solution.py:187
  104.5 4.6 %all-to-all-done.2 = bf16[8,8,256]{2,0,1:T(8,128)(2,1)S(1)} async-done(((bf16[8,8,256]{2,0,1:T(8,128)(2,1)}), bf16[8,8,256]{2,0,1:T(8,128)(2,1)S(1)}, u32[]{:S(2)}, u32[]{:S(2)}) %all-to-all-start.2) | async-done | bytes 32800 | tf_op jit(solution)/shard_map/all_to_all | solution.py:187
  109.5 28.8 %all_to_all.58 = bf16[32,32,256]{2,1,0:T(8,128)(2,1)} all-to-all(bf16[32,32,256]{2,1,0:T(8,128)(2,1)S(1)} %bitcast.224), channel_id=1, replica_groups=mesh['dp'=32,'tensor'=8] {'dp'}, dimensions={0} | all-to-all | bytes 1048576 | tf_op jit(solution)/shard_map/all_to_all | solution.py:202
  138.4 32.4 %all-gather.4.cloned.1.call-done = bf16[32,32,2048]{2,1,0:T(8,128)(2,1)} async-done(((bf16[32,32,256]{2,1,0:T(8,128)(2,1)}), bf16[32,32,2048]{2,1,0:T(8,128)(2,1)}) %all-gather.4.cloned.1.call-update) | async-done | bytes 4194320 | tf_op jit(solution)/shard_map/all_gather | solution.py:203
  170.7 4.1 %fusion.36 = f32[32,4,8,96]{3,2,0,1:T(8,128)S(1)} fusion(bf16[4,2048,96]{1,2,0:T(8,128)(2,1)} %param.26, bf16[32,32,2048]{2,1,0:T(8,128)(2,1)} %all-gather.4.cloned.1.call-done), kind=kOutput, calls=%fused_computation.36 | convolution fusion | flops 402653184 | bytes 6160384 | tf_op jit(solution)/shard_map/necd,edf->necf/dot_general | solution.py:206
  175.1 1.9 fusion.51
  177.1 1.9 copy.329
  179.5 33.9 %all_to_all.59 = bf16[8,4,96,256]{3,2,1,0:T(8,128)(2,1)} all-to-all(bf16[8,4,96,256]{3,2,1,0:T(8,128)(2,1)S(1)} %copy.292), channel_id=1, replica_groups=mesh['dp'=32,'tensor'=8] {'tensor'}, dimensions={0} | all-to-all | bytes 3145728 | tf_op jit(solution)/shard_map/all_to_all | solution.py:214
  213.9 2.8 %fusion.33 = bf16[32,4,8,256]{3,2,0,1:T(8,128)(2,1)S(1)} fusion(bf16[8,32,4,8,96]{4,3,1,0,2:T(8,128)(2,1)} %bitcast.245, bf16[8,4,96,256]{3,2,1,0:T(8,128)(2,1)} %all_to_all.59), kind=kOutput, calls=%fused_computation.35 | convolution fusion | flops 402915328 | bytes 3670016 | tf_op jit(solution)/shard_map/tnecf,tefd->necd/dot_general | solution.py:215
  217.6 10.1 %all-to-all-start.5 = ((bf16[32,32,256]{2,1,0:T(8,128)(2,1)}), bf16[32,32,256]{2,1,0:T(8,128)(2,1)}, u32[]{:S(2)}, u32[]{:S(2)}) async-start(bf16[32,32,256]{2,1,0:T(8,128)(2,1)} %bitcast.214), calls=%async_computation.5 | async-start | bytes 1048576 | tf_op jit(solution)/shard_map/all_to_all | solution.py:218
  228.1 17.8 %all-to-all-done.5 = bf16[32,32,256]{2,1,0:T(8,128)(2,1)} async-done(((bf16[32,32,256]{2,1,0:T(8,128)(2,1)}), bf16[32,32,256]{2,1,0:T(8,128)(2,1)}, u32[]{:S(2)}, u32[]{:S(2)}) %all-to-all-start.5) | async-done | bytes 524320 | tf_op jit(solution)/shard_map/all_to_all | solution.py:218
  247.0 2.2 gather_fusion
  249.2 1.3 fusion.66
  250.5 8.6 %all_to_all.60 = bf16[8,8,256]{2,1,0:T(8,128)(2,1)S(1)} all-to-all(bf16[8,8,256]{2,1,0:T(8,128)(2,1)S(1)} %bitcast.240), channel_id=1, replica_groups=mesh['dp'=32,'tensor'=8] {'tensor'}, dimensions={0} | all-to-all | bytes 65536 | tf_op jit(solution)/shard_map/all_to_all | solution.py:228
  (144 shorter events, 18.5 us)
Async XLA Ops:
  7.2 80.3 %copy-start = (bf16[512,2048]{1,0:T(8,128)(2,1)S(1)}, bf16[512,2048]{1,0:T(8,128)(2,1)}, u32[]{:S(2)}) copy-start(bf16[512,2048]{1,0:T(8,128)(2,1)} %param.24) | copy-start | bytes 6291460
  20.7 4.9 %copy-start.14 = (f32[128]{0:T(128)S(1)}, f32[128]{0:T(128)}, u32[]{:S(2)}) copy-start(f32[128]{0:T(128)} %param.22) | copy-start | bytes 1540
  22.3 3.6 %copy-start.15 = (s32[64]{0:T(128)S(1)}, s32[64]{0:T(128)}, u32[]{:S(2)}) copy-start(s32[64]{0:T(128)} %param.35) | copy-start | bytes 772
  22.4 3.6 %copy-start.16 = (s32[2]{0:T(128)S(1)}, s32[2]{0:T(128)}, u32[]{:S(2)}) copy-start(s32[2]{0:T(128)} %param.33) | copy-start | bytes 28
  22.4 3.8 %copy-start.17 = (s32[64]{0:T(128)S(1)}, s32[64]{0:T(128)}, u32[]{:S(2)}) copy-start(s32[64]{0:T(128)} %param.34) | copy-start | bytes 772
  22.4 3.8 %copy-start.13 = (f32[128]{0:T(128)S(1)}, f32[128]{0:T(128)}, u32[]{:S(2)}) copy-start(f32[128]{0:T(128)} %param.23) | copy-start | bytes 1540
  26.4 13.7 %copy-start.9 = (bf16[64,128]{1,0:T(8,128)(2,1)}, bf16[64,128]{1,0:T(8,128)(2,1)S(1)}, u32[]{:S(2)}) copy-start(bf16[64,128]{1,0:T(8,128)(2,1)S(1)} %get-tuple-element.21) | copy-start | bytes 49156
  41.2 13.2 %copy-start.6 = (f32[64,4,1,8]{0,3,1,2:T(8,128)}, f32[64,4,1,8]{0,3,1,2:T(8,128)S(1)}, u32[]{:S(2)}) copy-start(f32[64,4,1,8]{0,3,1,2:T(8,128)S(1)} %copy.300) | copy-start | bytes 24580
  56.4 4.4 %copy-start.1 = (f32[4,64,8,2,256]{4,2,3,1,0:T(8,128)S(1)}, f32[4,64,8,2,256]{4,2,3,1,0:T(8,128)}, u32[]{:S(2)}) copy-start(f32[4,64,8,2,256]{4,2,3,1,0:T(8,128)} %get-tuple-element.28) | copy-start | bytes 12582916
  60.8 4.6 %copy-start.2 = (f32[64,4,8,16]{3,2,1,0:T(8,128)S(1)}, f32[64,4,8,16]{3,2,1,0:T(8,128)}, u32[]{:S(2)}) copy-start(f32[64,4,8,16]{3,2,1,0:T(8,128)} %get-tuple-element.30) | copy-start | bytes 393220
  65.4 1.2 copy-start.3
  65.4 1.2 copy-start.5
  66.7 2.3 copy-start.4
  66.7 2.4 copy-start.7
  68.9 6.2 %copy-start.11 = (s32[64,8]{0,1:T(8,128)S(1)}, s32[64,8]{0,1:T(8,128)}, u32[]{:S(2)}) copy-start(s32[64,8]{0,1:T(8,128)} %param.29) | copy-start | bytes 6148
  70.8 14.7 %all-to-all-start = ((bf16[8,262,128]{2,1,0:T(8,128)(2,1)}), bf16[8,262,128]{2,1,0:T(8,128)(2,1)}, u32[]{:S(2)}, u32[]{:S(2)}) async-start(bf16[8,262,128]{2,1,0:T(8,128)(2,1)} %copy.280), calls=%async_computation | async-start | bytes 1081344 | tf_op jit(solution)/shard_map/all_to_all | solution.py:161
  87.3 12.3 %copy-start.8 = (bf16[8,2048]{1,0:T(8,128)(2,1)S(1)}, bf16[8,2048]{1,0:T(8,128)(2,1)}, u32[]{:S(2)}) copy-start(bf16[8,2048]{1,0:T(8,128)(2,1)} %param.18) | copy-start | bytes 98308
  87.3 12.4 %copy-start.12 = (f32[2048]{0:T(1024)S(1)}, f32[2048]{0:T(1024)}, u32[]{:S(2)}) copy-start(f32[2048]{0:T(1024)} %param.25) | copy-start | bytes 24580
  88.6 10.8 %all-to-all-start.1 = ((bf16[8,8,2048]{2,1,0:T(8,128)(2,1)}), bf16[8,8,2048]{2,1,0:T(8,128)(2,1)S(1)}, u32[]{:S(2)}, u32[]{:S(2)}) async-start(bf16[8,8,2048]{2,1,0:T(8,128)(2,1)} %fusion.9), calls=%async_computation.1 | async-start | bytes 524288 | tf_op jit(solution)/shard_map/all_to_all | solution.py:177
  100.4 8.7 %all-to-all-start.2 = ((bf16[8,8,256]{2,0,1:T(8,128)(2,1)}), bf16[8,8,256]{2,0,1:T(8,128)(2,1)S(1)}, u32[]{:S(2)}, u32[]{:S(2)}) async-start(bf16[8,8,256]{2,0,1:T(8,128)(2,1)} %bitcast.33), calls=%async_computation.2 | async-start | bytes 65536 | tf_op jit(solution)/shard_map/all_to_all | solution.py:187
  103.7 67.0 %all-gather.4.cloned.1.call-start = ((), (), s32[]{:S(2)}) async-start(), calls=%async_computation.7 | async-start | bytes 4718592 | tf_op jit(solution)/shard_map/all_gather | solution.py:203
  138.3 75.6 %all-gather.6.cloned.1.call-start = ((), (), s32[]{:S(2)}) async-start(), calls=%async_computation.8 | async-start | bytes 2359296 | tf_op jit(solution)/shard_map/all_gather | solution.py:209
  170.7 4.1 %copy-start.18 = (bf16[32,32,2048]{2,1,0:T(8,128)(2,1)S(1)}, bf16[32,32,2048]{2,1,0:T(8,128)(2,1)}, u32[]{:S(2)}) copy-start(bf16[32,32,2048]{2,1,0:T(8,128)(2,1)} %all-gather.4.cloned.1.call-done) | copy-start | bytes 12582916
  170.7 4.4 %copy-start.19 = (bf16[4,2048,96]{1,2,0:T(8,128)(2,1)S(1)}, bf16[4,2048,96]{1,2,0:T(8,128)(2,1)}, u32[]{:S(2)}) copy-start(bf16[4,2048,96]{1,2,0:T(8,128)(2,1)} %param.27) | copy-start | bytes 4718596
  216.7 11.2 %copy-start.10 = (f32[64,8]{0,1:T(8,128)S(1)}, f32[64,8]{0,1:T(8,128)}, u32[]{:S(2)}) copy-start(f32[64,8]{0,1:T(8,128)} %param.30) | copy-start | bytes 6148
  217.6 28.2 %all-to-all-start.5 = ((bf16[32,32,256]{2,1,0:T(8,128)(2,1)}), bf16[32,32,256]{2,1,0:T(8,128)(2,1)}, u32[]{:S(2)}, u32[]{:S(2)}) async-start(bf16[32,32,256]{2,1,0:T(8,128)(2,1)} %bitcast.214), calls=%async_computation.5 | async-start | bytes 1048576 | tf_op jit(solution)/shard_map/all_to_all | solution.py:218
Sparse Core Ops, SparseCore 0:
  138.4 32.2 all-gather.3
  177.2 36.5 all-gather.5

commit v9 on v8

--- a/solution.py
+++ b/solution.py
@@ -203,15 +203,16 @@
     rows = lax.all_gather(arrived, "tensor", axis=2, tiled=True).reshape(
         owners, local_experts, capacity, model_width
     )
+    ff_here = down_weight.shape[1]
+    down_split = down_weight.reshape(local_experts, ff_here, tensor_size, width_here).transpose(
+        2, 0, 1, 3
+    )
+    down_cols = lax.all_to_all(down_split, "tensor", 0, 0, tiled=True)
+    rows, down_cols = lax.optimization_barrier((rows, down_cols))
     gate_val = jnp.einsum("necd,edf->necf", rows, gate_weight, preferred_element_type=jnp.float32)
     lift_val = jnp.einsum("necd,edf->necf", rows, lift_weight, preferred_element_type=jnp.float32)
     hidden_units = (jax.nn.silu(gate_val) * lift_val).astype(jnp.bfloat16)
     hidden_all = lax.all_gather(hidden_units, "tensor", axis=0)
-    ff_here = down_weight.shape[1]
-    down_split = down_weight.reshape(local_experts, ff_here, tensor_size, width_here).transpose(
-        2, 0, 1, 3
-    )
-    down_cols = lax.all_to_all(down_split, "tensor", 0, 0, tiled=True)
     summed_out = jnp.einsum(
         "tnecf,tefd->necd", hidden_all, down_cols, preferred_element_type=jnp.float32
     ).astype(jnp.bfloat16)

time: 268 us -> 271 us (1.011)
    all_gather x1, waiting for transfers between devices: 0.51 us -> 24.2 us  [body(): hidden_all = lax.all_gather(hidden_units, 'tensor', axis=0)]
    all_gather x1, waiting for transfers between devices: 32.4 us -> 11.2 us  [body(): lax.all_gather(arrived, 'tensor', axis=2, tiled=True)]
where the time goes in v9:
time: 271 us; the launch traced here: 269 us
  blocking collectives  98.3 us (36%)
  waiting for transfers between devices  74.4 us (27%)
  matrix products  25 us (9%)
  starting transfers between devices  21.3 us (8%)
  local copies, waits for them, and re-layouts  20.7 us (8%)
  other arithmetic  15.1 us (6%)
  between operations  14.7 us (5%)
    all_to_all x1, blocking collectives, body(): down_cols = lax.all_to_all(down_split, 'tensor', 0, 0, tiled=True)  34 us
    all_to_all x1, blocking collectives, body(): lax.all_to_all(outgoing, 'dp', split_axis=0, concat_axis=0, tiled=True)  28.8 us
    all_gather x1, waiting for transfers between devices, body(): hidden_all = lax.all_gather(hidden_units, 'tensor', axis=0)  24.2 us
    all_to_all x1, waiting for transfers between devices, body(): lax.all_to_all(summed_out.reshape(owners, local_experts * capacity, width...  17.8 us
    all_gather x1, blocking collectives, body(): residual_all = lax.all_gather(residual_in, 'tensor', axis=0, tiled=True)  13.5 us
    all_gather x1, blocking collectives, body(): lax.all_gather(joined, 'tensor', axis=1, tiled=True)  13.3 us
    all_gather x1, waiting for transfers between devices, body(): lax.all_gather(arrived, 'tensor', axis=2, tiled=True)  11.2 us
    all_to_all x1, starting transfers between devices, body(): lax.all_to_all(summed_out.reshape(owners, local_experts * capacity, width...  10.1 us
  transfers between devices with their start and end apart: 6, of which 6 were waited for; matrix products, arithmetic and copies ran while one was open for 2% of the time, Pallas kernels for 0%

profile of v9, /device:TPU:32, one launch (start us, length us, event | category | flops | bytes accessed | tf_op | source)
XLA Modules:
  0.0 269.4 jit_solution(10030943008383160532)
XLA Ops:
  7.2 13.5 %all_gather.15 = bf16[64,2048]{1,0:T(8,128)(2,1)S(1)} all-gather(bf16[8,2048]{1,0:T(8,128)(2,1)} %param.18), channel_id=1, replica_groups=mesh['dp'=32,'tensor'=8] {'tensor'}, dimensions={0}, use_global_device_ids=true | all-gather | bytes 294912 | tf_op jit(solution)/shard_map/all_gather | solution.py:65
  20.9 1.4 multiply_reduce_fusion.1
  23.3 2.1 fusion.84
  26.8 13.3 %all_gather.16 = bf16[64,5120]{1,0:T(8,128)(2,1)S(1)} all-gather(bf16[64,640]{1,0:T(8,128)(2,1)S(1)} %pad_maximum_fusion.1), channel_id=1, replica_groups=mesh['dp'=32,'tensor'=8] {'tensor'}, dimensions={1}, use_global_device_ids=true | all-gather | bytes 737280 | tf_op jit(solution)/shard_map/all_gather | solution.py:86
  41.3 2.1 fusion.104
  43.4 2.0 copy.359
  45.6 4.0 %fusion = (bf16[64,4,8]{2,0,1:T(8,128)(2,1)S(1)}, f32[4,64,8,2,256]{4,2,3,1,0:T(8,128)}) fusion(pred[64,2,256]{2,1,0:T(4,128)(4,1)S(1)} %broadcast_and_fusion, bf16[2,256,4,128,1]{1,3,2,0,4:T(8,128)(2,1)} %bitcast.204, bf16[64,4,8,128]{3,2,1,0:T(8,128)(2,1)S(1)} %reshape.369), kind=kOutput, calls=%fused_computation.3 | convolution fusion | flops 271579136 | bytes 5279744 | tf_op jit(solution)/shard_map/rgqd,npgd->rgqnp/dot_general | solution.py:102
  49.7 2.9 %slice_bitcast_fusion = (bf16[64,2,4,8,128]{4,3,2,1,0:T(8,128)(2,1)}, bf16[64,2,4,8,128]{4,3,2,1,0:T(8,128)(2,1)S(1)}) fusion(bf16[64,16,1024]{2,1,0:T(8,128)(2,1)} %param.32), kind=kLoop, calls=%fused_computation.45 | loop fusion | bytes 4194304
  52.7 1.7 select_reduce_fusion
  56.4 4.4 %fusion.7 = f32[64,4,8]{2,0,1:T(8,128)} fusion(f32[4,64,8,2,256]{4,2,3,1,0:T(8,128)} %get-tuple-element.32, f32[64,4,8]{2,0,1:T(8,128)S(1)} %copy.302, pred[64,2,256]{2,1,0:T(4,128)(4,1)S(1)} %broadcast_and_fusion), kind=kLoop, calls=%fused_computation.10 | loop fusion | flops 4192256 | bytes 4243456 | tf_op jit(solution)/shard_map/reduce_sum | solution.py:129
  60.8 3.2 %fusion.27 = f32[64,4,8,128]{3,2,0,1:T(8,128)} fusion(f32[4,64,8,2,256]{4,2,3,1,0:T(8,128)S(1)} %copy-done.1, f32[64,4,8]{2,0,1:T(8,128)S(1)} %copy.302, pred[64,2,256]{2,1,0:T(4,128)(4,1)S(1)} %broadcast_and_fusion, bf16[2,256,4,128,1]{1,3,2,0,4:T(8,128)(2,1)} %bitcast.209), kind=kOutput, calls=%fused_computation.28 | convolution fusion | flops 272629760 | bytes 5808128 | tf_op jit(solution)/shard_map/rgqnp,npgd->rgqd/dot_general | solution.py:130
  64.0 1.5 copy.308
  66.7 1.8 fusion.36
  70.8 4.4 %all-to-all-start = ((bf16[8,262,128]{2,1,0:T(8,128)(2,1)}), bf16[8,262,128]{2,1,0:T(8,128)(2,1)}, u32[]{:S(2)}, u32[]{:S(2)}) async-start(bf16[8,262,128]{2,1,0:T(8,128)(2,1)} %copy.320), calls=%async_computation | async-start | bytes 1081344 | tf_op jit(solution)/shard_map/all_to_all | solution.py:161
  76.1 9.4 %all-to-all-done = bf16[8,262,128]{2,1,0:T(8,128)(2,1)} async-done(((bf16[8,262,128]{2,1,0:T(8,128)(2,1)}), bf16[8,262,128]{2,1,0:T(8,128)(2,1)}, u32[]{:S(2)}, u32[]{:S(2)}) %all-to-all-start) | async-done | bytes 536608 | tf_op jit(solution)/shard_map/all_to_all | solution.py:161
  88.6 3.4 %all-to-all-start.1 = ((bf16[8,8,2048]{2,1,0:T(8,128)(2,1)}), bf16[8,8,2048]{2,1,0:T(8,128)(2,1)S(1)}, u32[]{:S(2)}, u32[]{:S(2)}) async-start(bf16[8,8,2048]{2,1,0:T(8,128)(2,1)} %fusion.9), calls=%async_computation.1 | async-start | bytes 524288 | tf_op jit(solution)/shard_map/all_to_all | solution.py:177
  92.3 7.2 %all-to-all-done.1 = bf16[8,8,2048]{2,1,0:T(8,128)(2,1)S(1)} async-done(((bf16[8,8,2048]{2,1,0:T(8,128)(2,1)}), bf16[8,8,2048]{2,1,0:T(8,128)(2,1)S(1)}, u32[]{:S(2)}, u32[]{:S(2)}) %all-to-all-start.1) | async-done | bytes 262176 | tf_op jit(solution)/shard_map/all_to_all | solution.py:177
  100.4 3.3 %all-to-all-start.2 = ((bf16[8,8,256]{2,0,1:T(8,128)(2,1)}), bf16[8,8,256]{2,0,1:T(8,128)(2,1)S(1)}, u32[]{:S(2)}, u32[]{:S(2)}) async-start(bf16[8,8,256]{2,0,1:T(8,128)(2,1)} %bitcast.33), calls=%async_computation.2 | async-start | bytes 65536 | tf_op jit(solution)/shard_map/all_to_all | solution.py:187
  104.5 4.6 %all-to-all-done.2 = bf16[8,8,256]{2,0,1:T(8,128)(2,1)S(1)} async-done(((bf16[8,8,256]{2,0,1:T(8,128)(2,1)}), bf16[8,8,256]{2,0,1:T(8,128)(2,1)S(1)}, u32[]{:S(2)}, u32[]{:S(2)}) %all-to-all-start.2) | async-done | bytes 32800 | tf_op jit(solution)/shard_map/all_to_all | solution.py:187
  109.5 28.8 %all_to_all.58 = bf16[32,32,256]{2,1,0:T(8,128)(2,1)} all-to-all(bf16[32,32,256]{2,1,0:T(8,128)(2,1)S(1)} %bitcast.202), channel_id=1, replica_groups=mesh['dp'=32,'tensor'=8] {'dp'}, dimensions={0} | all-to-all | bytes 1048576 | tf_op jit(solution)/shard_map/all_to_all | solution.py:202
  138.4 1.9 copy.369
  140.7 34.0 %all_to_all.59 = bf16[8,4,96,256]{3,2,1,0:T(8,128)(2,1)} all-to-all(bf16[8,4,96,256]{3,2,1,0:T(8,128)(2,1)S(1)} %copy.330), channel_id=1, replica_groups=mesh['dp'=32,'tensor'=8] {'tensor'}, dimensions={0} | all-to-all | bytes 3145728 | tf_op jit(solution)/shard_map/all_to_all | solution.py:210
  174.7 11.2 %all-gather.4.cloned.1.call-done = bf16[32,32,2048]{2,1,0:T(8,128)(2,1)} async-done(((bf16[32,32,256]{2,1,0:T(8,128)(2,1)}), bf16[32,32,2048]{2,1,0:T(8,128)(2,1)}) %all-gather.4.cloned.1.call-update) | async-done | bytes 4194320 | tf_op jit(solution)/shard_map/all_gather | solution.py:203
  186.0 4.1 %fusion.37 = f32[32,4,8,96]{3,2,0,1:T(8,128)S(1)} fusion(bf16[4,2048,96]{1,2,0:T(8,128)(2,1)} %param.26, bf16[32,4,8,2048]{3,2,1,0:T(8,128)(2,1)} %bitcast.224), kind=kOutput, calls=%fused_computation.35 | convolution fusion | flops 402653184 | bytes 6160384 | tf_op jit(solution)/shard_map/necd,edf->necf/dot_general | solution.py:212
  190.4 2.0 fusion.52
  192.4 24.2 %all-gather.6.cloned.1.call-done = bf16[256,4,8,96]{3,2,0,1:T(8,128)(2,1)} async-done(((bf16[32,4,8,96]{3,2,0,1:T(8,128)(2,1)}), bf16[256,4,8,96]{3,2,0,1:T(8,128)(2,1)}) %all-gather.6.cloned.1.call-update) | async-done | bytes 1572880 | tf_op jit(solution)/shard_map/all_gather | solution.py:215
  216.5 2.9 %fusion.31 = bf16[4,256,32,8]{1,2,3,0:T(8,128)(2,1)S(1)} fusion(bf16[8,32,4,8,96]{4,3,1,0,2:T(8,128)(2,1)} %bitcast.226, bf16[8,4,96,256]{3,2,1,0:T(8,128)(2,1)} %all_to_all.59), kind=kOutput, calls=%fused_computation.32 | convolution fusion | flops 402915328 | bytes 3670016 | tf_op jit(solution)/shard_map/tnecf,tefd->necd/dot_general | solution.py:216
  220.5 10.1 %all-to-all-start.5 = ((bf16[32,32,256]{2,1,0:T(8,128)(2,1)}), bf16[32,32,256]{2,1,0:T(8,128)(2,1)}, u32[]{:S(2)}, u32[]{:S(2)}) async-start(bf16[32,32,256]{2,1,0:T(8,128)(2,1)} %copy.335), calls=%async_computation.5 | async-start | bytes 1048576 | tf_op jit(solution)/shard_map/all_to_all | solution.py:219
  231.0 17.8 %all-to-all-done.5 = bf16[32,32,256]{2,1,0:T(8,128)(2,1)} async-done(((bf16[32,32,256]{2,1,0:T(8,128)(2,1)}), bf16[32,32,256]{2,1,0:T(8,128)(2,1)}, u32[]{:S(2)}, u32[]{:S(2)}) %all-to-all-start.5) | async-done | bytes 524320 | tf_op jit(solution)/shard_map/all_to_all | solution.py:219
  249.9 2.2 gather_fusion
  252.1 1.3 fusion.67
  253.4 8.6 %all_to_all.60 = bf16[8,8,256]{2,1,0:T(8,128)(2,1)S(1)} all-to-all(bf16[8,8,256]{2,1,0:T(8,128)(2,1)S(1)} %bitcast.219), channel_id=1, replica_groups=mesh['dp'=32,'tensor'=8] {'tensor'}, dimensions={0} | all-to-all | bytes 65536 | tf_op jit(solution)/shard_map/all_to_all | solution.py:229
  (144 shorter events, 19.4 us)
Async XLA Ops:
  7.2 80.3 %copy-start = (bf16[512,2048]{1,0:T(8,128)(2,1)S(1)}, bf16[512,2048]{1,0:T(8,128)(2,1)}, u32[]{:S(2)}) copy-start(bf16[512,2048]{1,0:T(8,128)(2,1)} %param.24) | copy-start | bytes 6291460
  20.7 4.9 %copy-start.14 = (f32[128]{0:T(128)S(1)}, f32[128]{0:T(128)}, u32[]{:S(2)}) copy-start(f32[128]{0:T(128)} %param.22) | copy-start | bytes 1540
  22.3 3.6 %copy-start.15 = (s32[64]{0:T(128)S(1)}, s32[64]{0:T(128)}, u32[]{:S(2)}) copy-start(s32[64]{0:T(128)} %param.35) | copy-start | bytes 772
  22.4 3.6 %copy-start.16 = (s32[2]{0:T(128)S(1)}, s32[2]{0:T(128)}, u32[]{:S(2)}) copy-start(s32[2]{0:T(128)} %param.33) | copy-start | bytes 28
  22.4 3.8 %copy-start.17 = (s32[64]{0:T(128)S(1)}, s32[64]{0:T(128)}, u32[]{:S(2)}) copy-start(s32[64]{0:T(128)} %param.34) | copy-start | bytes 772
  22.4 3.8 %copy-start.13 = (f32[128]{0:T(128)S(1)}, f32[128]{0:T(128)}, u32[]{:S(2)}) copy-start(f32[128]{0:T(128)} %param.23) | copy-start | bytes 1540
  26.4 13.7 %copy-start.9 = (bf16[64,128]{1,0:T(8,128)(2,1)}, bf16[64,128]{1,0:T(8,128)(2,1)S(1)}, u32[]{:S(2)}) copy-start(bf16[64,128]{1,0:T(8,128)(2,1)S(1)} %get-tuple-element.25) | copy-start | bytes 49156
  41.2 13.2 %copy-start.6 = (f32[64,4,1,8]{0,3,1,2:T(8,128)}, f32[64,4,1,8]{0,3,1,2:T(8,128)S(1)}, u32[]{:S(2)}) copy-start(f32[64,4,1,8]{0,3,1,2:T(8,128)S(1)} %copy.340) | copy-start | bytes 24580
  56.4 4.4 %copy-start.1 = (f32[4,64,8,2,256]{4,2,3,1,0:T(8,128)S(1)}, f32[4,64,8,2,256]{4,2,3,1,0:T(8,128)}, u32[]{:S(2)}) copy-start(f32[4,64,8,2,256]{4,2,3,1,0:T(8,128)} %get-tuple-element.32) | copy-start | bytes 12582916
  60.8 4.6 %copy-start.2 = (f32[64,4,8,16]{3,2,1,0:T(8,128)S(1)}, f32[64,4,8,16]{3,2,1,0:T(8,128)}, u32[]{:S(2)}) copy-start(f32[64,4,8,16]{3,2,1,0:T(8,128)} %get-tuple-element.34) | copy-start | bytes 393220
  65.4 1.2 copy-start.3
  65.4 1.2 copy-start.5
  66.7 2.3 copy-start.4
  66.7 2.4 copy-start.7
  68.9 6.2 %copy-start.11 = (s32[64,8]{0,1:T(8,128)S(1)}, s32[64,8]{0,1:T(8,128)}, u32[]{:S(2)}) copy-start(s32[64,8]{0,1:T(8,128)} %param.29) | copy-start | bytes 6148
  70.8 14.7 %all-to-all-start = ((bf16[8,262,128]{2,1,0:T(8,128)(2,1)}), bf16[8,262,128]{2,1,0:T(8,128)(2,1)}, u32[]{:S(2)}, u32[]{:S(2)}) async-start(bf16[8,262,128]{2,1,0:T(8,128)(2,1)} %copy.320), calls=%async_computation | async-start | bytes 1081344 | tf_op jit(solution)/shard_map/all_to_all | solution.py:161
  87.3 12.3 %copy-start.8 = (bf16[8,2048]{1,0:T(8,128)(2,1)S(1)}, bf16[8,2048]{1,0:T(8,128)(2,1)}, u32[]{:S(2)}) copy-start(bf16[8,2048]{1,0:T(8,128)(2,1)} %param.18) | copy-start | bytes 98308
  87.3 12.4 %copy-start.12 = (f32[2048]{0:T(1024)S(1)}, f32[2048]{0:T(1024)}, u32[]{:S(2)}) copy-start(f32[2048]{0:T(1024)} %param.25) | copy-start | bytes 24580
  88.6 10.8 %all-to-all-start.1 = ((bf16[8,8,2048]{2,1,0:T(8,128)(2,1)}), bf16[8,8,2048]{2,1,0:T(8,128)(2,1)S(1)}, u32[]{:S(2)}, u32[]{:S(2)}) async-start(bf16[8,8,2048]{2,1,0:T(8,128)(2,1)} %fusion.9), calls=%async_computation.1 | async-start | bytes 524288 | tf_op jit(solution)/shard_map/all_to_all | solution.py:177
  100.4 8.7 %all-to-all-start.2 = ((bf16[8,8,256]{2,0,1:T(8,128)(2,1)}), bf16[8,8,256]{2,0,1:T(8,128)(2,1)S(1)}, u32[]{:S(2)}, u32[]{:S(2)}) async-start(bf16[8,8,256]{2,0,1:T(8,128)(2,1)} %bitcast.33), calls=%async_computation.2 | async-start | bytes 65536 | tf_op jit(solution)/shard_map/all_to_all | solution.py:187
  103.7 82.2 %all-gather.4.cloned.1.call-start = ((), (), s32[]{:S(2)}) async-start(), calls=%async_computation.7 | async-start | bytes 4718592 | tf_op jit(solution)/shard_map/all_gather | solution.py:203
  138.3 78.2 %all-gather.6.cloned.1.call-start = ((), (), s32[]{:S(2)}) async-start(), calls=%async_computation.8 | async-start | bytes 2359296 | tf_op jit(solution)/shard_map/all_gather | solution.py:215
  186.0 4.1 %copy-start.18 = (bf16[32,32,2048]{2,1,0:T(8,128)(2,1)S(1)}, bf16[32,32,2048]{2,1,0:T(8,128)(2,1)}, u32[]{:S(2)}) copy-start(bf16[32,32,2048]{2,1,0:T(8,128)(2,1)} %all-gather.4.cloned.1.call-done) | copy-start | bytes 12582916
  186.0 4.4 %copy-start.19 = (bf16[4,2048,96]{1,2,0:T(8,128)(2,1)S(1)}, bf16[4,2048,96]{1,2,0:T(8,128)(2,1)}, u32[]{:S(2)}) copy-start(bf16[4,2048,96]{1,2,0:T(8,128)(2,1)} %param.27) | copy-start | bytes 4718596
  219.4 11.4 %copy-start.10 = (f32[64,8]{0,1:T(8,128)S(1)}, f32[64,8]{0,1:T(8,128)}, u32[]{:S(2)}) copy-start(f32[64,8]{0,1:T(8,128)} %param.30) | copy-start | bytes 6148
  220.5 28.2 %all-to-all-start.5 = ((bf16[32,32,256]{2,1,0:T(8,128)(2,1)}), bf16[32,32,256]{2,1,0:T(8,128)(2,1)}, u32[]{:S(2)}, u32[]{:S(2)}) async-start(bf16[32,32,256]{2,1,0:T(8,128)(2,1)} %copy.335), calls=%async_computation.5 | async-start | bytes 1048576 | tf_op jit(solution)/shard_map/all_to_all | solution.py:219
Sparse Core Ops, SparseCore 0:
  138.4 47.4 all-gather.3
  192.5 23.9 all-gather.5

commit v10 on v8

--- a/solution.py
+++ b/solution.py
@@ -62,7 +62,13 @@
     groups_dev = prefix_cache.shape[0]
     pre_local = prefix_cache.shape[1]
     suf_local = suffix_cache.shape[1]
-    residual_all = lax.all_gather(residual_in, "tensor", axis=0, tiled=True)
+    residual_all = lax.all_to_all(
+        jnp.broadcast_to(residual_in[None], (tensor_size,) + residual_in.shape),
+        "tensor",
+        0,
+        0,
+        tiled=True,
+    ).reshape(-1, residual_in.shape[1])
     piece = rms_scale(residual_all.astype(jnp.float32), attn_gain).astype(jnp.bfloat16)
     projected = jnp.concatenate(
         [
@@ -83,9 +89,9 @@
     keyed = rotate(rms_scale(kv_raw, key_gain), positions)
     new_rows = jnp.where(is_key, keyed, kv_raw).astype(jnp.bfloat16).reshape(requests, kv_cols)
     joined = jnp.concatenate([queries.reshape(requests, query_cols), new_rows], axis=1)
-    every_head = lax.all_gather(joined, "tensor", axis=1, tiled=True).reshape(
-        requests, tensor_size, query_cols + kv_cols
-    )
+    every_head = lax.all_to_all(
+        jnp.broadcast_to(joined[None], (tensor_size,) + joined.shape), "tensor", 0, 0, tiled=True
+    ).transpose(1, 0, 2)
     all_queries = every_head[:, :, :query_cols].reshape(requests, kv_heads_all, per_group, head_dim)
     all_kv = every_head[:, :, query_cols:]
     own_keys = all_kv[:, :kv_heads_all]

time: 268 us -> 266 us (level)
  blocking collectives: 98.2 us -> 71.3 us
  starting transfers between devices: 21.3 us -> 30.4 us
  local copies, waits for them, and re-layouts: 20.5 us -> 27.3 us
  waiting for transfers between devices: 71.8 us -> 77.1 us
    all_gather x2 -> x0, blocking collectives: 26.9 us -> none  [the longest x1 13.5 us: body(): residual_all = lax.all_gather(residual_in, 'tensor', axis=0, tiled=True)]
    all_to_all x0 -> x2, starting transfers between devices: none -> 9.11 us  [the longest x1 4.81 us: body(): lax.all_to_all(jnp.broadcast_to(joined[None], (tensor_size,) + joined.sha...]
    all_to_all x0 -> x2, waiting for transfers between devices: none -> 4.8 us  [the longest x1 4.79 us: body(): lax.all_to_all(jnp.broadcast_to(joined[None], (tensor_size,) + joined.sha...]
    dot_general x0 -> x1, local copies, waits for them, and re-layouts: none -> 3.95 us  [body(): jnp.dot(piece, query_weight, preferred_element_type=jnp.float32)]
    unnamed x47 -> x50, local copies, waits for them, and re-layouts: 8.93 us -> 9.2 us
  transfers between devices with their start and end apart: 6 -> 8, of which waited for: 6 -> 7; matrix products, arithmetic and copies ran while one was open for 2% -> 7% of each run, Pallas kernels for 0% -> 0%
where the time goes in v10:
time: 266 us; the launch traced here: 265 us
  waiting for transfers between devices  77.1 us (29%)
  blocking collectives  71.3 us (27%)
  starting transfers between devices  30.4 us (11%)
  local copies, waits for them, and re-layouts  27.3 us (10%)
  matrix products  26.7 us (10%)
  other arithmetic  17 us (6%)
  between operations  14.7 us (6%)
    all_to_all x1, blocking collectives, body(): down_cols = lax.all_to_all(down_split, 'tensor', 0, 0, tiled=True)  33.9 us
    all_gather x1, waiting for transfers between devices, body(): lax.all_gather(arrived, 'tensor', axis=2, tiled=True)  32.4 us
    all_to_all x1, blocking collectives, body(): lax.all_to_all(outgoing, 'dp', split_axis=0, concat_axis=0, tiled=True)  28.8 us
    all_to_all x1, waiting for transfers between devices, body(): lax.all_to_all(summed_out.reshape(owners, local_experts * capacity, width...  17.8 us
    all_to_all x1, starting transfers between devices, body(): lax.all_to_all(summed_out.reshape(owners, local_experts * capacity, width...  10.1 us
    all_to_all x1, waiting for transfers between devices, body(): lax.all_to_all(packed, 'tensor', 0, 0, tiled=True).astype(jnp.float32)  9.87 us
    unnamed x50, local copies, waits for them, and re-layouts  9.2 us
    all_to_all x1, blocking collectives, body(): lax.all_to_all(moe_cols, 'tensor', split_axis=0, concat_axis=1, tiled=True)  8.63 us
  transfers between devices with their start and end apart: 8, of which 7 were waited for; matrix products, arithmetic and copies ran while one was open for 7% of the time, Pallas kernels for 0%

profile of v10, /device:TPU:32, one launch (start us, length us, event | category | flops | bytes accessed | tf_op | source)
XLA Modules:
  0.0 264.5 jit_solution(12099427573284592728)
XLA Ops:
  7.2 1.6 broadcast_in_dim.70
  8.8 4.3 %all-to-all-start = ((bf16[8,8,2048]{2,1,0:T(8,128)(2,1)}), bf16[8,8,2048]{2,1,0:T(8,128)(2,1)S(1)}, u32[]{:S(2)}, u32[]{:S(2)}) async-start(bf16[8,8,2048]{2,1,0:T(8,128)(2,1)} %broadcast_in_dim.70), calls=%async_computation | async-start | bytes 524288 | tf_op jit(solution)/shard_map/all_to_all | solution.py:65
  15.5 2.1 fusion.112
  17.7 4.0 %copy.234 = bf16[512,2048]{1,0:T(8,128)(2,1)} copy(bf16[512,2048]{0,1:T(8,128)(2,1)} %bitcast.228) | data formatting | bytes 4194304 | tf_op jit(solution)/shard_map/dot_general | solution.py:75
  23.6 2.5 multiply_reduce_fusion
  28.1 4.8 %all-to-all-start.1 = ((bf16[8,64,640]{2,1,0:T(8,128)(2,1)}), bf16[8,64,640]{2,1,0:T(8,128)(2,1)S(1)}, u32[]{:S(2)}, u32[]{:S(2)}) async-start(bf16[8,64,640]{2,1,0:T(8,128)(2,1)} %broadcast_in_dim.74), calls=%async_computation.1 | async-start | bytes 1310720 | tf_op jit(solution)/shard_map/all_to_all | solution.py:92
  33.0 2.0 copy.244
  36.5 3.3 %slice_bitcast_fusion = (bf16[64,2,4,8,128]{4,3,2,1,0:T(8,128)(2,1)}, bf16[64,2,4,8,128]{4,3,2,1,0:T(8,128)(2,1)}) fusion(bf16[64,16,1024]{2,1,0:T(8,128)(2,1)} %param.32), kind=kLoop, calls=%fused_computation.46 | loop fusion | bytes 4194304
  39.8 4.8 %all-to-all-done.1 = bf16[8,64,640]{2,1,0:T(8,128)(2,1)S(1)} async-done(((bf16[8,64,640]{2,1,0:T(8,128)(2,1)}), bf16[8,64,640]{2,1,0:T(8,128)(2,1)S(1)}, u32[]{:S(2)}, u32[]{:S(2)}) %all-to-all-start.1) | async-done | bytes 655392 | tf_op jit(solution)/shard_map/all_to_all | solution.py:92
  46.4 4.0 %fusion = (bf16[64,4,8]{2,0,1:T(8,128)(2,1)S(1)}, f32[4,64,8,2,256]{4,2,3,1,0:T(8,128)}) fusion(pred[64,2,256]{2,1,0:T(4,128)(4,1)S(1)} %broadcast_and_fusion, bf16[2,256,4,128,1]{1,3,2,0,4:T(8,128)(2,1)} %bitcast.232, bf16[64,4,8,128]{3,2,1,0:T(8,128)(2,1)S(1)} %reshape.385), kind=kOutput, calls=%fused_computation.3 | convolution fusion | flops 271579136 | bytes 5279744 | tf_op jit(solution)/shard_map/rgqd,npgd->rgqnp/dot_general | solution.py:108
  50.5 2.9 %select_reduce_fusion = (bf16[64,4,8]{2,1,0:T(4,128)(2,1)S(1)}, f32[64,4,8,16]{3,2,1,0:T(8,128)}) fusion(pred[64,16]{1,0:T(8,128)(4,1)S(1)} %broadcast_compare_fusion, bf16[64,4,8,128]{3,2,1,0:T(8,128)(2,1)S(1)} %reshape.385, bf16[64,2,4,8,128]{4,3,2,1,0:T(8,128)(2,1)} %get-tuple-element.11), kind=kOutput, calls=%fused_computation.48 | convolution fusion | flops 8484864 | bytes 1709056 | tf_op jit(solution)/shard_map/rgqd,rsgd->rgqs/dot_general | solution.py:112
  54.5 4.4 %fusion.7 = f32[64,4,8]{2,0,1:T(8,128)} fusion(f32[4,64,8,2,256]{4,2,3,1,0:T(8,128)} %get-tuple-element.30, f32[64,4,8]{2,0,1:T(8,128)S(1)} %copy.187, pred[64,2,256]{2,1,0:T(4,128)(4,1)S(1)} %broadcast_and_fusion), kind=kLoop, calls=%fused_computation.10 | loop fusion | flops 4192256 | bytes 4243456 | tf_op jit(solution)/shard_map/reduce_sum | solution.py:135
  58.9 3.2 %fusion.25 = f32[64,4,8,128]{3,2,0,1:T(8,128)} fusion(f32[4,64,8,2,256]{4,2,3,1,0:T(8,128)S(1)} %copy-done.1, f32[64,4,8]{2,0,1:T(8,128)} %copy-done.5, pred[64,2,256]{2,1,0:T(4,128)(4,1)S(1)} %broadcast_and_fusion, bf16[2,256,4,128,1]{1,3,2,0,4:T(8,128)(2,1)} %bitcast.237), kind=kOutput, calls=%fused_computation.28 | convolution fusion | flops 272629760 | bytes 5808128 | tf_op jit(solution)/shard_map/rgqnp,npgd->rgqd/dot_general | solution.py:136
  62.9 1.7 fusion.62
  64.6 1.8 fusion.32
  68.8 4.4 %all-to-all-start.2 = ((bf16[8,262,128]{2,1,0:T(8,128)(2,1)}), bf16[8,262,128]{2,1,0:T(8,128)(2,1)}, u32[]{:S(2)}, u32[]{:S(2)}) async-start(bf16[8,262,128]{2,1,0:T(8,128)(2,1)} %copy.204), calls=%async_computation.2 | async-start | bytes 1081344 | tf_op jit(solution)/shard_map/all_to_all | solution.py:167
  73.6 9.9 %all-to-all-done.2 = bf16[8,262,128]{2,1,0:T(8,128)(2,1)} async-done(((bf16[8,262,128]{2,1,0:T(8,128)(2,1)}), bf16[8,262,128]{2,1,0:T(8,128)(2,1)}, u32[]{:S(2)}, u32[]{:S(2)}) %all-to-all-start.2) | async-done | bytes 536608 | tf_op jit(solution)/shard_map/all_to_all | solution.py:167
  86.6 3.4 %all-to-all-start.3 = ((bf16[8,8,2048]{2,1,0:T(8,128)(2,1)}), bf16[8,8,2048]{2,1,0:T(8,128)(2,1)S(1)}, u32[]{:S(2)}, u32[]{:S(2)}) async-start(bf16[8,8,2048]{2,1,0:T(8,128)(2,1)} %fusion.9), calls=%async_computation.3 | async-start | bytes 524288 | tf_op jit(solution)/shard_map/all_to_all | solution.py:183
  90.3 7.2 %all-to-all-done.3 = bf16[8,8,2048]{2,1,0:T(8,128)(2,1)S(1)} async-done(((bf16[8,8,2048]{2,1,0:T(8,128)(2,1)}), bf16[8,8,2048]{2,1,0:T(8,128)(2,1)S(1)}, u32[]{:S(2)}, u32[]{:S(2)}) %all-to-all-start.3) | async-done | bytes 262176 | tf_op jit(solution)/shard_map/all_to_all | solution.py:183
  98.4 3.3 %all-to-all-start.4 = ((bf16[8,8,256]{2,0,1:T(8,128)(2,1)}), bf16[8,8,256]{2,0,1:T(8,128)(2,1)S(1)}, u32[]{:S(2)}, u32[]{:S(2)}) async-start(bf16[8,8,256]{2,0,1:T(8,128)(2,1)} %bitcast.38), calls=%async_computation.4 | async-start | bytes 65536 | tf_op jit(solution)/shard_map/all_to_all | solution.py:193
  102.5 4.6 %all-to-all-done.4 = bf16[8,8,256]{2,0,1:T(8,128)(2,1)S(1)} async-done(((bf16[8,8,256]{2,0,1:T(8,128)(2,1)}), bf16[8,8,256]{2,0,1:T(8,128)(2,1)S(1)}, u32[]{:S(2)}, u32[]{:S(2)}) %all-to-all-start.4) | async-done | bytes 32800 | tf_op jit(solution)/shard_map/all_to_all | solution.py:193
  107.5 28.8 %all_to_all.68 = bf16[32,32,256]{2,1,0:T(8,128)(2,1)} all-to-all(bf16[32,32,256]{2,1,0:T(8,128)(2,1)S(1)} %bitcast.230), channel_id=1, replica_groups=mesh['dp'=32,'tensor'=8] {'dp'}, dimensions={0} | all-to-all | bytes 1048576 | tf_op jit(solution)/shard_map/all_to_all | solution.py:208
  136.3 32.4 %all-gather.4.cloned.1.call-done = bf16[32,32,2048]{2,1,0:T(8,128)(2,1)} async-done(((bf16[32,32,256]{2,1,0:T(8,128)(2,1)}), bf16[32,32,2048]{2,1,0:T(8,128)(2,1)}) %all-gather.4.cloned.1.call-update) | async-done | bytes 4194320 | tf_op jit(solution)/shard_map/all_gather | solution.py:209
  168.7 4.1 %fusion.36 = f32[32,4,8,96]{3,2,0,1:T(8,128)S(1)} fusion(bf16[4,2048,96]{1,2,0:T(8,128)(2,1)} %param.26, bf16[32,32,2048]{2,1,0:T(8,128)(2,1)} %all-gather.4.cloned.1.call-done), kind=kOutput, calls=%fused_computation.36 | convolution fusion | flops 402653184 | bytes 6160384 | tf_op jit(solution)/shard_map/necd,edf->necf/dot_general | solution.py:212
  173.1 2.0 fusion.51
  175.1 1.9 copy.250
  177.5 33.9 %all_to_all.69 = bf16[8,4,96,256]{3,2,1,0:T(8,128)(2,1)} all-to-all(bf16[8,4,96,256]{3,2,1,0:T(8,128)(2,1)S(1)} %copy.216), channel_id=1, replica_groups=mesh['dp'=32,'tensor'=8] {'tensor'}, dimensions={0} | all-to-all | bytes 3145728 | tf_op jit(solution)/shard_map/all_to_all | solution.py:220
  211.9 2.8 %fusion.33 = bf16[32,4,8,256]{3,2,0,1:T(8,128)(2,1)S(1)} fusion(bf16[8,32,4,8,96]{4,3,1,0,2:T(8,128)(2,1)} %bitcast.248, bf16[8,4,96,256]{3,2,1,0:T(8,128)(2,1)} %all_to_all.69), kind=kOutput, calls=%fused_computation.35 | convolution fusion | flops 402915328 | bytes 3670016 | tf_op jit(solution)/shard_map/tnecf,tefd->necd/dot_general | solution.py:221
  215.6 10.1 %all-to-all-start.7 = ((bf16[32,32,256]{2,1,0:T(8,128)(2,1)}), bf16[32,32,256]{2,1,0:T(8,128)(2,1)}, u32[]{:S(2)}, u32[]{:S(2)}) async-start(bf16[32,32,256]{2,1,0:T(8,128)(2,1)} %bitcast.219), calls=%async_computation.7 | async-start | bytes 1048576 | tf_op jit(solution)/shard_map/all_to_all | solution.py:224
  226.1 17.8 %all-to-all-done.7 = bf16[32,32,256]{2,1,0:T(8,128)(2,1)} async-done(((bf16[32,32,256]{2,1,0:T(8,128)(2,1)}), bf16[32,32,256]{2,1,0:T(8,128)(2,1)}, u32[]{:S(2)}, u32[]{:S(2)}) %all-to-all-start.7) | async-done | bytes 524320 | tf_op jit(solution)/shard_map/all_to_all | solution.py:224
  244.9 2.2 gather_fusion
  248.4 8.6 %all_to_all.70 = bf16[8,8,256]{2,1,0:T(8,128)(2,1)S(1)} all-to-all(bf16[8,8,256]{2,1,0:T(8,128)(2,1)S(1)} %bitcast.243), channel_id=1, replica_groups=mesh['dp'=32,'tensor'=8] {'tensor'}, dimensions={0} | all-to-all | bytes 65536 | tf_op jit(solution)/shard_map/all_to_all | solution.py:234
  (147 shorter events, 25.1 us)
Async XLA Ops:
  7.2 78.3 %copy-start = (bf16[512,2048]{1,0:T(8,128)(2,1)S(1)}, bf16[512,2048]{1,0:T(8,128)(2,1)}, u32[]{:S(2)}) copy-start(bf16[512,2048]{1,0:T(8,128)(2,1)} %param.24) | copy-start | bytes 6291460
  7.2 10.4 %copy-start.19 = (s32[64]{0:T(128)S(1)}, s32[64]{0:T(128)}, u32[]{:S(2)}) copy-start(s32[64]{0:T(128)} %param.34) | copy-start | bytes 772
  8.8 13.0 %all-to-all-start = ((bf16[8,8,2048]{2,1,0:T(8,128)(2,1)}), bf16[8,8,2048]{2,1,0:T(8,128)(2,1)S(1)}, u32[]{:S(2)}, u32[]{:S(2)}) async-start(bf16[8,8,2048]{2,1,0:T(8,128)(2,1)} %broadcast_in_dim.70), calls=%async_computation | async-start | bytes 524288 | tf_op jit(solution)/shard_map/all_to_all | solution.py:65
  17.7 4.4 %copy-start.15 = (f32[2048]{0:T(1024)S(1)}, f32[2048]{0:T(1024)}, u32[]{:S(2)}) copy-start(f32[2048]{0:T(1024)} %param.19) | copy-start | bytes 24580
  17.7 5.8 %copy-start.17 = (f32[128]{0:T(128)S(1)}, f32[128]{0:T(128)}, u32[]{:S(2)}) copy-start(f32[128]{0:T(128)} %param.23) | copy-start | bytes 1540
  21.6 4.5 %copy-start.18 = (f32[128]{0:T(128)S(1)}, f32[128]{0:T(128)}, u32[]{:S(2)}) copy-start(f32[128]{0:T(128)} %param.22) | copy-start | bytes 1540
  26.5 0.6 copy-start.11
  27.2 8.9 %copy-start.13 = (s32[64,8]{0,1:T(8,128)S(1)}, s32[64,8]{0,1:T(8,128)}, u32[]{:S(2)}) copy-start(s32[64,8]{0,1:T(8,128)} %param.29) | copy-start | bytes 6148
  28.1 16.5 %all-to-all-start.1 = ((bf16[8,64,640]{2,1,0:T(8,128)(2,1)}), bf16[8,64,640]{2,1,0:T(8,128)(2,1)S(1)}, u32[]{:S(2)}, u32[]{:S(2)}) async-start(bf16[8,64,640]{2,1,0:T(8,128)(2,1)} %broadcast_in_dim.74), calls=%async_computation.1 | async-start | bytes 1310720 | tf_op jit(solution)/shard_map/all_to_all | solution.py:92
  36.1 3.7 %copy-start.6 = (s32[64,8]{1,0:T(8,128)}, s32[64,8]{1,0:T(8,128)S(1)}, u32[]{:S(2)}) copy-start(s32[64,8]{1,0:T(8,128)S(1)} %copy.208) | copy-start | bytes 6148
  46.4 7.1 %copy-start.8 = (f32[64,4,1,8]{0,3,1,2:T(8,128)}, f32[64,4,1,8]{0,3,1,2:T(8,128)S(1)}, u32[]{:S(2)}) copy-start(f32[64,4,1,8]{0,3,1,2:T(8,128)S(1)} %copy.224) | copy-start | bytes 24580
  53.7 5.2 %copy-start.5 = (f32[64,4,8]{2,0,1:T(8,128)}, f32[64,4,8]{2,0,1:T(8,128)S(1)}, u32[]{:S(2)}) copy-start(f32[64,4,8]{2,0,1:T(8,128)S(1)} %copy.187) | copy-start | bytes 24580
  54.5 4.5 %copy-start.1 = (f32[4,64,8,2,256]{4,2,3,1,0:T(8,128)S(1)}, f32[4,64,8,2,256]{4,2,3,1,0:T(8,128)}, u32[]{:S(2)}) copy-start(f32[4,64,8,2,256]{4,2,3,1,0:T(8,128)} %get-tuple-element.30) | copy-start | bytes 12582916
  58.9 4.0 %copy-start.2 = (f32[64,4,8,16]{3,2,1,0:T(8,128)S(1)}, f32[64,4,8,16]{3,2,1,0:T(8,128)}, u32[]{:S(2)}) copy-start(f32[64,4,8,16]{3,2,1,0:T(8,128)} %get-tuple-element.32) | copy-start | bytes 393220
  62.9 1.7 copy-start.3
  64.6 2.4 copy-start.4
  64.6 2.5 copy-start.9
  66.9 6.3 %copy-start.7 = (s32[64,8]{1,0:T(8,128)S(1)}, s32[64,8]{1,0:T(8,128)}, u32[]{:S(2)}) copy-start(s32[64,8]{1,0:T(8,128)} %copy-done.6) | copy-start | bytes 6148
  68.8 14.7 %all-to-all-start.2 = ((bf16[8,262,128]{2,1,0:T(8,128)(2,1)}), bf16[8,262,128]{2,1,0:T(8,128)(2,1)}, u32[]{:S(2)}, u32[]{:S(2)}) async-start(bf16[8,262,128]{2,1,0:T(8,128)(2,1)} %copy.204), calls=%async_computation.2 | async-start | bytes 1081344 | tf_op jit(solution)/shard_map/all_to_all | solution.py:167
  85.3 5.0 %copy-start.14 = (s32[64,8]{0,1:T(8,128)S(1)}, s32[64,8]{0,1:T(8,128)}, u32[]{:S(2)}) copy-start(s32[64,8]{0,1:T(8,128)} %param.29) | copy-start | bytes 6148
  85.3 12.3 %copy-start.10 = (bf16[8,2048]{1,0:T(8,128)(2,1)S(1)}, bf16[8,2048]{1,0:T(8,128)(2,1)}, u32[]{:S(2)}) copy-start(bf16[8,2048]{1,0:T(8,128)(2,1)} %param.18) | copy-start | bytes 98308
  85.3 12.4 %copy-start.16 = (f32[2048]{0:T(1024)S(1)}, f32[2048]{0:T(1024)}, u32[]{:S(2)}) copy-start(f32[2048]{0:T(1024)} %param.25) | copy-start | bytes 24580
  86.6 10.8 %all-to-all-start.3 = ((bf16[8,8,2048]{2,1,0:T(8,128)(2,1)}), bf16[8,8,2048]{2,1,0:T(8,128)(2,1)S(1)}, u32[]{:S(2)}, u32[]{:S(2)}) async-start(bf16[8,8,2048]{2,1,0:T(8,128)(2,1)} %fusion.9), calls=%async_computation.3 | async-start | bytes 524288 | tf_op jit(solution)/shard_map/all_to_all | solution.py:183
  98.4 8.7 %all-to-all-start.4 = ((bf16[8,8,256]{2,0,1:T(8,128)(2,1)}), bf16[8,8,256]{2,0,1:T(8,128)(2,1)S(1)}, u32[]{:S(2)}, u32[]{:S(2)}) async-start(bf16[8,8,256]{2,0,1:T(8,128)(2,1)} %bitcast.38), calls=%async_computation.4 | async-start | bytes 65536 | tf_op jit(solution)/shard_map/all_to_all | solution.py:193
  101.7 67.0 %all-gather.4.cloned.1.call-start = ((), (), s32[]{:S(2)}) async-start(), calls=%async_computation.9 | async-start | bytes 4718592 | tf_op jit(solution)/shard_map/all_gather | solution.py:209
  136.3 75.6 %all-gather.6.cloned.1.call-start = ((), (), s32[]{:S(2)}) async-start(), calls=%async_computation.10 | async-start | bytes 2359296 | tf_op jit(solution)/shard_map/all_gather | solution.py:215
  168.7 4.1 %copy-start.20 = (bf16[32,32,2048]{2,1,0:T(8,128)(2,1)S(1)}, bf16[32,32,2048]{2,1,0:T(8,128)(2,1)}, u32[]{:S(2)}) copy-start(bf16[32,32,2048]{2,1,0:T(8,128)(2,1)} %all-gather.4.cloned.1.call-done) | copy-start | bytes 12582916
  168.7 4.4 %copy-start.21 = (bf16[4,2048,96]{1,2,0:T(8,128)(2,1)S(1)}, bf16[4,2048,96]{1,2,0:T(8,128)(2,1)}, u32[]{:S(2)}) copy-start(bf16[4,2048,96]{1,2,0:T(8,128)(2,1)} %param.27) | copy-start | bytes 4718596
  214.7 11.2 %copy-start.12 = (f32[64,8]{0,1:T(8,128)S(1)}, f32[64,8]{0,1:T(8,128)}, u32[]{:S(2)}) copy-start(f32[64,8]{0,1:T(8,128)} %param.30) | copy-start | bytes 6148
  215.6 28.2 %all-to-all-start.7 = ((bf16[32,32,256]{2,1,0:T(8,128)(2,1)}), bf16[32,32,256]{2,1,0:T(8,128)(2,1)}, u32[]{:S(2)}, u32[]{:S(2)}) async-start(bf16[32,32,256]{2,1,0:T(8,128)(2,1)} %bitcast.219), calls=%async_computation.7 | async-start | bytes 1048576 | tf_op jit(solution)/shard_map/all_to_all | solution.py:224
Sparse Core Ops, SparseCore 0:
  136.4 32.2 all-gather.3
  175.2 36.5 all-gather.5

commit v11 on v10

--- a/solution.py
+++ b/solution.py
@@ -209,15 +209,19 @@
     rows = lax.all_gather(arrived, "tensor", axis=2, tiled=True).reshape(
         owners, local_experts, capacity, model_width
     )
+    ff_here = down_weight.shape[1]
+    down_split = down_weight.reshape(local_experts, ff_here, tensor_size, width_here).transpose(
+        2, 0, 1, 3
+    )
+    half_experts = local_experts // 2
+    down_first = lax.all_to_all(down_split[:, :half_experts], "tensor", 0, 0, tiled=True)
+    rows, down_first = lax.optimization_barrier((rows, down_first))
     gate_val = jnp.einsum("necd,edf->necf", rows, gate_weight, preferred_element_type=jnp.float32)
     lift_val = jnp.einsum("necd,edf->necf", rows, lift_weight, preferred_element_type=jnp.float32)
     hidden_units = (jax.nn.silu(gate_val) * lift_val).astype(jnp.bfloat16)
     hidden_all = lax.all_gather(hidden_units, "tensor", axis=0)
-    ff_here = down_weight.shape[1]
-    down_split = down_weight.reshape(local_experts, ff_here, tensor_size, width_here).transpose(
-        2, 0, 1, 3
-    )
-    down_cols = lax.all_to_all(down_split, "tensor", 0, 0, tiled=True)
+    down_second = lax.all_to_all(down_split[:, half_experts:], "tensor", 0, 0, tiled=True)
+    down_cols = jnp.concatenate([down_first, down_second], axis=1)
     summed_out = jnp.einsum(
         "tnecf,tefd->necd", hidden_all, down_cols, preferred_element_type=jnp.float32
     ).astype(jnp.bfloat16)

time: 266 us -> 261 us (0.981)
  waiting for transfers between devices: 77.1 us -> 65.5 us
  blocking collectives: 71.3 us -> 80.6 us
    all_gather x1, waiting for transfers between devices: 32.4 us -> 15.5 us  [body(): lax.all_gather(arrived, 'tensor', axis=2, tiled=True)]
    all_to_all x1 -> x2, blocking collectives: 33.9 us -> 43.2 us  [the longest x1 21.9 us: body(): lax.all_to_all(down_split[:, :half_experts], 'tensor', 0, 0, tiled=True)]
    all_gather x1, waiting for transfers between devices: 0.51 us -> 5.78 us  [body(): hidden_all = lax.all_gather(hidden_units, 'tensor', axis=0)]
  transfers between devices with their start and end apart: 8 -> 8, of which waited for: 7 -> 7; matrix products, arithmetic and copies ran while one was open for 7% -> 8% of each run, Pallas kernels for 0% -> 0%
where the time goes in v11:
time: 261 us; the launch traced here: 260 us
  blocking collectives  80.6 us (31%)
  waiting for transfers between devices  65.5 us (25%)
  starting transfers between devices  27.9 us (11%)
  local copies, waits for them, and re-layouts  27.6 us (11%)
  matrix products  26.5 us (10%)
  other arithmetic  17 us (7%)
  between operations  14.7 us (6%)
    all_to_all x1, blocking collectives, body(): lax.all_to_all(outgoing, 'dp', split_axis=0, concat_axis=0, tiled=True)  28.8 us
    all_to_all x1, blocking collectives, body(): lax.all_to_all(down_split[:, :half_experts], 'tensor', 0, 0, tiled=True)  21.9 us
    all_to_all x1, blocking collectives, body(): lax.all_to_all(down_split[:, half_experts:], 'tensor', 0, 0, tiled=True)  21.4 us
    all_to_all x1, waiting for transfers between devices, body(): lax.all_to_all(summed_out.reshape(owners, local_experts * capacity, width...  17.8 us
    all_gather x1, waiting for transfers between devices, body(): lax.all_gather(arrived, 'tensor', axis=2, tiled=True)  15.5 us
    all_to_all x1, waiting for transfers between devices, body(): lax.all_to_all(packed, 'tensor', 0, 0, tiled=True).astype(jnp.float32)  9.87 us
    unnamed x50, local copies, waits for them, and re-layouts  9.2 us
    all_to_all x1, blocking collectives, body(): lax.all_to_all(moe_cols, 'tensor', split_axis=0, concat_axis=1, tiled=True)  8.57 us
  transfers between devices with their start and end apart: 8, of which 7 were waited for; matrix products, arithmetic and copies ran while one was open for 8% of the time, Pallas kernels for 0%

profile of v11, /device:TPU:32, one launch (start us, length us, event | category | flops | bytes accessed | tf_op | source)
XLA Modules:
  0.0 259.8 jit_solution(1000580431855901364)
XLA Ops:
  8.8 4.3 %all-to-all-start = ((bf16[8,8,2048]{2,1,0:T(8,128)(2,1)}), bf16[8,8,2048]{2,1,0:T(8,128)(2,1)S(1)}, u32[]{:S(2)}, u32[]{:S(2)}) async-start(bf16[8,8,2048]{2,1,0:T(8,128)(2,1)} %broadcast_in_dim.70), calls=%async_computation | async-start | bytes 524288 | tf_op jit(solution)/shard_map/all_to_all | solution.py:65
  15.5 2.1 fusion.114
  17.7 4.0 %copy.241 = bf16[512,2048]{1,0:T(8,128)(2,1)} copy(bf16[512,2048]{0,1:T(8,128)(2,1)} %bitcast.206) | data formatting | bytes 4194304 | tf_op jit(solution)/shard_map/dot_general | solution.py:75
  23.6 2.5 multiply_reduce_fusion
  28.1 4.8 %all-to-all-start.1 = ((bf16[8,64,640]{2,1,0:T(8,128)(2,1)}), bf16[8,64,640]{2,1,0:T(8,128)(2,1)S(1)}, u32[]{:S(2)}, u32[]{:S(2)}) async-start(bf16[8,64,640]{2,1,0:T(8,128)(2,1)} %broadcast_in_dim.74), calls=%async_computation.1 | async-start | bytes 1310720 | tf_op jit(solution)/shard_map/all_to_all | solution.py:92
  33.0 2.0 copy.252
  36.5 3.3 %slice_bitcast_fusion = (bf16[64,2,4,8,128]{4,3,2,1,0:T(8,128)(2,1)}, bf16[64,2,4,8,128]{4,3,2,1,0:T(8,128)(2,1)}) fusion(bf16[64,16,1024]{2,1,0:T(8,128)(2,1)} %param.32), kind=kLoop, calls=%fused_computation.46 | loop fusion | bytes 4194304
  39.8 4.8 %all-to-all-done.1 = bf16[8,64,640]{2,1,0:T(8,128)(2,1)S(1)} async-done(((bf16[8,64,640]{2,1,0:T(8,128)(2,1)}), bf16[8,64,640]{2,1,0:T(8,128)(2,1)S(1)}, u32[]{:S(2)}, u32[]{:S(2)}) %all-to-all-start.1) | async-done | bytes 655392 | tf_op jit(solution)/shard_map/all_to_all | solution.py:92
  46.4 4.0 %fusion = (bf16[64,4,8]{2,0,1:T(8,128)(2,1)S(1)}, f32[4,64,8,2,256]{4,2,3,1,0:T(8,128)}) fusion(pred[64,2,256]{2,1,0:T(4,128)(4,1)S(1)} %broadcast_and_fusion, bf16[2,256,4,128,1]{1,3,2,0,4:T(8,128)(2,1)} %bitcast.210, bf16[64,4,8,128]{3,2,1,0:T(8,128)(2,1)S(1)} %reshape.385), kind=kOutput, calls=%fused_computation.3 | convolution fusion | flops 271579136 | bytes 5279744 | tf_op jit(solution)/shard_map/rgqd,npgd->rgqnp/dot_general | solution.py:108
  50.5 2.9 %select_reduce_fusion = (bf16[64,4,8]{2,1,0:T(4,128)(2,1)S(1)}, f32[64,4,8,16]{3,2,1,0:T(8,128)}) fusion(pred[64,16]{1,0:T(8,128)(4,1)S(1)} %broadcast_compare_fusion, bf16[64,4,8,128]{3,2,1,0:T(8,128)(2,1)S(1)} %reshape.385, bf16[64,2,4,8,128]{4,3,2,1,0:T(8,128)(2,1)} %get-tuple-element.15), kind=kOutput, calls=%fused_computation.48 | convolution fusion | flops 8484864 | bytes 1709056 | tf_op jit(solution)/shard_map/rgqd,rsgd->rgqs/dot_general | solution.py:112
  54.5 4.4 %fusion.7 = f32[64,4,8]{2,0,1:T(8,128)} fusion(f32[4,64,8,2,256]{4,2,3,1,0:T(8,128)} %get-tuple-element.36, f32[64,4,8]{2,0,1:T(8,128)S(1)} %copy.192, pred[64,2,256]{2,1,0:T(4,128)(4,1)S(1)} %broadcast_and_fusion), kind=kLoop, calls=%fused_computation.10 | loop fusion | flops 4192256 | bytes 4243456 | tf_op jit(solution)/shard_map/reduce_sum | solution.py:135
  58.9 3.2 %fusion.27 = f32[64,4,8,128]{3,2,0,1:T(8,128)} fusion(f32[4,64,8,2,256]{4,2,3,1,0:T(8,128)S(1)} %copy-done.1, f32[64,4,8]{2,0,1:T(8,128)} %copy-done.5, pred[64,2,256]{2,1,0:T(4,128)(4,1)S(1)} %broadcast_and_fusion, bf16[2,256,4,128,1]{1,3,2,0,4:T(8,128)(2,1)} %bitcast.215), kind=kOutput, calls=%fused_computation.29 | convolution fusion | flops 272629760 | bytes 5808128 | tf_op jit(solution)/shard_map/rgqnp,npgd->rgqd/dot_general | solution.py:136
  64.6 1.8 fusion.36
  68.8 4.4 %all-to-all-start.2 = ((bf16[8,262,128]{2,1,0:T(8,128)(2,1)}), bf16[8,262,128]{2,1,0:T(8,128)(2,1)}, u32[]{:S(2)}, u32[]{:S(2)}) async-start(bf16[8,262,128]{2,1,0:T(8,128)(2,1)} %copy.209), calls=%async_computation.2 | async-start | bytes 1081344 | tf_op jit(solution)/shard_map/all_to_all | solution.py:167
  73.6 9.9 %all-to-all-done.2 = bf16[8,262,128]{2,1,0:T(8,128)(2,1)} async-done(((bf16[8,262,128]{2,1,0:T(8,128)(2,1)}), bf16[8,262,128]{2,1,0:T(8,128)(2,1)}, u32[]{:S(2)}, u32[]{:S(2)}) %all-to-all-start.2) | async-done | bytes 536608 | tf_op jit(solution)/shard_map/all_to_all | solution.py:167
  86.6 3.4 %all-to-all-start.3 = ((bf16[8,8,2048]{2,1,0:T(8,128)(2,1)}), bf16[8,8,2048]{2,1,0:T(8,128)(2,1)S(1)}, u32[]{:S(2)}, u32[]{:S(2)}) async-start(bf16[8,8,2048]{2,1,0:T(8,128)(2,1)} %fusion.9), calls=%async_computation.3 | async-start | bytes 524288 | tf_op jit(solution)/shard_map/all_to_all | solution.py:183
  90.3 7.2 %all-to-all-done.3 = bf16[8,8,2048]{2,1,0:T(8,128)(2,1)S(1)} async-done(((bf16[8,8,2048]{2,1,0:T(8,128)(2,1)}), bf16[8,8,2048]{2,1,0:T(8,128)(2,1)S(1)}, u32[]{:S(2)}, u32[]{:S(2)}) %all-to-all-start.3) | async-done | bytes 262176 | tf_op jit(solution)/shard_map/all_to_all | solution.py:183
  98.4 3.3 %all-to-all-start.4 = ((bf16[8,8,256]{2,0,1:T(8,128)(2,1)}), bf16[8,8,256]{2,0,1:T(8,128)(2,1)S(1)}, u32[]{:S(2)}, u32[]{:S(2)}) async-start(bf16[8,8,256]{2,0,1:T(8,128)(2,1)} %bitcast.38), calls=%async_computation.4 | async-start | bytes 65536 | tf_op jit(solution)/shard_map/all_to_all | solution.py:193
  102.5 4.6 %all-to-all-done.4 = bf16[8,8,256]{2,0,1:T(8,128)(2,1)S(1)} async-done(((bf16[8,8,256]{2,0,1:T(8,128)(2,1)}), bf16[8,8,256]{2,0,1:T(8,128)(2,1)S(1)}, u32[]{:S(2)}, u32[]{:S(2)}) %all-to-all-start.4) | async-done | bytes 32800 | tf_op jit(solution)/shard_map/all_to_all | solution.py:193
  107.5 28.8 %all_to_all.73 = bf16[32,32,256]{2,1,0:T(8,128)(2,1)} all-to-all(bf16[32,32,256]{2,1,0:T(8,128)(2,1)S(1)} %bitcast.208), channel_id=1, replica_groups=mesh['dp'=32,'tensor'=8] {'dp'}, dimensions={0} | all-to-all | bytes 1048576 | tf_op jit(solution)/shard_map/all_to_all | solution.py:208
  136.3 1.9 copy.258
  138.6 21.9 %all_to_all.74 = bf16[8,2,96,256]{3,2,1,0:T(8,128)(2,1)} all-to-all(bf16[8,2,96,256]{3,2,1,0:T(8,128)(2,1)S(1)} %copy.219), channel_id=1, replica_groups=mesh['dp'=32,'tensor'=8] {'tensor'}, dimensions={0} | all-to-all | bytes 1572864 | tf_op jit(solution)/shard_map/all_to_all | solution.py:217
  160.5 15.5 %all-gather.4.cloned.1.call-done = bf16[32,32,2048]{2,1,0:T(8,128)(2,1)} async-done(((bf16[32,32,256]{2,1,0:T(8,128)(2,1)}), bf16[32,32,2048]{2,1,0:T(8,128)(2,1)}) %all-gather.4.cloned.1.call-update) | async-done | bytes 4194320 | tf_op jit(solution)/shard_map/all_gather | solution.py:209
  176.0 4.1 %fusion.37 = f32[32,4,8,96]{3,2,0,1:T(8,128)S(1)} fusion(bf16[4,2048,96]{1,2,0:T(8,128)(2,1)} %param.26, bf16[32,4,8,2048]{3,2,1,0:T(8,128)(2,1)} %bitcast.227), kind=kOutput, calls=%fused_computation.36 | convolution fusion | flops 402653184 | bytes 6160384 | tf_op jit(solution)/shard_map/necd,edf->necf/dot_general | solution.py:219
  180.4 2.0 fusion.52
  182.5 21.4 %all_to_all.75 = bf16[8,2,96,256]{3,2,1,0:T(8,128)(2,1)S(1)} all-to-all(bf16[8,2,96,256]{3,2,1,0:T(8,128)(2,1)S(1)} %copy.220), channel_id=1, replica_groups=mesh['dp'=32,'tensor'=8] {'tensor'}, dimensions={0} | all-to-all | bytes 1572864 | tf_op jit(solution)/shard_map/all_to_all | solution.py:223
  203.9 5.8 %all-gather.6.cloned.1.call-done = bf16[256,4,8,96]{3,2,0,1:T(8,128)(2,1)} async-done(((bf16[32,4,8,96]{3,2,0,1:T(8,128)(2,1)}), bf16[256,4,8,96]{3,2,0,1:T(8,128)(2,1)}) %all-gather.6.cloned.1.call-update) | async-done | bytes 1572880 | tf_op jit(solution)/shard_map/all_gather | solution.py:222
  209.7 2.7 %fusion.31 = bf16[4,256,32,8]{1,2,3,0:T(8,128)(2,1)S(1)} fusion(bf16[8,32,4,8,96]{4,3,1,0,2:T(8,128)(2,1)} %bitcast.229, bf16[8,2,96,256]{3,2,1,0:T(8,128)(2,1)S(1)} %all_to_all.75, bf16[8,2,96,256]{3,2,1,0:T(8,128)(2,1)} %all_to_all.74), kind=kOutput, calls=%fused_computation.33 | convolution fusion | flops 403701760 | bytes 3670016 | tf_op jit(solution)/shard_map/tnecf,tefd->necd/dot_general | solution.py:225
  213.5 7.6 %all-to-all-start.8 = ((bf16[32,32,256]{2,1,0:T(8,128)(2,1)}), bf16[32,32,256]{2,1,0:T(8,128)(2,1)}, u32[]{:S(2)}, u32[]{:S(2)}) async-start(bf16[32,32,256]{2,1,0:T(8,128)(2,1)} %copy.226), calls=%async_computation.8 | async-start | bytes 1048576 | tf_op jit(solution)/shard_map/all_to_all | solution.py:228
  221.4 17.8 %all-to-all-done.8 = bf16[32,32,256]{2,1,0:T(8,128)(2,1)} async-done(((bf16[32,32,256]{2,1,0:T(8,128)(2,1)}), bf16[32,32,256]{2,1,0:T(8,128)(2,1)}, u32[]{:S(2)}, u32[]{:S(2)}) %all-to-all-start.8) | async-done | bytes 524320 | tf_op jit(solution)/shard_map/all_to_all | solution.py:228
  240.3 2.2 gather_fusion
  243.8 8.6 %all_to_all.76 = bf16[8,8,256]{2,1,0:T(8,128)(2,1)S(1)} all-to-all(bf16[8,8,256]{2,1,0:T(8,128)(2,1)S(1)} %bitcast.222), channel_id=1, replica_groups=mesh['dp'=32,'tensor'=8] {'tensor'}, dimensions={0} | all-to-all | bytes 65536 | tf_op jit(solution)/shard_map/all_to_all | solution.py:238
  (150 shorter events, 28.2 us)
Async XLA Ops:
  7.2 78.3 %copy-start = (bf16[512,2048]{1,0:T(8,128)(2,1)S(1)}, bf16[512,2048]{1,0:T(8,128)(2,1)}, u32[]{:S(2)}) copy-start(bf16[512,2048]{1,0:T(8,128)(2,1)} %param.24) | copy-start | bytes 6291460
  7.2 10.4 %copy-start.19 = (s32[64]{0:T(128)S(1)}, s32[64]{0:T(128)}, u32[]{:S(2)}) copy-start(s32[64]{0:T(128)} %param.34) | copy-start | bytes 772
  8.8 13.0 %all-to-all-start = ((bf16[8,8,2048]{2,1,0:T(8,128)(2,1)}), bf16[8,8,2048]{2,1,0:T(8,128)(2,1)S(1)}, u32[]{:S(2)}, u32[]{:S(2)}) async-start(bf16[8,8,2048]{2,1,0:T(8,128)(2,1)} %broadcast_in_dim.70), calls=%async_computation | async-start | bytes 524288 | tf_op jit(solution)/shard_map/all_to_all | solution.py:65
  17.7 4.4 %copy-start.15 = (f32[2048]{0:T(1024)S(1)}, f32[2048]{0:T(1024)}, u32[]{:S(2)}) copy-start(f32[2048]{0:T(1024)} %param.19) | copy-start | bytes 24580
  17.7 5.8 %copy-start.17 = (f32[128]{0:T(128)S(1)}, f32[128]{0:T(128)}, u32[]{:S(2)}) copy-start(f32[128]{0:T(128)} %param.23) | copy-start | bytes 1540
  21.6 4.5 %copy-start.18 = (f32[128]{0:T(128)S(1)}, f32[128]{0:T(128)}, u32[]{:S(2)}) copy-start(f32[128]{0:T(128)} %param.22) | copy-start | bytes 1540
  26.5 0.6 copy-start.11
  27.2 8.9 %copy-start.13 = (s32[64,8]{0,1:T(8,128)S(1)}, s32[64,8]{0,1:T(8,128)}, u32[]{:S(2)}) copy-start(s32[64,8]{0,1:T(8,128)} %param.29) | copy-start | bytes 6148
  28.1 16.5 %all-to-all-start.1 = ((bf16[8,64,640]{2,1,0:T(8,128)(2,1)}), bf16[8,64,640]{2,1,0:T(8,128)(2,1)S(1)}, u32[]{:S(2)}, u32[]{:S(2)}) async-start(bf16[8,64,640]{2,1,0:T(8,128)(2,1)} %broadcast_in_dim.74), calls=%async_computation.1 | async-start | bytes 1310720 | tf_op jit(solution)/shard_map/all_to_all | solution.py:92
  36.1 3.7 %copy-start.6 = (s32[64,8]{1,0:T(8,128)}, s32[64,8]{1,0:T(8,128)S(1)}, u32[]{:S(2)}) copy-start(s32[64,8]{1,0:T(8,128)S(1)} %copy.213) | copy-start | bytes 6148
  46.4 7.1 %copy-start.8 = (f32[64,4,1,8]{0,3,1,2:T(8,128)}, f32[64,4,1,8]{0,3,1,2:T(8,128)S(1)}, u32[]{:S(2)}) copy-start(f32[64,4,1,8]{0,3,1,2:T(8,128)S(1)} %copy.231) | copy-start | bytes 24580
  53.7 5.2 %copy-start.5 = (f32[64,4,8]{2,0,1:T(8,128)}, f32[64,4,8]{2,0,1:T(8,128)S(1)}, u32[]{:S(2)}) copy-start(f32[64,4,8]{2,0,1:T(8,128)S(1)} %copy.192) | copy-start | bytes 24580
  54.5 4.5 %copy-start.1 = (f32[4,64,8,2,256]{4,2,3,1,0:T(8,128)S(1)}, f32[4,64,8,2,256]{4,2,3,1,0:T(8,128)}, u32[]{:S(2)}) copy-start(f32[4,64,8,2,256]{4,2,3,1,0:T(8,128)} %get-tuple-element.36) | copy-start | bytes 12582916
  58.9 4.0 %copy-start.2 = (f32[64,4,8,16]{3,2,1,0:T(8,128)S(1)}, f32[64,4,8,16]{3,2,1,0:T(8,128)}, u32[]{:S(2)}) copy-start(f32[64,4,8,16]{3,2,1,0:T(8,128)} %get-tuple-element.38) | copy-start | bytes 393220
  62.9 1.7 copy-start.3
  64.6 2.4 copy-start.4
  64.6 2.5 copy-start.9
  66.9 6.3 %copy-start.7 = (s32[64,8]{1,0:T(8,128)S(1)}, s32[64,8]{1,0:T(8,128)}, u32[]{:S(2)}) copy-start(s32[64,8]{1,0:T(8,128)} %copy-done.6) | copy-start | bytes 6148
  68.8 14.7 %all-to-all-start.2 = ((bf16[8,262,128]{2,1,0:T(8,128)(2,1)}), bf16[8,262,128]{2,1,0:T(8,128)(2,1)}, u32[]{:S(2)}, u32[]{:S(2)}) async-start(bf16[8,262,128]{2,1,0:T(8,128)(2,1)} %copy.209), calls=%async_computation.2 | async-start | bytes 1081344 | tf_op jit(solution)/shard_map/all_to_all | solution.py:167
  85.3 5.0 %copy-start.14 = (s32[64,8]{0,1:T(8,128)S(1)}, s32[64,8]{0,1:T(8,128)}, u32[]{:S(2)}) copy-start(s32[64,8]{0,1:T(8,128)} %param.29) | copy-start | bytes 6148
  85.3 12.3 %copy-start.10 = (bf16[8,2048]{1,0:T(8,128)(2,1)S(1)}, bf16[8,2048]{1,0:T(8,128)(2,1)}, u32[]{:S(2)}) copy-start(bf16[8,2048]{1,0:T(8,128)(2,1)} %param.18) | copy-start | bytes 98308
  85.3 12.4 %copy-start.16 = (f32[2048]{0:T(1024)S(1)}, f32[2048]{0:T(1024)}, u32[]{:S(2)}) copy-start(f32[2048]{0:T(1024)} %param.25) | copy-start | bytes 24580
  86.6 10.8 %all-to-all-start.3 = ((bf16[8,8,2048]{2,1,0:T(8,128)(2,1)}), bf16[8,8,2048]{2,1,0:T(8,128)(2,1)S(1)}, u32[]{:S(2)}, u32[]{:S(2)}) async-start(bf16[8,8,2048]{2,1,0:T(8,128)(2,1)} %fusion.9), calls=%async_computation.3 | async-start | bytes 524288 | tf_op jit(solution)/shard_map/all_to_all | solution.py:183
  98.4 8.7 %all-to-all-start.4 = ((bf16[8,8,256]{2,0,1:T(8,128)(2,1)}), bf16[8,8,256]{2,0,1:T(8,128)(2,1)S(1)}, u32[]{:S(2)}, u32[]{:S(2)}) async-start(bf16[8,8,256]{2,0,1:T(8,128)(2,1)} %bitcast.38), calls=%async_computation.4 | async-start | bytes 65536 | tf_op jit(solution)/shard_map/all_to_all | solution.py:193
  101.7 74.2 %all-gather.4.cloned.1.call-start = ((), (), s32[]{:S(2)}) async-start(), calls=%async_computation.10 | async-start | bytes 4718592 | tf_op jit(solution)/shard_map/all_gather | solution.py:209
  136.3 73.4 %all-gather.6.cloned.1.call-start = ((), (), s32[]{:S(2)}) async-start(), calls=%async_computation.11 | async-start | bytes 2359296 | tf_op jit(solution)/shard_map/all_gather | solution.py:222
  176.0 4.1 %copy-start.20 = (bf16[32,32,2048]{2,1,0:T(8,128)(2,1)S(1)}, bf16[32,32,2048]{2,1,0:T(8,128)(2,1)}, u32[]{:S(2)}) copy-start(bf16[32,32,2048]{2,1,0:T(8,128)(2,1)} %all-gather.4.cloned.1.call-done) | copy-start | bytes 12582916
  176.0 4.4 %copy-start.21 = (bf16[4,2048,96]{1,2,0:T(8,128)(2,1)S(1)}, bf16[4,2048,96]{1,2,0:T(8,128)(2,1)}, u32[]{:S(2)}) copy-start(bf16[4,2048,96]{1,2,0:T(8,128)(2,1)} %param.27) | copy-start | bytes 4718596
  212.4 8.9 %copy-start.12 = (f32[64,8]{0,1:T(8,128)S(1)}, f32[64,8]{0,1:T(8,128)}, u32[]{:S(2)}) copy-start(f32[64,8]{0,1:T(8,128)} %param.30) | copy-start | bytes 6148
  213.5 25.7 %all-to-all-start.8 = ((bf16[32,32,256]{2,1,0:T(8,128)(2,1)}), bf16[32,32,256]{2,1,0:T(8,128)(2,1)}, u32[]{:S(2)}, u32[]{:S(2)}) async-start(bf16[32,32,256]{2,1,0:T(8,128)(2,1)} %copy.226), calls=%async_computation.8 | async-start | bytes 1048576 | tf_op jit(solution)/shard_map/all_to_all | solution.py:228
Sparse Core Ops, SparseCore 0:
  136.4 39.5 all-gather.3
  182.5 27.1 all-gather.5

commit v12 on v11

--- a/solution.py
+++ b/solution.py
@@ -213,7 +213,7 @@
     down_split = down_weight.reshape(local_experts, ff_here, tensor_size, width_here).transpose(
         2, 0, 1, 3
     )
-    half_experts = local_experts // 2
+    half_experts = 3 * local_experts // 4
     down_first = lax.all_to_all(down_split[:, :half_experts], "tensor", 0, 0, tiled=True)
     rows, down_first = lax.optimization_barrier((rows, down_first))
     gate_val = jnp.einsum("necd,edf->necf", rows, gate_weight, preferred_element_type=jnp.float32)

time: 261 us -> 266 us (1.019)
  waiting for transfers between devices: 65.5 us -> 71.5 us
  blocking collectives: 80.6 us -> 76.1 us
    all_to_all x1, blocking collectives: 21.4 us -> 12.2 us  [body(): lax.all_to_all(down_split[:, half_experts:], 'tensor', 0, 0, tiled=True)]
    all_gather x1, waiting for transfers between devices: 5.78 us -> 13.1 us  [body(): hidden_all = lax.all_gather(hidden_units, 'tensor', axis=0)]
    all_to_all x1, blocking collectives: 21.9 us -> 26.5 us  [body(): lax.all_to_all(down_split[:, :half_experts], 'tensor', 0, 0, tiled=True)]
    unnamed x50 -> x52, local copies, waits for them, and re-layouts: 9.2 us -> 10.1 us
  transfers between devices with their start and end apart: 8 -> 8, of which waited for: 7 -> 7; matrix products, arithmetic and copies ran while one was open for 8% -> 7% of each run, Pallas kernels for 0% -> 0%
where the time goes in v12:
time: 266 us; the launch traced here: 265 us
  blocking collectives  76.1 us (29%)
  waiting for transfers between devices  71.5 us (27%)
  starting transfers between devices  30.4 us (11%)
  local copies, waits for them, and re-layouts  28.4 us (11%)
  matrix products  26.6 us (10%)
  other arithmetic  17 us (6%)
  between operations  14.7 us (6%)
    all_to_all x1, blocking collectives, body(): lax.all_to_all(outgoing, 'dp', split_axis=0, concat_axis=0, tiled=True)  28.8 us
    all_to_all x1, blocking collectives, body(): lax.all_to_all(down_split[:, :half_experts], 'tensor', 0, 0, tiled=True)  26.5 us
    all_to_all x1, waiting for transfers between devices, body(): lax.all_to_all(summed_out.reshape(owners, local_experts * capacity, width...  17.8 us
    all_gather x1, waiting for transfers between devices, body(): lax.all_gather(arrived, 'tensor', axis=2, tiled=True)  14.2 us
    all_gather x1, waiting for transfers between devices, body(): hidden_all = lax.all_gather(hidden_units, 'tensor', axis=0)  13.1 us
    all_to_all x1, blocking collectives, body(): lax.all_to_all(down_split[:, half_experts:], 'tensor', 0, 0, tiled=True)  12.2 us
    all_to_all x1, starting transfers between devices, body(): lax.all_to_all(summed_out.reshape(owners, local_experts * capacity, width...  10.1 us
    unnamed x52, local copies, waits for them, and re-layouts  10.1 us
  transfers between devices with their start and end apart: 8, of which 7 were waited for; matrix products, arithmetic and copies ran while one was open for 7% of the time, Pallas kernels for 0%

profile of v12, /device:TPU:32, one launch (start us, length us, event | category | flops | bytes accessed | tf_op | source)
XLA Modules:
  0.0 264.7 jit_solution(10925306512845241036)
XLA Ops:
  8.8 4.3 %all-to-all-start = ((bf16[8,8,2048]{2,1,0:T(8,128)(2,1)}), bf16[8,8,2048]{2,1,0:T(8,128)(2,1)S(1)}, u32[]{:S(2)}, u32[]{:S(2)}) async-start(bf16[8,8,2048]{2,1,0:T(8,128)(2,1)} %broadcast_in_dim.70), calls=%async_computation | async-start | bytes 524288 | tf_op jit(solution)/shard_map/all_to_all | solution.py:65
  15.5 2.1 fusion.111
  17.6 4.0 %copy.241 = bf16[512,2048]{1,0:T(8,128)(2,1)} copy(bf16[512,2048]{0,1:T(8,128)(2,1)} %bitcast.212) | data formatting | bytes 4194304 | tf_op jit(solution)/shard_map/dot_general | solution.py:75
  23.6 2.5 multiply_reduce_fusion
  28.0 4.8 %all-to-all-start.1 = ((bf16[8,64,640]{2,1,0:T(8,128)(2,1)}), bf16[8,64,640]{2,1,0:T(8,128)(2,1)S(1)}, u32[]{:S(2)}, u32[]{:S(2)}) async-start(bf16[8,64,640]{2,1,0:T(8,128)(2,1)} %broadcast_in_dim.74), calls=%async_computation.1 | async-start | bytes 1310720 | tf_op jit(solution)/shard_map/all_to_all | solution.py:92
  32.9 2.1 copy.249
  36.5 3.3 %slice_bitcast_fusion = (bf16[64,2,4,8,128]{4,3,2,1,0:T(8,128)(2,1)}, bf16[64,2,4,8,128]{4,3,2,1,0:T(8,128)(2,1)}) fusion(bf16[64,16,1024]{2,1,0:T(8,128)(2,1)} %param.32), kind=kLoop, calls=%fused_computation.47 | loop fusion | bytes 4194304
  39.8 4.8 %all-to-all-done.1 = bf16[8,64,640]{2,1,0:T(8,128)(2,1)S(1)} async-done(((bf16[8,64,640]{2,1,0:T(8,128)(2,1)}), bf16[8,64,640]{2,1,0:T(8,128)(2,1)S(1)}, u32[]{:S(2)}, u32[]{:S(2)}) %all-to-all-start.1) | async-done | bytes 655392 | tf_op jit(solution)/shard_map/all_to_all | solution.py:92
  46.4 4.0 %fusion = (bf16[64,4,8]{2,0,1:T(8,128)(2,1)S(1)}, f32[4,64,8,2,256]{4,2,3,1,0:T(8,128)}) fusion(pred[64,2,256]{2,1,0:T(4,128)(4,1)S(1)} %broadcast_and_fusion, bf16[2,256,4,128,1]{1,3,2,0,4:T(8,128)(2,1)} %bitcast.216, bf16[64,4,8,128]{3,2,1,0:T(8,128)(2,1)S(1)} %reshape.385), kind=kOutput, calls=%fused_computation.3 | convolution fusion | flops 271579136 | bytes 5279744 | tf_op jit(solution)/shard_map/rgqd,npgd->rgqnp/dot_general | solution.py:108
  50.5 2.9 %select_reduce_fusion = (bf16[64,4,8]{2,1,0:T(4,128)(2,1)S(1)}, f32[64,4,8,16]{3,2,1,0:T(8,128)}) fusion(pred[64,16]{1,0:T(8,128)(4,1)S(1)} %broadcast_compare_fusion, bf16[64,4,8,128]{3,2,1,0:T(8,128)(2,1)S(1)} %reshape.385, bf16[64,2,4,8,128]{4,3,2,1,0:T(8,128)(2,1)} %get-tuple-element.15), kind=kOutput, calls=%fused_computation.49 | convolution fusion | flops 8484864 | bytes 1709056 | tf_op jit(solution)/shard_map/rgqd,rsgd->rgqs/dot_general | solution.py:112
  54.4 4.4 %fusion.7 = f32[64,4,8]{2,0,1:T(8,128)} fusion(f32[4,64,8,2,256]{4,2,3,1,0:T(8,128)} %get-tuple-element.34, f32[64,4,8]{2,0,1:T(8,128)S(1)} %copy.192, pred[64,2,256]{2,1,0:T(4,128)(4,1)S(1)} %broadcast_and_fusion), kind=kLoop, calls=%fused_computation.10 | loop fusion | flops 4192256 | bytes 4243456 | tf_op jit(solution)/shard_map/reduce_sum | solution.py:135
  58.9 3.2 %fusion.26 = f32[64,4,8,128]{3,2,0,1:T(8,128)} fusion(f32[4,64,8,2,256]{4,2,3,1,0:T(8,128)S(1)} %copy-done.1, f32[64,4,8]{2,0,1:T(8,128)} %copy-done.6, pred[64,2,256]{2,1,0:T(4,128)(4,1)S(1)} %broadcast_and_fusion, bf16[2,256,4,128,1]{1,3,2,0,4:T(8,128)(2,1)} %bitcast.221), kind=kOutput, calls=%fused_computation.30 | convolution fusion | flops 272629760 | bytes 5808128 | tf_op jit(solution)/shard_map/rgqnp,npgd->rgqd/dot_general | solution.py:136
  64.5 1.8 fusion.33
  68.7 4.4 %all-to-all-start.2 = ((bf16[8,262,128]{2,1,0:T(8,128)(2,1)}), bf16[8,262,128]{2,1,0:T(8,128)(2,1)}, u32[]{:S(2)}, u32[]{:S(2)}) async-start(bf16[8,262,128]{2,1,0:T(8,128)(2,1)} %copy.209), calls=%async_computation.2 | async-start | bytes 1081344 | tf_op jit(solution)/shard_map/all_to_all | solution.py:167
  73.5 9.9 %all-to-all-done.2 = bf16[8,262,128]{2,1,0:T(8,128)(2,1)} async-done(((bf16[8,262,128]{2,1,0:T(8,128)(2,1)}), bf16[8,262,128]{2,1,0:T(8,128)(2,1)}, u32[]{:S(2)}, u32[]{:S(2)}) %all-to-all-start.2) | async-done | bytes 536608 | tf_op jit(solution)/shard_map/all_to_all | solution.py:167
  86.6 3.4 %all-to-all-start.3 = ((bf16[8,8,2048]{2,1,0:T(8,128)(2,1)}), bf16[8,8,2048]{2,1,0:T(8,128)(2,1)S(1)}, u32[]{:S(2)}, u32[]{:S(2)}) async-start(bf16[8,8,2048]{2,1,0:T(8,128)(2,1)} %fusion.9), calls=%async_computation.3 | async-start | bytes 524288 | tf_op jit(solution)/shard_map/all_to_all | solution.py:183
  90.3 7.2 %all-to-all-done.3 = bf16[8,8,2048]{2,1,0:T(8,128)(2,1)S(1)} async-done(((bf16[8,8,2048]{2,1,0:T(8,128)(2,1)}), bf16[8,8,2048]{2,1,0:T(8,128)(2,1)S(1)}, u32[]{:S(2)}, u32[]{:S(2)}) %all-to-all-start.3) | async-done | bytes 262176 | tf_op jit(solution)/shard_map/all_to_all | solution.py:183
  98.3 3.3 %all-to-all-start.4 = ((bf16[8,8,256]{2,0,1:T(8,128)(2,1)}), bf16[8,8,256]{2,0,1:T(8,128)(2,1)S(1)}, u32[]{:S(2)}, u32[]{:S(2)}) async-start(bf16[8,8,256]{2,0,1:T(8,128)(2,1)} %bitcast.38), calls=%async_computation.4 | async-start | bytes 65536 | tf_op jit(solution)/shard_map/all_to_all | solution.py:193
  102.4 4.6 %all-to-all-done.4 = bf16[8,8,256]{2,0,1:T(8,128)(2,1)S(1)} async-done(((bf16[8,8,256]{2,0,1:T(8,128)(2,1)}), bf16[8,8,256]{2,0,1:T(8,128)(2,1)S(1)}, u32[]{:S(2)}, u32[]{:S(2)}) %all-to-all-start.4) | async-done | bytes 32800 | tf_op jit(solution)/shard_map/all_to_all | solution.py:193
  107.4 28.8 %all_to_all.73 = bf16[32,32,256]{2,1,0:T(8,128)(2,1)} all-to-all(bf16[32,32,256]{2,1,0:T(8,128)(2,1)S(1)} %bitcast.214), channel_id=1, replica_groups=mesh['dp'=32,'tensor'=8] {'dp'}, dimensions={0} | all-to-all | bytes 1048576 | tf_op jit(solution)/shard_map/all_to_all | solution.py:208
  136.3 1.9 copy.255
  139.5 26.5 %all_to_all.74 = bf16[8,3,96,256]{3,2,1,0:T(8,128)(2,1)} all-to-all(bf16[8,3,96,256]{3,2,1,0:T(8,128)(2,1)S(1)} %copy.219), channel_id=1, replica_groups=mesh['dp'=32,'tensor'=8] {'tensor'}, dimensions={0} | all-to-all | bytes 2359296 | tf_op jit(solution)/shard_map/all_to_all | solution.py:217
  166.0 14.2 %all-gather.4.cloned.1.call-done = bf16[32,32,2048]{2,1,0:T(8,128)(2,1)} async-done(((bf16[32,32,256]{2,1,0:T(8,128)(2,1)}), bf16[32,32,2048]{2,1,0:T(8,128)(2,1)}) %all-gather.4.cloned.1.call-update) | async-done | bytes 4194320 | tf_op jit(solution)/shard_map/all_gather | solution.py:209
  180.2 4.1 %fusion.34 = f32[32,4,8,96]{3,2,0,1:T(8,128)S(1)} fusion(bf16[4,2048,96]{1,2,0:T(8,128)(2,1)} %param.26, bf16[32,4,8,2048]{3,2,1,0:T(8,128)(2,1)} %bitcast.234), kind=kOutput, calls=%fused_computation.37 | convolution fusion | flops 402653184 | bytes 6160384 | tf_op jit(solution)/shard_map/necd,edf->necf/dot_general | solution.py:219
  184.5 2.0 fusion.49
  186.6 12.2 %all_to_all.75 = bf16[8,1,96,256]{3,2,1,0:T(8,128)(2,1)S(1)} all-to-all(bf16[8,1,96,256]{3,2,1,0:T(8,128)(2,1)S(1)} %copy.220), channel_id=1, replica_groups=mesh['dp'=32,'tensor'=8] {'tensor'}, dimensions={0} | all-to-all | bytes 786432 | tf_op jit(solution)/shard_map/all_to_all | solution.py:223
  198.8 13.1 %all-gather.6.cloned.1.call-done = bf16[256,4,8,96]{3,2,0,1:T(8,128)(2,1)} async-done(((bf16[32,4,8,96]{3,2,0,1:T(8,128)(2,1)}), bf16[256,4,8,96]{3,2,0,1:T(8,128)(2,1)}) %all-gather.6.cloned.1.call-update) | async-done | bytes 1572880 | tf_op jit(solution)/shard_map/all_gather | solution.py:222
  211.9 2.8 %fusion.30 = bf16[4,256,32,8]{1,2,3,0:T(8,128)(2,1)S(1)} fusion(bf16[8,32,4,8,96]{4,3,1,0,2:T(8,128)(2,1)} %bitcast.236, bf16[8,1,96,256]{3,2,0,1:T(8,128)(2,1)S(1)} %bitcast.223, bf16[8,3,96,256]{3,2,1,0:T(8,128)(2,1)} %all_to_all.74), kind=kOutput, calls=%fused_computation.34 | convolution fusion | flops 406061056 | bytes 3670016 | tf_op jit(solution)/shard_map/tnecf,tefd->necd/dot_general | solution.py:225
  215.8 10.1 %all-to-all-start.8 = ((bf16[32,32,256]{2,1,0:T(8,128)(2,1)}), bf16[32,32,256]{2,1,0:T(8,128)(2,1)}, u32[]{:S(2)}, u32[]{:S(2)}) async-start(bf16[32,32,256]{2,1,0:T(8,128)(2,1)} %copy.226), calls=%async_computation.8 | async-start | bytes 1048576 | tf_op jit(solution)/shard_map/all_to_all | solution.py:228
  226.3 17.8 %all-to-all-done.8 = bf16[32,32,256]{2,1,0:T(8,128)(2,1)} async-done(((bf16[32,32,256]{2,1,0:T(8,128)(2,1)}), bf16[32,32,256]{2,1,0:T(8,128)(2,1)}, u32[]{:S(2)}, u32[]{:S(2)}) %all-to-all-start.8) | async-done | bytes 524320 | tf_op jit(solution)/shard_map/all_to_all | solution.py:228
  245.2 2.2 gather_fusion
  248.7 8.6 %all_to_all.76 = bf16[8,8,256]{2,1,0:T(8,128)(2,1)S(1)} all-to-all(bf16[8,8,256]{2,1,0:T(8,128)(2,1)S(1)} %bitcast.229), channel_id=1, replica_groups=mesh['dp'=32,'tensor'=8] {'tensor'}, dimensions={0} | all-to-all | bytes 65536 | tf_op jit(solution)/shard_map/all_to_all | solution.py:238
  (154 shorter events, 28.9 us)
Async XLA Ops:
  7.2 78.2 %copy-start = (bf16[512,2048]{1,0:T(8,128)(2,1)S(1)}, bf16[512,2048]{1,0:T(8,128)(2,1)}, u32[]{:S(2)}) copy-start(bf16[512,2048]{1,0:T(8,128)(2,1)} %param.24) | copy-start | bytes 6291460
  7.2 10.4 %copy-start.20 = (s32[64]{0:T(128)S(1)}, s32[64]{0:T(128)}, u32[]{:S(2)}) copy-start(s32[64]{0:T(128)} %param.34) | copy-start | bytes 772
  8.8 12.9 %all-to-all-start = ((bf16[8,8,2048]{2,1,0:T(8,128)(2,1)}), bf16[8,8,2048]{2,1,0:T(8,128)(2,1)S(1)}, u32[]{:S(2)}, u32[]{:S(2)}) async-start(bf16[8,8,2048]{2,1,0:T(8,128)(2,1)} %broadcast_in_dim.70), calls=%async_computation | async-start | bytes 524288 | tf_op jit(solution)/shard_map/all_to_all | solution.py:65
  17.6 4.4 %copy-start.16 = (f32[2048]{0:T(1024)S(1)}, f32[2048]{0:T(1024)}, u32[]{:S(2)}) copy-start(f32[2048]{0:T(1024)} %param.19) | copy-start | bytes 24580
  17.6 5.8 %copy-start.18 = (f32[128]{0:T(128)S(1)}, f32[128]{0:T(128)}, u32[]{:S(2)}) copy-start(f32[128]{0:T(128)} %param.23) | copy-start | bytes 1540
  21.6 4.5 %copy-start.19 = (f32[128]{0:T(128)S(1)}, f32[128]{0:T(128)}, u32[]{:S(2)}) copy-start(f32[128]{0:T(128)} %param.22) | copy-start | bytes 1540
  26.5 0.6 copy-start.12
  27.1 8.9 %copy-start.14 = (s32[64,8]{0,1:T(8,128)S(1)}, s32[64,8]{0,1:T(8,128)}, u32[]{:S(2)}) copy-start(s32[64,8]{0,1:T(8,128)} %param.29) | copy-start | bytes 6148
  28.0 16.5 %all-to-all-start.1 = ((bf16[8,64,640]{2,1,0:T(8,128)(2,1)}), bf16[8,64,640]{2,1,0:T(8,128)(2,1)S(1)}, u32[]{:S(2)}, u32[]{:S(2)}) async-start(bf16[8,64,640]{2,1,0:T(8,128)(2,1)} %broadcast_in_dim.74), calls=%async_computation.1 | async-start | bytes 1310720 | tf_op jit(solution)/shard_map/all_to_all | solution.py:92
  36.1 3.7 %copy-start.7 = (s32[64,8]{1,0:T(8,128)}, s32[64,8]{1,0:T(8,128)S(1)}, u32[]{:S(2)}) copy-start(s32[64,8]{1,0:T(8,128)S(1)} %copy.213) | copy-start | bytes 6148
  46.4 7.1 %copy-start.9 = (f32[64,4,1,8]{0,3,1,2:T(8,128)}, f32[64,4,1,8]{0,3,1,2:T(8,128)S(1)}, u32[]{:S(2)}) copy-start(f32[64,4,1,8]{0,3,1,2:T(8,128)S(1)} %copy.231) | copy-start | bytes 24580
  53.6 5.2 %copy-start.6 = (f32[64,4,8]{2,0,1:T(8,128)}, f32[64,4,8]{2,0,1:T(8,128)S(1)}, u32[]{:S(2)}) copy-start(f32[64,4,8]{2,0,1:T(8,128)S(1)} %copy.192) | copy-start | bytes 24580
  54.4 4.4 %copy-start.1 = (f32[4,64,8,2,256]{4,2,3,1,0:T(8,128)S(1)}, f32[4,64,8,2,256]{4,2,3,1,0:T(8,128)}, u32[]{:S(2)}) copy-start(f32[4,64,8,2,256]{4,2,3,1,0:T(8,128)} %get-tuple-element.34) | copy-start | bytes 12582916
  58.9 4.0 %copy-start.3 = (f32[64,4,8,16]{3,2,1,0:T(8,128)S(1)}, f32[64,4,8,16]{3,2,1,0:T(8,128)}, u32[]{:S(2)}) copy-start(f32[64,4,8,16]{3,2,1,0:T(8,128)} %get-tuple-element.36) | copy-start | bytes 393220
  62.8 1.7 copy-start.4
  64.5 2.4 copy-start.5
  64.5 2.5 copy-start.10
  66.9 6.2 %copy-start.8 = (s32[64,8]{1,0:T(8,128)S(1)}, s32[64,8]{1,0:T(8,128)}, u32[]{:S(2)}) copy-start(s32[64,8]{1,0:T(8,128)} %copy-done.7) | copy-start | bytes 6148
  68.7 14.7 %all-to-all-start.2 = ((bf16[8,262,128]{2,1,0:T(8,128)(2,1)}), bf16[8,262,128]{2,1,0:T(8,128)(2,1)}, u32[]{:S(2)}, u32[]{:S(2)}) async-start(bf16[8,262,128]{2,1,0:T(8,128)(2,1)} %copy.209), calls=%async_computation.2 | async-start | bytes 1081344 | tf_op jit(solution)/shard_map/all_to_all | solution.py:167
  85.2 5.0 %copy-start.15 = (s32[64,8]{0,1:T(8,128)S(1)}, s32[64,8]{0,1:T(8,128)}, u32[]{:S(2)}) copy-start(s32[64,8]{0,1:T(8,128)} %param.29) | copy-start | bytes 6148
  85.2 12.2 %copy-start.11 = (bf16[8,2048]{1,0:T(8,128)(2,1)S(1)}, bf16[8,2048]{1,0:T(8,128)(2,1)}, u32[]{:S(2)}) copy-start(bf16[8,2048]{1,0:T(8,128)(2,1)} %param.18) | copy-start | bytes 98308
  85.2 12.4 %copy-start.17 = (f32[2048]{0:T(1024)S(1)}, f32[2048]{0:T(1024)}, u32[]{:S(2)}) copy-start(f32[2048]{0:T(1024)} %param.25) | copy-start | bytes 24580
  86.6 10.8 %all-to-all-start.3 = ((bf16[8,8,2048]{2,1,0:T(8,128)(2,1)}), bf16[8,8,2048]{2,1,0:T(8,128)(2,1)S(1)}, u32[]{:S(2)}, u32[]{:S(2)}) async-start(bf16[8,8,2048]{2,1,0:T(8,128)(2,1)} %fusion.9), calls=%async_computation.3 | async-start | bytes 524288 | tf_op jit(solution)/shard_map/all_to_all | solution.py:183
  98.3 8.7 %all-to-all-start.4 = ((bf16[8,8,256]{2,0,1:T(8,128)(2,1)}), bf16[8,8,256]{2,0,1:T(8,128)(2,1)S(1)}, u32[]{:S(2)}, u32[]{:S(2)}) async-start(bf16[8,8,256]{2,0,1:T(8,128)(2,1)} %bitcast.38), calls=%async_computation.4 | async-start | bytes 65536 | tf_op jit(solution)/shard_map/all_to_all | solution.py:193
  101.7 78.5 %all-gather.4.cloned.1.call-start = ((), (), s32[]{:S(2)}) async-start(), calls=%async_computation.10 | async-start | bytes 4718592 | tf_op jit(solution)/shard_map/all_gather | solution.py:209
  136.3 75.7 %all-gather.6.cloned.1.call-start = ((), (), s32[]{:S(2)}) async-start(), calls=%async_computation.11 | async-start | bytes 2359296 | tf_op jit(solution)/shard_map/all_gather | solution.py:222
  138.3 1.2 copy-start.2
  180.1 4.1 %copy-start.21 = (bf16[32,32,2048]{2,1,0:T(8,128)(2,1)S(1)}, bf16[32,32,2048]{2,1,0:T(8,128)(2,1)}, u32[]{:S(2)}) copy-start(bf16[32,32,2048]{2,1,0:T(8,128)(2,1)} %all-gather.4.cloned.1.call-done) | copy-start | bytes 12582916
  180.2 4.4 %copy-start.22 = (bf16[4,2048,96]{1,2,0:T(8,128)(2,1)S(1)}, bf16[4,2048,96]{1,2,0:T(8,128)(2,1)}, u32[]{:S(2)}) copy-start(bf16[4,2048,96]{1,2,0:T(8,128)(2,1)} %param.27) | copy-start | bytes 4718596
  184.5 2.0 slice-start
  214.7 11.4 %copy-start.13 = (f32[64,8]{0,1:T(8,128)S(1)}, f32[64,8]{0,1:T(8,128)}, u32[]{:S(2)}) copy-start(f32[64,8]{0,1:T(8,128)} %param.30) | copy-start | bytes 6148
  215.8 28.2 %all-to-all-start.8 = ((bf16[32,32,256]{2,1,0:T(8,128)(2,1)}), bf16[32,32,256]{2,1,0:T(8,128)(2,1)}, u32[]{:S(2)}, u32[]{:S(2)}) async-start(bf16[32,32,256]{2,1,0:T(8,128)(2,1)} %copy.226), calls=%async_computation.8 | async-start | bytes 1048576 | tf_op jit(solution)/shard_map/all_to_all | solution.py:228
Sparse Core Ops, SparseCore 0:
  136.4 43.7 all-gather.3
  186.7 25.2 all-gather.5
